TPU v7x, 256 devices: a whole 4x4x8 slice. The times are simulated.
256 devices in a mesh: target: 32 (over x_lo, z, core), surface: 8 (over x_hi, y).
Axes of the slice: x: 4 (x_hi: 2, x_lo: 2; x = x_hi * 2 + x_lo), y: 4, z: 8, core: 2. Of those that a mesh axis runs over, the one named last changes fastest.
Arguments:
- response: float32 [64, 32, 32, 512], P('target', None, 'surface'), may hold values from -6 to 6
- data_spectra: bfloat16 [32, 16, 2, 32, 32, 256], P('target', None, None, 'surface'), may hold values from -0.01171875 to 0.01171875
- observed: bfloat16 [32, 2, 32, 32, 256], P('target', None, None, 'surface'), may hold values from -6 to 6
- block_lists: int32 [32, 16], replicated, may hold values from 0 to 63, as said below
Outputs:
- response_next: float32 [64, 32, 32, 512], P('target', None, 'surface')
- response_copy: bfloat16 [64, 32, 32, 512], P('target', None, 'surface')
- residual: float32 [32, 2, 32, 32, 256], P('target', None, None, 'surface')
Inputs may be any that keep to these rules, and one draw needn't show every extreme that they name: `block_lists`: block b is owned by index b // 2 of target. Each tile lists 16 blocks, no two of the same owner.
All inputs are finite; a program needn't handle non-finite values.
Results may differ from a plain program's by a relative error of at most 0.0048.
Values may be sent and summed in bfloat16 or wider, within the bound.
No kernel may reach another device: no remote copies, remote signals or barrier semaphores. Data moves between devices by JAX's collectives and lax.ppermute only.
A program may use at most 128 MiB of HBM per device.

v0:
```python
import math

import jax
import jax.numpy as jnp
from jax import lax
from jax.sharding import PartitionSpec as P

step_length = 0.5


def make_table(samples):
    freqs = samples // 2
    sample_index = lax.broadcasted_iota(jnp.int32, (samples, freqs), 0)
    freq_index = lax.broadcasted_iota(jnp.int32, (samples, freqs), 1)
    phase = (sample_index * freq_index % samples).astype(jnp.float32) * (2.0 * math.pi / samples)
    return jnp.concatenate([jnp.cos(phase), -jnp.sin(phase)], axis=1)


def contract(spec, listed):
    return jnp.einsum("lakf,lkrf->arf", spec, listed, preferred_element_type=jnp.float32)


def correlate(misfit_part, listed):
    return jnp.einsum("arf,lkrf->lakf", misfit_part, listed, preferred_element_type=jnp.float32)


def per_device(response, data_spectra, observed, block_lists):
    owners = lax.axis_size("target")
    channels = lax.axis_size("surface")
    my_index = lax.axis_index("target")
    owned = response.shape[0]
    samples = response.shape[3]
    freqs = samples // 2
    dft_table = make_table(samples)
    table_half = dft_table.astype(jnp.bfloat16).reshape(samples, 2, freqs)
    own_ids = lax.dynamic_slice_in_dim(block_lists, my_index, 1, 0)[0]
    own_owner = own_ids // owned
    wanted = block_lists // owned == my_index
    present = jnp.any(wanted, axis=1)
    slot_for = jnp.sum(jnp.where(wanted, block_lists % owned, 0), axis=1)
    chosen = (slot_for[None, :] == jnp.arange(owned, dtype=jnp.int32)[:, None]) & present[None, :]
    present_rows = present[:, None, None, None]
    zero_half = jnp.zeros((), jnp.bfloat16)
    copy_now = response.astype(jnp.bfloat16)
    outgoing = jnp.where(present_rows, copy_now[slot_for], zero_half)
    arrived = lax.all_to_all(outgoing, "target", split_axis=0, concat_axis=0, tiled=True)
    data_real = jnp.moveaxis(data_spectra[0, :, 0], -1, 0)
    data_imag = jnp.moveaxis(data_spectra[0, :, 1], -1, 0)
    forward = jnp.stack(
        [jnp.stack([data_real, data_imag], 3), jnp.stack([-data_imag, data_real], 3)], 3
    )
    backward = jnp.stack(
        [jnp.stack([-data_real, -data_imag], 3), jnp.stack([data_imag, -data_real], 3)], 3
    )
    spectra = jnp.einsum(
        "lakn,ncf->flakc", arrived[own_owner], table_half, preferred_element_type=jnp.float32
    ).astype(jnp.bfloat16)
    partial_value = jnp.einsum(
        "flakc,flkcdr->fdar", spectra, forward, preferred_element_type=jnp.float32
    )
    f_dim, parts, shots, recvs = partial_value.shape
    split_value = partial_value.reshape(f_dim, parts, shots, channels, recvs // channels)
    exchanged = lax.all_to_all(split_value, "surface", split_axis=3, concat_axis=3, tiled=True)
    summed_share = jnp.moveaxis(jnp.sum(exchanged, axis=3), 0, -1)
    residual_share = observed[0].astype(jnp.float32) - summed_share
    misfit_share = jnp.moveaxis(residual_share.astype(jnp.bfloat16), -1, 0)
    spread = jnp.broadcast_to(misfit_share[:, :, :, None], misfit_share.shape[:3] + (channels,) + misfit_share.shape[3:])
    gathered = lax.all_to_all(spread, "surface", split_axis=3, concat_axis=3, tiled=True)
    misfit = gathered.reshape(f_dim, parts, shots, recvs)
    grad_spectra = jnp.einsum(
        "fcar,flkecr->lakef", misfit, backward, preferred_element_type=jnp.float32
    )
    grad_flat = grad_spectra.reshape(grad_spectra.shape[:3] + (samples,))
    grad_time = jnp.dot(grad_flat, dft_table.T, precision=lax.Precision.HIGHEST)
    grad_half = grad_time.astype(jnp.bfloat16)
    returning = jnp.zeros((owners,) + grad_time.shape[1:], jnp.bfloat16).at[own_owner].set(grad_half)
    received = lax.all_to_all(returning, "target", split_axis=0, concat_axis=0, tiled=True)
    taken = jnp.where(
        chosen[:, :, None, None, None], received[None].astype(jnp.float32), jnp.zeros((), jnp.float32)
    )
    gradient = jnp.sum(taken, axis=1)
    response_next = response - step_length * gradient
    return (response_next, response_next.astype(jnp.bfloat16), residual_share[None])


def solution(mesh):
    return jax.shard_map(
        per_device,
        mesh=mesh,
        in_specs=(
            P("target", None, "surface", None),
            P("target", None, None, "surface", None, None),
            P("target", None, None, "surface", None),
            P(),
        ),
        out_specs=(
            P("target", None, "surface", None),
            P("target", None, "surface", None),
            P("target", None, None, "surface", None),
        ),
        check_vma=False,
    )
```

profile of v0, /device:TPU:1, one launch (start us, length us, event | category | flops | bytes accessed | tf_op | source)
XLA Modules:
  0.0 381.3 jit_solution(14138851360742844757)
XLA Ops:
  0.6 0.7 fusion.46
  1.4 0.7 fusion.37
  2.1 1.2 copy.125
  3.3 2.7 gather_fusion
  6.0 4.4 %broadcast_select_fusion = bf16[32,32,4,512]{3,1,2,0:T(8,128)(2,1)} fusion(bf16[32,32,4,512]{3,1,2,0:T(8,128)(2,1)} %gather_fusion, pred[32]{0:T(512)(128)(4,1)S(1)} %get-tuple-element.17), kind=kLoop, calls=%fused_computation.20 | loop fusion | flops 2097152 | bytes 8388640 | tf_op jit(solution)/shard_map/jit(_where)/select_n | solution.py:45
  10.5 11.1 %all-to-all-start = ((bf16[32,32,4,512]{3,1,2,0:T(8,128)(2,1)}), bf16[32,32,4,512]{3,1,2,0:T(8,128)(2,1)}, u32[]{:S(2)}, u32[]{:S(2)}) async-start(bf16[32,32,4,512]{3,1,2,0:T(8,128)(2,1)} %broadcast_select_fusion), calls=%async_computation | async-start | bytes 8388608 | tf_op jit(solution)/shard_map/all_to_all | solution.py:46
  21.6 1.8 fusion.48
  23.4 0.0 copy-start.4
  23.4 6.5 %copy.117 = bf16[1,16,1,4,32,256]{4,1,3,5,2,0:T(8,128)(2,1)} copy(bf16[1,16,1,4,32,256]{5,4,3,2,1,0:T(8,128)(2,1)S(1)} %get-tuple-element.24) | data formatting | bytes 2097152
  29.9 6.5 %copy.118 = bf16[1,16,1,4,32,256]{4,1,3,5,2,0:T(8,128)(2,1)} copy(bf16[1,16,1,4,32,256]{5,4,3,2,1,0:T(8,128)(2,1)S(1)} %get-tuple-element.23) | data formatting | bytes 2097152
  36.4 0.0 copy-done.4
  36.4 0.2 dynamic-slice_reduce_fusion
  36.6 2.2 negate_convert_fusion
  38.8 0.0 copy-start
  38.8 0.0 copy-start.1
  38.8 6.6 %fusion.9 = (bf16[256,16,4,1,32]{4,1,2,3,0:T(8,128)(2,1)S(1)}, bf16[256,16,4,1,32]{4,1,2,3,0:T(8,128)(2,1)}) fusion(bf16[1,16,1,4,32,256]{4,1,3,5,2,0:T(8,128)(2,1)} %copy.117, bf16[1,16,1,4,32,256]{4,1,3,5,2,0:T(8,128)(2,1)} %copy.118), kind=kLoop, calls=%fused_computation.17 | loop fusion | flops 1048576 | bytes 4194304 | tf_op jit(solution)/shard_map/stack | solution.py:53
  45.4 0.0 copy-done
  45.4 0.0 copy-done.1
  45.4 14.7 %maximum_bitcast_fusion = (bf16[256,16,4,1,2,32]{5,1,2,4,0,3:T(8,128)(2,1)}, bf16[256,16,4,1,2,32]{5,1,2,4,0,3:T(8,128)(2,1)}, bf16[256,16,4,1,2,32]{5,1,2,3,4,0:T(8,128)(2,1)}, bf16[256,16,4,1,2,32]{5,1,2,3,4,0:T(8,128)(2,1)}) fusion(bf16[256,16,4,1,32]{4,1,2,3,0:T(8,128)(2,1)} %get-tuple-element.30, bf16[256,16,4,1,32]{4,1,2,3,0:T(8,128)(2,1)S(1)} %get-tuple-element.29, ...), kind=kLoop, calls=%fused_computation.12 | loop fusion | flops 4194304 | bytes 12582912 | tf_op jit(solution)/shard_map/stack | solution.py:52
  60.2 56.1 %all-to-all-done = bf16[32,32,4,512]{3,1,2,0:T(8,128)(2,1)} async-done(((bf16[32,32,4,512]{3,1,2,0:T(8,128)(2,1)}), bf16[32,32,4,512]{3,1,2,0:T(8,128)(2,1)}, u32[]{:S(2)}, u32[]{:S(2)}) %all-to-all-start) | async-done | bytes 4194336 | tf_op jit(solution)/shard_map/all_to_all | solution.py:46
  116.3 4.2 %gather_fusion.1 = bf16[16,32,4,512]{3,1,2,0:T(8,128)(2,1)} fusion(bf16[32,32,4,512]{3,1,2,0:T(8,128)(2,1)} %all-to-all-done, s32[1024]{0:T(1024)S(1)} %pad_clamp_fusion), kind=kCustom, calls=%fused_computation.1 | custom fusion | bytes 4194368 | tf_op jit(solution)/shard_map/gather | solution.py:56
  120.4 2.8 convert_bitcast_fusion
  123.3 12.0 %copy.107 = bf16[256,16,32,4,2,1]{2,1,3,4,5,0:T(8,128)(2,1)} copy(bf16[256,16,32,4,2,1]{0,2,3,1,4,5:T(8,128)(2,1)S(1)} %convert_bitcast_fusion) | data formatting | bytes 4194304 | tf_op jit(solution)/shard_map/convert_element_type | solution.py:57
  135.3 13.4 %fusion = f32[256,2,32,32,1,1]{3,2,5,4,1,0:T(8,128)} fusion(bf16[256,16,32,4,2,1]{2,1,3,4,5,0:T(8,128)(2,1)} %copy.107, bf16[256,16,4,1,2,32]{5,1,2,3,4,0:T(8,128)(2,1)} %get-tuple-element.22, bf16[256,16,4,1,2,32]{5,1,2,3,4,0:T(8,128)(2,1)} %get-tuple-element.21), kind=kOutput, calls=%fused_computation.4 | convolution fusion | flops 136314880 | bytes 8388608 | tf_op jit(solution)/shard_map/flakc,flkcdr->fdar/dot_general | solution.py:58
  148.6 8.0 %copy.95 = f32[256,2,32,8,4]{0,2,4,1,3:T(8,128)} copy(f32[256,2,32,8,4]{2,4,3,1,0:T(4,128)} %bitcast.103) | data formatting | bytes 4194304 | tf_op jit(solution)/shard_map/reshape | solution.py:62
  156.6 0.0 copy-start.3
  156.6 6.5 %all-to-all-start.1 = ((f32[256,2,32,8,4]{0,2,4,1,3:T(8,128)}), f32[256,2,32,8,4]{0,2,4,1,3:T(8,128)S(1)}, u32[]{:S(2)}, u32[]{:S(2)}) async-start(f32[256,2,32,8,4]{0,2,4,1,3:T(8,128)} %copy.95), calls=%async_computation.1 | async-start | bytes 4194304 | tf_op jit(solution)/shard_map/all_to_all | solution.py:63
  163.1 0.0 copy-done.3
  163.1 1.1 copy.91
  164.2 25.0 %all-to-all-done.1 = f32[256,2,32,8,4]{0,2,4,1,3:T(8,128)S(1)} async-done(((f32[256,2,32,8,4]{0,2,4,1,3:T(8,128)}), f32[256,2,32,8,4]{0,2,4,1,3:T(8,128)S(1)}, u32[]{:S(2)}, u32[]{:S(2)}) %all-to-all-start.1) | async-done | bytes 2097184 | tf_op jit(solution)/shard_map/all_to_all | solution.py:63
  189.3 0.2 reduce_sum.31
  189.4 0.5 copy.116
  189.9 1.4 fusion.17
  191.3 0.3 copy.97
  191.7 1.1 broadcast_in_dim.56
  192.8 5.2 %all-to-all-start.2 = ((bf16[256,2,32,8,4]{0,2,4,1,3:T(8,128)(2,1)}), bf16[256,2,32,8,4]{0,2,4,1,3:T(8,128)(2,1)S(1)}, u32[]{:S(2)}, u32[]{:S(2)}) async-start(bf16[256,2,32,8,4]{0,2,4,1,3:T(8,128)(2,1)} %broadcast_in_dim.56), calls=%async_computation.2 | async-start | bytes 2097152 | tf_op jit(solution)/shard_map/all_to_all | solution.py:68
  198.0 2.9 sine_negate_fusion
  200.9 11.5 %all-to-all-done.2 = bf16[256,2,32,8,4]{0,2,4,1,3:T(8,128)(2,1)S(1)} async-done(((bf16[256,2,32,8,4]{0,2,4,1,3:T(8,128)(2,1)}), bf16[256,2,32,8,4]{0,2,4,1,3:T(8,128)(2,1)S(1)}, u32[]{:S(2)}, u32[]{:S(2)}) %all-to-all-start.2) | async-done | bytes 1048608 | tf_op jit(solution)/shard_map/all_to_all | solution.py:68
  212.4 0.1 copy.98
  212.5 7.0 %copy.109 = bf16[256,2,32,32,1,1]{3,2,1,5,4,0:T(8,128)(2,1)} copy(bf16[256,2,32,32,1,1]{0,2,3,1,5,4:T(8,128)(2,1)S(1)} %bitcast.104) | data formatting | bytes 2097152 | tf_op jit(solution)/shard_map/reshape | solution.py:69
  219.4 12.9 %fusion.6 = f32[16,32,4,2,256]{1,0,3,2,4:T(8,128)} fusion(bf16[256,2,32,32,1,1]{3,2,1,5,4,0:T(8,128)(2,1)} %copy.109, bf16[256,16,4,1,2,32]{5,1,2,4,0,3:T(8,128)(2,1)} %get-tuple-element.20, bf16[256,16,4,1,2,32]{5,1,2,4,0,3:T(8,128)(2,1)} %get-tuple-element.19), kind=kOutput, calls=%fused_computation.11 | convolution fusion | flops 136314880 | bytes 9437184 | tf_op jit(solution)/shard_map/fcar,flkecr->lakef/dot_general | solution.py:70
  232.3 15.8 %copy.101 = f32[16,32,4,2,256]{4,3,1,2,0:T(2,128)} copy(f32[16,32,4,2,256]{1,0,3,2,4:T(8,128)} %fusion.6) | data formatting | bytes 8388608 | tf_op jit(solution)/shard_map/fcar,flkecr->lakef/transpose | solution.py:70
  248.1 6.4 %reshape.190 = f32[16,32,4,512]{3,1,2,0:T(8,128)} reshape(f32[16,32,4,2,256]{4,3,1,2,0:T(2,128)} %copy.101) | data formatting | bytes 8388608 | tf_op jit(solution)/shard_map/reshape | solution.py:73
  254.5 8.8 %convolution_convert_fusion = bf16[16,32,4,512]{3,1,2,0:T(8,128)(2,1)S(1)} fusion(f32[16,32,4,512]{3,1,2,0:T(8,128)} %reshape.190, f32[512,256]{1,0:T(8,128)} %get-tuple-element.31, f32[512,256]{1,0:T(8,128)} %get-tuple-element.32), kind=kOutput, calls=%fused_computation.24 | convolution fusion | flops 6443761664 | bytes 7340032 | tf_op jit(solution)/shard_map/dot_general | solution.py:74
  263.3 2.5 broadcast_in_dim.54
  265.8 5.2 %scatter_fusion = bf16[32,32,4,512]{3,1,2,0:T(8,128)(2,1)} fusion(bf16[32,32,4,512]{3,1,2,0:T(8,128)(2,1)} %broadcast_in_dim.54, s32[16]{0:T(128)S(1)} %fusion.40, bf16[16,32,4,512]{3,1,2,0:T(8,128)(2,1)S(1)} %convolution_convert_fusion), kind=kCustom, calls=%fused_computation.2 | custom fusion | bytes 6291520 | tf_op jit(solution)/shard_map/scatter | solution.py:76
  271.1 8.1 %all-to-all-start.3 = ((bf16[32,32,4,512]{3,1,2,0:T(8,128)(2,1)}), bf16[32,32,4,512]{3,1,2,0:T(8,128)(2,1)}, u32[]{:S(2)}, u32[]{:S(2)}) async-start(bf16[32,32,4,512]{3,1,2,0:T(8,128)(2,1)} %scatter_fusion), calls=%async_computation.3 | async-start | bytes 8388608 | tf_op jit(solution)/shard_map/all_to_all | solution.py:77
  279.2 1.2 copy.105
  280.4 93.5 %all-to-all-done.3 = bf16[32,32,4,512]{3,1,2,0:T(8,128)(2,1)} async-done(((bf16[32,32,4,512]{3,1,2,0:T(8,128)(2,1)}), bf16[32,32,4,512]{3,1,2,0:T(8,128)(2,1)}, u32[]{:S(2)}, u32[]{:S(2)}) %all-to-all-start.3) | async-done | bytes 4194336 | tf_op jit(solution)/shard_map/all_to_all | solution.py:77
  373.8 3.4 convert_element_type.56
  377.2 0.0 copy-start.2
  377.2 1.7 select_reduce_fusion
  379.0 0.0 copy-done.2
  379.0 0.2 fusion.45
  379.2 1.1 copy.103
  380.3 0.9 copy.104
  (5 shorter events, 0.0 us)
Async XLA Ops:
  10.5 105.8 %all-to-all-start = ((bf16[32,32,4,512]{3,1,2,0:T(8,128)(2,1)}), bf16[32,32,4,512]{3,1,2,0:T(8,128)(2,1)}, u32[]{:S(2)}, u32[]{:S(2)}) async-start(bf16[32,32,4,512]{3,1,2,0:T(8,128)(2,1)} %broadcast_select_fusion), calls=%async_computation | async-start | bytes 8388608 | tf_op jit(solution)/shard_map/all_to_all | solution.py:46
  23.4 13.0 %copy-start.4 = (s32[32,16]{0,1:T(8,128)S(1)}, s32[32,16]{0,1:T(8,128)}, u32[]{:S(2)}) copy-start(s32[32,16]{0,1:T(8,128)} %param.7) | copy-start | bytes 6148
  38.8 6.7 %copy-start = (bf16[1,16,1,4,32,256]{4,1,3,5,2,0:T(8,128)(2,1)S(1)}, bf16[1,16,1,4,32,256]{4,1,3,5,2,0:T(8,128)(2,1)}, u32[]{:S(2)}) copy-start(bf16[1,16,1,4,32,256]{4,1,3,5,2,0:T(8,128)(2,1)} %copy.117) | copy-start | bytes 3145732
  38.8 6.7 %copy-start.1 = (bf16[1,16,1,4,32,256]{4,1,3,5,2,0:T(8,128)(2,1)S(1)}, bf16[1,16,1,4,32,256]{4,1,3,5,2,0:T(8,128)(2,1)}, u32[]{:S(2)}) copy-start(bf16[1,16,1,4,32,256]{4,1,3,5,2,0:T(8,128)(2,1)} %copy.118) | copy-start | bytes 3145732
  156.6 6.5 %copy-start.3 = (bf16[1,2,32,4,256]{4,3,2,1,0:T(4,128)(2,1)S(1)}, bf16[1,2,32,4,256]{4,3,2,1,0:T(4,128)(2,1)}, u32[]{:S(2)}) copy-start(bf16[1,2,32,4,256]{4,3,2,1,0:T(4,128)(2,1)} %param.6) | copy-start | bytes 393220
  156.6 32.6 %all-to-all-start.1 = ((f32[256,2,32,8,4]{0,2,4,1,3:T(8,128)}), f32[256,2,32,8,4]{0,2,4,1,3:T(8,128)S(1)}, u32[]{:S(2)}, u32[]{:S(2)}) async-start(f32[256,2,32,8,4]{0,2,4,1,3:T(8,128)} %copy.95), calls=%async_computation.1 | async-start | bytes 4194304 | tf_op jit(solution)/shard_map/all_to_all | solution.py:63
  192.8 19.6 %all-to-all-start.2 = ((bf16[256,2,32,8,4]{0,2,4,1,3:T(8,128)(2,1)}), bf16[256,2,32,8,4]{0,2,4,1,3:T(8,128)(2,1)S(1)}, u32[]{:S(2)}, u32[]{:S(2)}) async-start(bf16[256,2,32,8,4]{0,2,4,1,3:T(8,128)(2,1)} %broadcast_in_dim.56), calls=%async_computation.2 | async-start | bytes 2097152 | tf_op jit(solution)/shard_map/all_to_all | solution.py:68
  271.1 102.8 %all-to-all-start.3 = ((bf16[32,32,4,512]{3,1,2,0:T(8,128)(2,1)}), bf16[32,32,4,512]{3,1,2,0:T(8,128)(2,1)}, u32[]{:S(2)}, u32[]{:S(2)}) async-start(bf16[32,32,4,512]{3,1,2,0:T(8,128)(2,1)} %scatter_fusion), calls=%async_computation.3 | async-start | bytes 8388608 | tf_op jit(solution)/shard_map/all_to_all | solution.py:77
  377.2 1.8 copy-start.2
where the time goes:
time: 383 us; the launch traced here: 381 us
  waiting for transfers between devices  186 us (49%)
  local copies, waits for them, and re-layouts  86.3 us (23%)
  other arithmetic  39.3 us (10%)
  matrix products  37.9 us (10%)
  starting transfers between devices  30.9 us (8%)
    all_to_all x1, waiting for transfers between devices, per_device(): lax.all_to_all(returning, 'target', split_axis=0, concat_axis=0, tiled=True)  93.5 us
    all_to_all x1, waiting for transfers between devices, per_device(): lax.all_to_all(outgoing, 'target', split_axis=0, concat_axis=0, tiled=True)  56.1 us
    all_to_all x1, waiting for transfers between devices, per_device(): lax.all_to_all(split_value, 'surface', split_axis=3, concat_axis=3, tiled...  25 us
    unnamed x18, local copies, waits for them, and re-layouts  19 us
    transpose x1, local copies, waits for them, and re-layouts, per_device(): jnp.einsum('fcar,flkecr->lakef', misfit, backward, preferred_element_type...  15.8 us
    another operation x1, other arithmetic, per_device(): jnp.stack([jnp.stack([-data_real, -data_imag], 3), jnp.stack([data_imag,...  14.7 us
    dot_general x1, matrix products, per_device(): jnp.einsum('flakc,flkcdr->fdar', spectra, forward, preferred_element_type...  13.4 us
    dot_general x1, matrix products, per_device(): jnp.einsum('fcar,flkecr->lakef', misfit, backward, preferred_element_type...  12.9 us
  transfers between devices with their start and end apart: 4, of which 4 were waited for; matrix products, arithmetic and copies ran while one was open for 11% of the time, Pallas kernels for 0%

commit v1 on v0

--- a/solution.py
+++ b/solution.py
@@ -6,6 +6,7 @@
 from jax.sharding import PartitionSpec as P
 
 step_length = 0.5
+chunks = 2
 
 
 def make_table(samples):
@@ -43,7 +44,7 @@
     zero_half = jnp.zeros((), jnp.bfloat16)
     copy_now = response.astype(jnp.bfloat16)
     outgoing = jnp.where(present_rows, copy_now[slot_for], zero_half)
-    arrived = lax.all_to_all(outgoing, "target", split_axis=0, concat_axis=0, tiled=True)
+    arrived = lax.all_to_all(outgoing, "target", split_axis=0, concat_axis=0, tiled=True) if chunks == 1 else None
     data_real = jnp.moveaxis(data_spectra[0, :, 0], -1, 0)
     data_imag = jnp.moveaxis(data_spectra[0, :, 1], -1, 0)
     forward = jnp.stack(
@@ -52,12 +53,22 @@
     backward = jnp.stack(
         [jnp.stack([-data_real, -data_imag], 3), jnp.stack([data_imag, -data_real], 3)], 3
     )
-    spectra = jnp.einsum(
-        "lakn,ncf->flakc", arrived[own_owner], table_half, preferred_element_type=jnp.float32
-    ).astype(jnp.bfloat16)
-    partial_value = jnp.einsum(
-        "flakc,flkcdr->fdar", spectra, forward, preferred_element_type=jnp.float32
-    )
+    positions = response.shape[2]
+    width = positions // chunks
+    partial_value = None
+    for c in range(chunks):
+        lo, hi = c * width, (c + 1) * width
+        piece = outgoing if chunks == 1 else outgoing[:, :, lo:hi]
+        arrived_c = arrived if chunks == 1 else lax.all_to_all(
+            piece, "target", split_axis=0, concat_axis=0, tiled=True
+        )
+        spectra = jnp.einsum(
+            "lakn,ncf->flakc", arrived_c[own_owner], table_half, preferred_element_type=jnp.float32
+        ).astype(jnp.bfloat16)
+        partial_c = jnp.einsum(
+            "flakc,flkcdr->fdar", spectra, forward[:, :, lo:hi], preferred_element_type=jnp.float32
+        )
+        partial_value = partial_c if partial_value is None else partial_value + partial_c
     f_dim, parts, shots, recvs = partial_value.shape
     split_value = partial_value.reshape(f_dim, parts, shots, channels, recvs // channels)
     exchanged = lax.all_to_all(split_value, "surface", split_axis=3, concat_axis=3, tiled=True)
@@ -67,19 +78,23 @@
     spread = jnp.broadcast_to(misfit_share[:, :, :, None], misfit_share.shape[:3] + (channels,) + misfit_share.shape[3:])
     gathered = lax.all_to_all(spread, "surface", split_axis=3, concat_axis=3, tiled=True)
     misfit = gathered.reshape(f_dim, parts, shots, recvs)
-    grad_spectra = jnp.einsum(
-        "fcar,flkecr->lakef", misfit, backward, preferred_element_type=jnp.float32
-    )
-    grad_flat = grad_spectra.reshape(grad_spectra.shape[:3] + (samples,))
-    grad_time = jnp.dot(grad_flat, dft_table.T, precision=lax.Precision.HIGHEST)
-    grad_half = grad_time.astype(jnp.bfloat16)
-    returning = jnp.zeros((owners,) + grad_time.shape[1:], jnp.bfloat16).at[own_owner].set(grad_half)
-    received = lax.all_to_all(returning, "target", split_axis=0, concat_axis=0, tiled=True)
-    taken = jnp.where(
-        chosen[:, :, None, None, None], received[None].astype(jnp.float32), jnp.zeros((), jnp.float32)
-    )
-    gradient = jnp.sum(taken, axis=1)
-    response_next = response - step_length * gradient
+    next_parts = []
+    for c in range(chunks):
+        lo, hi = c * width, (c + 1) * width
+        grad_spectra = jnp.einsum(
+            "fcar,flkecr->lakef", misfit, backward[:, :, lo:hi], preferred_element_type=jnp.float32
+        )
+        grad_flat = grad_spectra.reshape(grad_spectra.shape[:3] + (samples,))
+        grad_time = jnp.dot(grad_flat, dft_table.T, precision=lax.Precision.HIGHEST)
+        grad_half = grad_time.astype(jnp.bfloat16)
+        returning = jnp.zeros((owners,) + grad_time.shape[1:], jnp.bfloat16).at[own_owner].set(grad_half)
+        received = lax.all_to_all(returning, "target", split_axis=0, concat_axis=0, tiled=True)
+        taken = jnp.where(
+            chosen[:, :, None, None, None], received[None].astype(jnp.float32), jnp.zeros((), jnp.float32)
+        )
+        gradient = jnp.sum(taken, axis=1)
+        next_parts.append(response[:, :, lo:hi] - step_length * gradient)
+    response_next = next_parts[0] if chunks == 1 else jnp.concatenate(next_parts, axis=2)
     return (response_next, response_next.astype(jnp.bfloat16), residual_share[None])
 
 

time: 383 us -> 399 us (1.042); the launches traced: 381 us -> 393 us
  waiting for transfers between devices: 186 us -> 133 us
  local copies, waits for them, and re-layouts: 86.3 us -> 107 us
  matrix products: 37.9 us -> 56.9 us
  starting transfers between devices: 30.9 us -> 44.7 us
  other arithmetic: 39.3 us -> 49.7 us
    all_to_all x1 -> x2, waiting for transfers between devices: 93.5 us -> 59.3 us  [per_device(): lax.all_to_all(returning, 'target', split_axis=0, concat_axis=0, tiled=True)]
    dot_general x3 -> x6, matrix products: 29.1 us -> 45.8 us  [the longest x2 22.9 us: per_device(): jnp.einsum('flakc,flkcdr->fdar', spectra, forward[:, :, lo:hi], preferred...]
    all_to_all x1, waiting for transfers between devices: 11.5 us -> 0.1 us  [per_device(): lax.all_to_all(spread, 'surface', split_axis=3, concat_axis=3, tiled=True)]
    another operation x1 -> x2, other arithmetic: 14.7 us -> 23.7 us  [per_device(): jnp.stack([jnp.stack([-data_real, -data_imag], 3), jnp.stack([data_imag,...]
    all_to_all x1 -> x2, starting transfers between devices: 8.1 us -> 15.8 us  [per_device(): lax.all_to_all(returning, 'target', split_axis=0, concat_axis=0, tiled=True)]
    slice x0 -> x2, local copies, waits for them, and re-layouts: none -> 7.02 us  [the longest x1 4.84 us: per_device(): piece = outgoing if chunks == 1 else outgoing[:, :, lo:hi]]
    all_to_all x1 -> x2, waiting for transfers between devices: 56.1 us -> 49.4 us  [per_device(): lax.all_to_all(piece, 'target', split_axis=0, concat_axis=0, tiled=True)]
    all_to_all x1 -> x2, starting transfers between devices: 11.1 us -> 17.1 us  [per_device(): lax.all_to_all(piece, 'target', split_axis=0, concat_axis=0, tiled=True)]
  transfers between devices with their start and end apart: 4 -> 6, of which waited for: 4 -> 5; matrix products, arithmetic and copies ran while one was open for 11% -> 27% of each run, Pallas kernels for 0% -> 0%
where the time goes in v1:
time: 399 us; the launch traced here: 393 us
  waiting for transfers between devices  133 us (33%)
  local copies, waits for them, and re-layouts  107 us (27%)
  matrix products  56.9 us (14%)
  other arithmetic  49.7 us (12%)
  starting transfers between devices  44.7 us (11%)
    all_to_all x2, waiting for transfers between devices, per_device(): lax.all_to_all(returning, 'target', split_axis=0, concat_axis=0, tiled=True)  59.3 us
    all_to_all x2, waiting for transfers between devices, per_device(): lax.all_to_all(piece, 'target', split_axis=0, concat_axis=0, tiled=True)  49.4 us
    all_to_all x1, waiting for transfers between devices, per_device(): lax.all_to_all(split_value, 'surface', split_axis=3, concat_axis=3, tiled...  23.9 us
    another operation x2, other arithmetic, per_device(): jnp.stack([jnp.stack([-data_real, -data_imag], 3), jnp.stack([data_imag,...  23.7 us
    dot_general x2, matrix products, per_device(): jnp.einsum('flakc,flkcdr->fdar', spectra, forward[:, :, lo:hi], preferred...  22.9 us
    unnamed x21, local copies, waits for them, and re-layouts  21.3 us
    dot_general x2, matrix products, per_device(): jnp.einsum('fcar,flkecr->lakef', misfit, backward[:, :, lo:hi], preferred...  20.2 us
    all_to_all x2, starting transfers between devices, per_device(): lax.all_to_all(piece, 'target', split_axis=0, concat_axis=0, tiled=True)  17.1 us
  transfers between devices with their start and end apart: 6, of which 5 were waited for; matrix products, arithmetic and copies ran while one was open for 27% of the time, Pallas kernels for 0%

profile of v1, /device:TPU:1, one launch (start us, length us, event | category | flops | bytes accessed | tf_op | source)
XLA Modules:
  0.0 392.7 jit_solution(16248530862039707689)
XLA Ops:
  0.6 0.7 fusion.51
  1.4 0.7 fusion.39
  2.1 1.1 convert_element_type.63
  3.2 5.6 %gather_fusion = bf16[32,32,4,512]{3,2,1,0:T(4,128)(2,1)} fusion(bf16[2,32,4,512]{3,2,1,0:T(4,128)(2,1)S(1)} %convert_element_type.63, s32[1024]{0:T(1024)S(1)} %pad_clamp_fusion.1), kind=kCustom, calls=%fused_computation | custom fusion | bytes 8388736 | tf_op jit(solution)/shard_map/gather | solution.py:46
  8.9 4.0 %broadcast_select_fusion = bf16[32,32,4,512]{3,2,1,0:T(4,128)(2,1)S(1)} fusion(bf16[32,32,4,512]{3,2,1,0:T(4,128)(2,1)} %gather_fusion, pred[32]{0:T(512)(128)(4,1)S(1)} %get-tuple-element.17), kind=kLoop, calls=%fused_computation.27 | loop fusion | flops 2097152 | bytes 8388640 | tf_op jit(solution)/shard_map/jit(_where)/select_n | solution.py:46
  12.8 4.8 %fusion.53 = (bf16[32,32,2,512]{3,2,1,0:T(2,128)(2,1)}, bf16[32,32,2,512]{3,2,1,0:T(2,128)(2,1)}) fusion(bf16[32,32,4,512]{3,2,1,0:T(4,128)(2,1)S(1)} %broadcast_select_fusion), kind=kLoop, calls=%fused_computation.103 | loop fusion | bytes 8388608 | tf_op jit(solution)/shard_map/slice | solution.py:61
  17.7 11.1 %all-to-all-start.1 = ((bf16[32,32,2,512]{3,2,1,0:T(2,128)(2,1)}), bf16[32,32,2,512]{3,2,1,0:T(2,128)(2,1)S(1)}, u32[]{:S(2)}, u32[]{:S(2)}) async-start(bf16[32,32,2,512]{3,2,1,0:T(2,128)(2,1)} %get-tuple-element.26), calls=%async_computation.1 | async-start | bytes 4194304 | tf_op jit(solution)/shard_map/all_to_all | solution.py:62
  28.7 49.4 %all-to-all-done.1 = bf16[32,32,2,512]{3,2,1,0:T(2,128)(2,1)S(1)} async-done(((bf16[32,32,2,512]{3,2,1,0:T(2,128)(2,1)}), bf16[32,32,2,512]{3,2,1,0:T(2,128)(2,1)S(1)}, u32[]{:S(2)}, u32[]{:S(2)}) %all-to-all-start.1) | async-done | bytes 2097184 | tf_op jit(solution)/shard_map/all_to_all | solution.py:62
  78.1 6.0 %all-to-all-start = ((bf16[32,32,2,512]{3,2,1,0:T(2,128)(2,1)}), bf16[32,32,2,512]{3,2,1,0:T(2,128)(2,1)}, u32[]{:S(2)}, u32[]{:S(2)}) async-start(bf16[32,32,2,512]{3,2,1,0:T(2,128)(2,1)} %get-tuple-element.25), calls=%async_computation | async-start | bytes 4194304 | tf_op jit(solution)/shard_map/all_to_all | solution.py:62
  84.1 3.2 fusion.54
  87.4 7.3 %copy.154 = bf16[1,16,1,4,32,256]{4,1,3,5,2,0:T(8,128)(2,1)} copy(bf16[1,16,1,4,32,256]{5,4,3,2,1,0:T(8,128)(2,1)} %get-tuple-element.28) | data formatting | bytes 2097152
  94.6 7.3 %copy.155 = bf16[1,16,1,4,32,256]{4,1,3,5,2,0:T(8,128)(2,1)} copy(bf16[1,16,1,4,32,256]{5,4,3,2,1,0:T(8,128)(2,1)} %get-tuple-element.27) | data formatting | bytes 2097152
  102.1 2.0 cosine_convert_fusion
  104.1 2.0 negate_convert_fusion
  106.2 2.9 fusion.7
  109.0 0.6 copy-done.1
  109.6 0.5 fusion.8
  110.1 1.6 copy-done
  111.8 11.4 %maximum_bitcast_fusion.1 = (bf16[256,16,4,1,2,32]{5,1,2,4,0,3:T(8,128)(2,1)}, bf16[256,16,4,1,2,32]{5,1,2,3,4,0:T(8,128)(2,1)}, bf16[256,16,4,1,2,32]{5,1,2,3,4,0:T(8,128)(2,1)}, bf16[256,16,4,1,2,32]{5,1,2,4,0,3:T(8,128)(2,1)}) fusion(bf16[256,16,4,1,32]{4,1,2,3,0:T(8,128)(2,1)S(1)} %fusion.7, bf16[256,16,4,1,32]{4,1,2,3,0:T(8,128)(2,1)S(1)} %bitcast.124, ...), kind=kLoop, calls=%fused_computation.13 | loop fusion | flops 4194304 | bytes 12582912 | tf_op jit(solution)/shard_map/stack | solution.py:53
  123.2 3.6 gather_fusion.2
  126.8 1.9 fusion.16
  128.7 6.9 %copy.138 = bf16[256,16,32,2,2,1]{2,1,3,4,5,0:T(8,128)(2,1)} copy(bf16[256,16,32,2,2,1]{0,2,3,1,4,5:T(8,128)(2,1)S(1)} %fusion.16) | data formatting | bytes 2097152 | tf_op jit(solution)/shard_map/convert_element_type | solution.py:67
  135.6 4.2 %gather_fusion.1 = bf16[16,32,2,512]{3,2,1,0:T(2,128)(2,1)S(1)} fusion(bf16[32,32,2,512]{3,2,1,0:T(2,128)(2,1)} %all-to-all-done, s32[1024]{0:T(1024)S(1)} %pad_clamp_fusion), kind=kCustom, calls=%fused_computation.1 | custom fusion | bytes 2097216 | tf_op jit(solution)/shard_map/gather | solution.py:66
  139.9 0.7 fusion.15
  140.6 6.5 %copy.136 = bf16[256,16,32,2,2,1]{2,1,3,4,5,0:T(8,128)(2,1)} copy(bf16[256,16,32,2,2,1]{0,2,3,1,4,5:T(8,128)(2,1)S(1)} %fusion.15) | data formatting | bytes 2097152 | tf_op jit(solution)/shard_map/convert_element_type | solution.py:67
  147.1 10.3 %fusion = f32[256,2,32,32,1,1]{3,2,5,4,1,0:T(8,128)} fusion(bf16[256,16,32,2,2,1]{2,1,3,4,5,0:T(8,128)(2,1)} %copy.138, bf16[256,16,4,1,2,32]{5,1,2,3,4,0:T(8,128)(2,1)} %get-tuple-element.23, bf16[256,16,4,1,2,32]{5,1,2,3,4,0:T(8,128)(2,1)} %get-tuple-element.22), kind=kOutput, calls=%fused_computation.8 | convolution fusion | flops 75497472 | bytes 7340032 | tf_op jit(solution)/shard_map/flakc,flkcdr->fdar/dot_general | solution.py:68
  157.4 12.7 %bitcast_add_fusion = f32[256,2,32,32]{3,2,1,0:T(8,128)} fusion(f32[256,2,32,32,1,1]{3,2,5,4,1,0:T(8,128)} %fusion, bf16[256,16,32,2,2,1]{2,1,3,4,5,0:T(8,128)(2,1)} %copy.136, bf16[256,16,4,1,2,32]{5,1,2,3,4,0:T(8,128)(2,1)} %get-tuple-element.23, bf16[256,16,4,1,2,32]{5,1,2,3,4,0:T(8,128)(2,1)} %get-tuple-element.22), kind=kOutput, calls=%fused_computation.16 | convolution fusion | flops 76021760 | bytes 9437184 | tf_op jit(solution)/shard_map/flakc,flkcdr->fdar/dot_general | solution.py:68
  170.0 8.0 %copy.121 = f32[256,2,32,8,4]{0,2,4,1,3:T(8,128)} copy(f32[256,2,32,8,4]{2,4,3,1,0:T(4,128)} %bitcast.125) | data formatting | bytes 4194304 | tf_op jit(solution)/shard_map/reshape | solution.py:73
  178.0 6.5 %all-to-all-start.2 = ((f32[256,2,32,8,4]{0,2,4,1,3:T(8,128)}), f32[256,2,32,8,4]{0,2,4,1,3:T(8,128)S(1)}, u32[]{:S(2)}, u32[]{:S(2)}) async-start(f32[256,2,32,8,4]{0,2,4,1,3:T(8,128)} %copy.121), calls=%async_computation.2 | async-start | bytes 4194304 | tf_op jit(solution)/shard_map/all_to_all | solution.py:74
  184.5 0.3 copy.115
  184.9 1.9 fusion.36
  186.8 23.9 %all-to-all-done.2 = f32[256,2,32,8,4]{0,2,4,1,3:T(8,128)S(1)} async-done(((f32[256,2,32,8,4]{0,2,4,1,3:T(8,128)}), f32[256,2,32,8,4]{0,2,4,1,3:T(8,128)S(1)}, u32[]{:S(2)}, u32[]{:S(2)}) %all-to-all-start.2) | async-done | bytes 2097184 | tf_op jit(solution)/shard_map/all_to_all | solution.py:74
  210.9 0.5 copy.153
  211.4 1.3 fusion.21
  212.7 0.3 copy.123
  213.0 1.2 broadcast_in_dim.68
  214.2 5.4 %all-to-all-start.3 = ((bf16[256,2,32,8,4]{0,2,4,1,3:T(8,128)(2,1)}), bf16[256,2,32,8,4]{0,2,4,1,3:T(8,128)(2,1)S(1)}, u32[]{:S(2)}, u32[]{:S(2)}) async-start(bf16[256,2,32,8,4]{0,2,4,1,3:T(8,128)(2,1)} %broadcast_in_dim.68), calls=%async_computation.3 | async-start | bytes 2097152 | tf_op jit(solution)/shard_map/all_to_all | solution.py:79
  219.6 1.9 sine_negate_fusion
  221.5 12.3 %pad_maximum_fusion.3 = (bf16[256,16,2,2,2,32]{5,1,2,4,0,3:T(8,128)(2,1)}, bf16[256,16,2,2,2,32]{5,1,2,4,0,3:T(8,128)(2,1)}) fusion(bf16[256,16,4,1,2,32]{5,1,2,4,0,3:T(8,128)(2,1)} %get-tuple-element.21, bf16[256,16,4,1,2,32]{5,1,2,4,0,3:T(8,128)(2,1)} %get-tuple-element.24), kind=kLoop, calls=%fused_computation.11 | loop fusion | flops 2097152 | bytes 8388608 | tf_op jit(solution)/shard_map/stack | solution.py:53
  234.0 6.8 %copy.140 = bf16[256,2,32,32,1,1]{3,2,1,5,4,0:T(8,128)(2,1)} copy(bf16[256,2,32,32,1,1]{0,2,3,1,5,4:T(8,128)(2,1)S(1)} %bitcast.126) | data formatting | bytes 2097152 | tf_op jit(solution)/shard_map/reshape | solution.py:80
  240.8 10.1 %fusion.12 = f32[16,32,2,2,256]{1,0,3,2,4:T(8,128)} fusion(bf16[256,2,32,32,1,1]{3,2,1,5,4,0:T(8,128)(2,1)} %copy.140, bf16[256,16,2,2,2,32]{5,1,2,4,0,3:T(8,128)(2,1)} %get-tuple-element.19), kind=kOutput, calls=%fused_computation.29 | convolution fusion | flops 67108864 | bytes 5242880 | tf_op jit(solution)/shard_map/fcar,flkecr->lakef/dot_general | solution.py:84
  250.9 7.5 %copy.131 = f32[16,32,2,2,256]{4,3,1,2,0:T(2,128)S(1)} copy(f32[16,32,2,2,256]{1,0,3,2,4:T(8,128)} %fusion.12) | data formatting | bytes 4194304 | tf_op jit(solution)/shard_map/fcar,flkecr->lakef/transpose | solution.py:84
  258.5 2.7 reshape.196
  261.2 5.1 %convolution_convert_fusion = bf16[16,32,2,512]{3,1,2,0:T(8,128)(2,1)S(1)} fusion(f32[16,32,2,512]{3,1,2,0:T(8,128)} %reshape.196, f32[512,256]{1,0:T(8,128)S(1)} %sine_negate_fusion, f32[512,256]{1,0:T(8,128)S(1)} %fusion.36), kind=kOutput, calls=%fused_computation.30 | convolution fusion | flops 3222011904 | bytes 4194304 | tf_op jit(solution)/shard_map/dot_general | solution.py:88
  266.3 1.6 broadcast.181.clone.1
  267.8 3.2 scatter_fusion.1
  271.1 9.7 %all-to-all-start.5 = ((bf16[32,32,2,512]{3,1,2,0:T(8,128)(2,1)}), bf16[32,32,2,512]{3,1,2,0:T(8,128)(2,1)S(1)}, u32[]{:S(2)}, u32[]{:S(2)}) async-start(bf16[32,32,2,512]{3,1,2,0:T(8,128)(2,1)} %scatter_fusion.1), calls=%async_computation.5 | async-start | bytes 4194304 | tf_op jit(solution)/shard_map/all_to_all | solution.py:91
  280.8 10.1 %fusion.9 = f32[16,32,2,2,256]{1,0,3,2,4:T(8,128)} fusion(bf16[256,2,32,32,1,1]{3,2,1,5,4,0:T(8,128)(2,1)} %copy.140, bf16[256,16,2,2,2,32]{5,1,2,4,0,3:T(8,128)(2,1)} %get-tuple-element.20), kind=kOutput, calls=%fused_computation.28 | convolution fusion | flops 67108864 | bytes 5242880 | tf_op jit(solution)/shard_map/fcar,flkecr->lakef/dot_general | solution.py:84
  290.9 8.5 %copy.127 = f32[16,32,2,2,256]{4,3,1,2,0:T(2,128)} copy(f32[16,32,2,2,256]{1,0,3,2,4:T(8,128)} %fusion.9) | data formatting | bytes 4194304 | tf_op jit(solution)/shard_map/fcar,flkecr->lakef/transpose | solution.py:84
  299.4 4.0 %reshape.195 = f32[16,32,2,512]{3,1,2,0:T(8,128)} reshape(f32[16,32,2,2,256]{4,3,1,2,0:T(2,128)} %copy.127) | data formatting | bytes 4194304 | tf_op jit(solution)/shard_map/reshape | solution.py:87
  303.3 6.1 %convolution_convert_fusion.1 = bf16[16,32,2,512]{3,1,2,0:T(8,128)(2,1)} fusion(f32[16,32,2,512]{3,1,2,0:T(8,128)} %reshape.195, f32[512,256]{1,0:T(8,128)S(1)} %sine_negate_fusion, f32[512,256]{1,0:T(8,128)S(1)} %fusion.36), kind=kOutput, calls=%fused_computation.31 | convolution fusion | flops 3222011904 | bytes 4194304 | tf_op jit(solution)/shard_map/dot_general | solution.py:88
  309.4 1.6 broadcast.181.clone
  311.0 3.4 scatter_fusion
  314.4 15.8 %all-to-all-done.5 = bf16[32,32,2,512]{3,1,2,0:T(8,128)(2,1)S(1)} async-done(((bf16[32,32,2,512]{3,1,2,0:T(8,128)(2,1)}), bf16[32,32,2,512]{3,1,2,0:T(8,128)(2,1)S(1)}, u32[]{:S(2)}, u32[]{:S(2)}) %all-to-all-start.5) | async-done | bytes 2097184 | tf_op jit(solution)/shard_map/all_to_all | solution.py:91
  330.2 6.1 %all-to-all-start.4 = ((bf16[32,32,2,512]{3,1,2,0:T(8,128)(2,1)}), bf16[32,32,2,512]{3,1,2,0:T(8,128)(2,1)}, u32[]{:S(2)}, u32[]{:S(2)}) async-start(bf16[32,32,2,512]{3,1,2,0:T(8,128)(2,1)} %scatter_fusion), calls=%async_computation.4 | async-start | bytes 4194304 | tf_op jit(solution)/shard_map/all_to_all | solution.py:91
  336.3 2.2 fusion.55
  338.5 1.2 copy.134
  339.6 2.5 convert_element_type.73
  342.2 43.5 %all-to-all-done.4 = bf16[32,32,2,512]{3,1,2,0:T(8,128)(2,1)} async-done(((bf16[32,32,2,512]{3,1,2,0:T(8,128)(2,1)}), bf16[32,32,2,512]{3,1,2,0:T(8,128)(2,1)}, u32[]{:S(2)}, u32[]{:S(2)}) %all-to-all-start.4) | async-done | bytes 2097184 | tf_op jit(solution)/shard_map/all_to_all | solution.py:91
  385.7 2.3 convert_element_type.71
  388.0 0.5 copy-done.2
  388.5 1.6 select_reduce_fusion.1
  390.4 0.9 copy.133
  391.3 1.1 copy.132
  (24 shorter events, 0.8 us)
Async XLA Ops:
  17.7 60.5 %all-to-all-start.1 = ((bf16[32,32,2,512]{3,2,1,0:T(2,128)(2,1)}), bf16[32,32,2,512]{3,2,1,0:T(2,128)(2,1)S(1)}, u32[]{:S(2)}, u32[]{:S(2)}) async-start(bf16[32,32,2,512]{3,2,1,0:T(2,128)(2,1)} %get-tuple-element.26), calls=%async_computation.1 | async-start | bytes 4194304 | tf_op jit(solution)/shard_map/all_to_all | solution.py:62
  78.1 57.5 %all-to-all-start = ((bf16[32,32,2,512]{3,2,1,0:T(2,128)(2,1)}), bf16[32,32,2,512]{3,2,1,0:T(2,128)(2,1)}, u32[]{:S(2)}, u32[]{:S(2)}) async-start(bf16[32,32,2,512]{3,2,1,0:T(2,128)(2,1)} %get-tuple-element.25), calls=%async_computation | async-start | bytes 4194304 | tf_op jit(solution)/shard_map/all_to_all | solution.py:62
  87.4 14.6 %copy-start.6 = (s32[32,16]{0,1:T(8,128)S(1)}, s32[32,16]{0,1:T(8,128)}, u32[]{:S(2)}) copy-start(s32[32,16]{0,1:T(8,128)} %param.7) | copy-start | bytes 6148
  106.1 3.5 copy-start.1
  109.6 2.2 copy-start
  178.0 6.5 %copy-start.5 = (bf16[1,2,32,4,256]{4,3,2,1,0:T(4,128)(2,1)S(1)}, bf16[1,2,32,4,256]{4,3,2,1,0:T(4,128)(2,1)}, u32[]{:S(2)}) copy-start(bf16[1,2,32,4,256]{4,3,2,1,0:T(4,128)(2,1)} %param.6) | copy-start | bytes 393220
  178.0 32.7 %all-to-all-start.2 = ((f32[256,2,32,8,4]{0,2,4,1,3:T(8,128)}), f32[256,2,32,8,4]{0,2,4,1,3:T(8,128)S(1)}, u32[]{:S(2)}, u32[]{:S(2)}) async-start(f32[256,2,32,8,4]{0,2,4,1,3:T(8,128)} %copy.121), calls=%async_computation.2 | async-start | bytes 4194304 | tf_op jit(solution)/shard_map/all_to_all | solution.py:74
  214.2 19.7 %all-to-all-start.3 = ((bf16[256,2,32,8,4]{0,2,4,1,3:T(8,128)(2,1)}), bf16[256,2,32,8,4]{0,2,4,1,3:T(8,128)(2,1)S(1)}, u32[]{:S(2)}, u32[]{:S(2)}) async-start(bf16[256,2,32,8,4]{0,2,4,1,3:T(8,128)(2,1)} %broadcast_in_dim.68), calls=%async_computation.3 | async-start | bytes 2097152 | tf_op jit(solution)/shard_map/all_to_all | solution.py:79
  271.1 59.1 %all-to-all-start.5 = ((bf16[32,32,2,512]{3,1,2,0:T(8,128)(2,1)}), bf16[32,32,2,512]{3,1,2,0:T(8,128)(2,1)S(1)}, u32[]{:S(2)}, u32[]{:S(2)}) async-start(bf16[32,32,2,512]{3,1,2,0:T(8,128)(2,1)} %scatter_fusion.1), calls=%async_computation.5 | async-start | bytes 4194304 | tf_op jit(solution)/shard_map/all_to_all | solution.py:91
  311.0 27.5 %copy-start.3 = (f32[1,2,32,4,256]{2,3,1,4,0:T(4,128)S(1)}, f32[1,2,32,4,256]{2,3,1,4,0:T(4,128)}, u32[]{:S(2)}) copy-start(f32[1,2,32,4,256]{2,3,1,4,0:T(4,128)} %get-tuple-element.29) | copy-start | bytes 786436
  330.2 55.5 %all-to-all-start.4 = ((bf16[32,32,2,512]{3,1,2,0:T(8,128)(2,1)}), bf16[32,32,2,512]{3,1,2,0:T(8,128)(2,1)}, u32[]{:S(2)}, u32[]{:S(2)}) async-start(bf16[32,32,2,512]{3,1,2,0:T(8,128)(2,1)} %scatter_fusion), calls=%async_computation.4 | async-start | bytes 4194304 | tf_op jit(solution)/shard_map/all_to_all | solution.py:91
  385.7 2.8 copy-start.2
  388.5 1.6 copy-start.4

commit v2 on v0

--- a/solution.py
+++ b/solution.py
@@ -60,8 +60,10 @@
     )
     f_dim, parts, shots, recvs = partial_value.shape
     split_value = partial_value.reshape(f_dim, parts, shots, channels, recvs // channels)
-    exchanged = lax.all_to_all(split_value, "surface", split_axis=3, concat_axis=3, tiled=True)
-    summed_share = jnp.moveaxis(jnp.sum(exchanged, axis=3), 0, -1)
+    exchanged = lax.all_to_all(
+        split_value.astype(jnp.bfloat16), "surface", split_axis=3, concat_axis=3, tiled=True
+    )
+    summed_share = jnp.moveaxis(jnp.sum(exchanged.astype(jnp.float32), axis=3), 0, -1)
     residual_share = observed[0].astype(jnp.float32) - summed_share
     misfit_share = jnp.moveaxis(residual_share.astype(jnp.bfloat16), -1, 0)
     spread = jnp.broadcast_to(misfit_share[:, :, :, None], misfit_share.shape[:3] + (channels,) + misfit_share.shape[3:])

time: 383 us -> 368 us (0.961)
  waiting for transfers between devices: 186 us -> 175 us
    all_to_all x1, waiting for transfers between devices: 25 us -> 13.5 us  [per_device(): lax.all_to_all(split_value.astype(jnp.bfloat16), 'surface', split_axis=3,...]
    reshape x1 -> x0, local copies, waits for them, and re-layouts: 8 us -> none  [per_device(): partial_value.reshape(f_dim, parts, shots, channels, recvs // channels)]
    convert_element_type x0 -> x1, local copies, waits for them, and re-layouts: none -> 6.8 us  [per_device(): split_value.astype(jnp.bfloat16)]
  transfers between devices with their start and end apart: 4 -> 4, of which waited for: 4 -> 4; matrix products, arithmetic and copies ran while one was open for 11% -> 12% of each run, Pallas kernels for 0% -> 0%
where the time goes in v2:
time: 368 us; the launch traced here: 367 us
  waiting for transfers between devices  175 us (48%)
  local copies, waits for them, and re-layouts  84.3 us (23%)
  other arithmetic  38.3 us (10%)
  matrix products  37.4 us (10%)
  starting transfers between devices  31.8 us (9%)
    all_to_all x1, waiting for transfers between devices, per_device(): lax.all_to_all(returning, 'target', split_axis=0, concat_axis=0, tiled=True)  93.5 us
    all_to_all x1, waiting for transfers between devices, per_device(): lax.all_to_all(outgoing, 'target', split_axis=0, concat_axis=0, tiled=True)  56.1 us
    unnamed x18, local copies, waits for them, and re-layouts  18.2 us
    transpose x1, local copies, waits for them, and re-layouts, per_device(): jnp.einsum('fcar,flkecr->lakef', misfit, backward, preferred_element_type...  15.8 us
    another operation x1, other arithmetic, per_device(): jnp.stack([jnp.stack([-data_real, -data_imag], 3), jnp.stack([data_imag,...  14.7 us
    all_to_all x1, waiting for transfers between devices, per_device(): lax.all_to_all(split_value.astype(jnp.bfloat16), 'surface', split_axis=3,...  13.5 us
    dot_general x1, matrix products, per_device(): jnp.einsum('flakc,flkcdr->fdar', spectra, forward, preferred_element_type...  12.9 us
    dot_general x1, matrix products, per_device(): jnp.einsum('fcar,flkecr->lakef', misfit, backward, preferred_element_type...  12.9 us
  transfers between devices with their start and end apart: 4, of which 4 were waited for; matrix products, arithmetic and copies ran while one was open for 12% of the time, Pallas kernels for 0%

profile of v2, /device:TPU:1, one launch (start us, length us, event | category | flops | bytes accessed | tf_op | source)
XLA Modules:
  0.0 367.1 jit_solution(15087396475922323830)
XLA Ops:
  0.6 0.7 fusion.48
  1.4 0.7 fusion.39
  2.1 1.2 copy.125
  3.3 2.7 gather_fusion
  6.0 4.4 %broadcast_select_fusion = bf16[32,32,4,512]{3,1,2,0:T(8,128)(2,1)} fusion(bf16[32,32,4,512]{3,1,2,0:T(8,128)(2,1)} %gather_fusion, pred[32]{0:T(512)(128)(4,1)S(1)} %get-tuple-element.17), kind=kLoop, calls=%fused_computation.21 | loop fusion | flops 2097152 | bytes 8388640 | tf_op jit(solution)/shard_map/jit(_where)/select_n | solution.py:45
  10.5 11.1 %all-to-all-start = ((bf16[32,32,4,512]{3,1,2,0:T(8,128)(2,1)}), bf16[32,32,4,512]{3,1,2,0:T(8,128)(2,1)}, u32[]{:S(2)}, u32[]{:S(2)}) async-start(bf16[32,32,4,512]{3,1,2,0:T(8,128)(2,1)} %broadcast_select_fusion), calls=%async_computation | async-start | bytes 8388608 | tf_op jit(solution)/shard_map/all_to_all | solution.py:46
  21.6 1.8 fusion.50
  23.4 0.0 copy-start.4
  23.4 6.5 %copy.117 = bf16[1,16,1,4,32,256]{4,1,3,5,2,0:T(8,128)(2,1)} copy(bf16[1,16,1,4,32,256]{5,4,3,2,1,0:T(8,128)(2,1)S(1)} %get-tuple-element.24) | data formatting | bytes 2097152
  29.9 6.5 %copy.118 = bf16[1,16,1,4,32,256]{4,1,3,5,2,0:T(8,128)(2,1)} copy(bf16[1,16,1,4,32,256]{5,4,3,2,1,0:T(8,128)(2,1)S(1)} %get-tuple-element.23) | data formatting | bytes 2097152
  36.4 0.0 copy-done.4
  36.4 0.2 dynamic-slice_reduce_fusion
  36.6 2.2 negate_convert_fusion
  38.8 0.0 copy-start
  38.8 0.0 copy-start.1
  38.8 6.6 %fusion.9 = (bf16[256,16,4,1,32]{4,1,2,3,0:T(8,128)(2,1)S(1)}, bf16[256,16,4,1,32]{4,1,2,3,0:T(8,128)(2,1)}) fusion(bf16[1,16,1,4,32,256]{4,1,3,5,2,0:T(8,128)(2,1)} %copy.117, bf16[1,16,1,4,32,256]{4,1,3,5,2,0:T(8,128)(2,1)} %copy.118), kind=kLoop, calls=%fused_computation.18 | loop fusion | flops 1048576 | bytes 4194304 | tf_op jit(solution)/shard_map/stack | solution.py:53
  45.4 0.0 copy-done
  45.4 0.0 copy-done.1
  45.4 14.7 %maximum_bitcast_fusion = (bf16[256,16,4,1,2,32]{5,1,2,4,0,3:T(8,128)(2,1)}, bf16[256,16,4,1,2,32]{5,1,2,4,0,3:T(8,128)(2,1)}, bf16[256,16,4,1,2,32]{5,1,2,3,4,0:T(8,128)(2,1)}, bf16[256,16,4,1,2,32]{5,1,2,3,4,0:T(8,128)(2,1)}) fusion(bf16[256,16,4,1,32]{4,1,2,3,0:T(8,128)(2,1)} %get-tuple-element.30, bf16[256,16,4,1,32]{4,1,2,3,0:T(8,128)(2,1)S(1)} %get-tuple-element.29, ...), kind=kLoop, calls=%fused_computation.12 | loop fusion | flops 4194304 | bytes 12582912 | tf_op jit(solution)/shard_map/stack | solution.py:52
  60.2 56.1 %all-to-all-done = bf16[32,32,4,512]{3,1,2,0:T(8,128)(2,1)} async-done(((bf16[32,32,4,512]{3,1,2,0:T(8,128)(2,1)}), bf16[32,32,4,512]{3,1,2,0:T(8,128)(2,1)}, u32[]{:S(2)}, u32[]{:S(2)}) %all-to-all-start) | async-done | bytes 4194336 | tf_op jit(solution)/shard_map/all_to_all | solution.py:46
  116.3 4.2 %gather_fusion.1 = bf16[16,32,4,512]{3,1,2,0:T(8,128)(2,1)} fusion(bf16[32,32,4,512]{3,1,2,0:T(8,128)(2,1)} %all-to-all-done, s32[1024]{0:T(1024)S(1)} %pad_clamp_fusion), kind=kCustom, calls=%fused_computation.1 | custom fusion | bytes 4194368 | tf_op jit(solution)/shard_map/gather | solution.py:56
  120.4 2.8 convert_bitcast_fusion
  123.3 12.0 %copy.107 = bf16[256,16,32,4,2,1]{2,1,3,4,5,0:T(8,128)(2,1)} copy(bf16[256,16,32,4,2,1]{0,2,3,1,4,5:T(8,128)(2,1)S(1)} %convert_bitcast_fusion) | data formatting | bytes 4194304 | tf_op jit(solution)/shard_map/convert_element_type | solution.py:57
  135.2 12.9 %bitcast_convert_fusion = bf16[256,2,32,32]{3,2,1,0:T(8,128)(2,1)} fusion(bf16[256,16,32,4,2,1]{2,1,3,4,5,0:T(8,128)(2,1)} %copy.107, bf16[256,16,4,1,2,32]{5,1,2,3,4,0:T(8,128)(2,1)} %get-tuple-element.22, bf16[256,16,4,1,2,32]{5,1,2,3,4,0:T(8,128)(2,1)} %get-tuple-element.21), kind=kOutput, calls=%fused_computation.16 | convolution fusion | flops 136839168 | bytes 7340032 | tf_op jit(solution)/shard_map/flakc,flkcdr->fdar/dot_general | solution.py:58
  148.1 0.0 copy-start.3
  148.1 6.8 %copy.95 = bf16[256,2,32,8,4]{0,2,4,1,3:T(8,128)(2,1)} copy(bf16[256,2,32,8,4]{2,4,3,1,0:T(4,128)(2,1)} %bitcast.103) | data formatting | bytes 2097152 | tf_op jit(solution)/shard_map/convert_element_type | solution.py:64
  154.9 6.4 %all-to-all-start.1 = ((bf16[256,2,32,8,4]{0,2,4,1,3:T(8,128)(2,1)}), bf16[256,2,32,8,4]{0,2,4,1,3:T(8,128)(2,1)S(1)}, u32[]{:S(2)}, u32[]{:S(2)}) async-start(bf16[256,2,32,8,4]{0,2,4,1,3:T(8,128)(2,1)} %copy.95), calls=%async_computation.1 | async-start | bytes 2097152 | tf_op jit(solution)/shard_map/all_to_all | solution.py:63
  161.3 0.0 copy-done.3
  161.3 0.3 copy.91
  161.6 13.5 %all-to-all-done.1 = bf16[256,2,32,8,4]{0,2,4,1,3:T(8,128)(2,1)S(1)} async-done(((bf16[256,2,32,8,4]{0,2,4,1,3:T(8,128)(2,1)}), bf16[256,2,32,8,4]{0,2,4,1,3:T(8,128)(2,1)S(1)}, u32[]{:S(2)}, u32[]{:S(2)}) %all-to-all-start.1) | async-done | bytes 1048608 | tf_op jit(solution)/shard_map/all_to_all | solution.py:63
  175.2 0.2 convert_reduce_fusion
  175.3 0.5 copy.116
  175.8 0.4 fusion.19
  176.2 0.3 copy.97
  176.5 1.1 broadcast_in_dim.56
  177.6 6.3 %all-to-all-start.2 = ((bf16[256,2,32,8,4]{0,2,4,1,3:T(8,128)(2,1)}), bf16[256,2,32,8,4]{0,2,4,1,3:T(8,128)(2,1)S(1)}, u32[]{:S(2)}, u32[]{:S(2)}) async-start(bf16[256,2,32,8,4]{0,2,4,1,3:T(8,128)(2,1)} %broadcast_in_dim.56), calls=%async_computation.2 | async-start | bytes 2097152 | tf_op jit(solution)/shard_map/all_to_all | solution.py:70
  183.9 2.9 sine_negate_fusion
  186.8 11.5 %all-to-all-done.2 = bf16[256,2,32,8,4]{0,2,4,1,3:T(8,128)(2,1)S(1)} async-done(((bf16[256,2,32,8,4]{0,2,4,1,3:T(8,128)(2,1)}), bf16[256,2,32,8,4]{0,2,4,1,3:T(8,128)(2,1)S(1)}, u32[]{:S(2)}, u32[]{:S(2)}) %all-to-all-start.2) | async-done | bytes 1048608 | tf_op jit(solution)/shard_map/all_to_all | solution.py:70
  198.3 0.1 copy.98
  198.4 7.0 %copy.109 = bf16[256,2,32,32,1,1]{3,2,1,5,4,0:T(8,128)(2,1)} copy(bf16[256,2,32,32,1,1]{0,2,3,1,5,4:T(8,128)(2,1)S(1)} %bitcast.104) | data formatting | bytes 2097152 | tf_op jit(solution)/shard_map/reshape | solution.py:71
  205.3 12.9 %fusion.6 = f32[16,32,4,2,256]{1,0,3,2,4:T(8,128)} fusion(bf16[256,2,32,32,1,1]{3,2,1,5,4,0:T(8,128)(2,1)} %copy.109, bf16[256,16,4,1,2,32]{5,1,2,4,0,3:T(8,128)(2,1)} %get-tuple-element.20, bf16[256,16,4,1,2,32]{5,1,2,4,0,3:T(8,128)(2,1)} %get-tuple-element.19), kind=kOutput, calls=%fused_computation.11 | convolution fusion | flops 136314880 | bytes 9437184 | tf_op jit(solution)/shard_map/fcar,flkecr->lakef/dot_general | solution.py:72
  218.2 15.8 %copy.101 = f32[16,32,4,2,256]{4,3,1,2,0:T(2,128)} copy(f32[16,32,4,2,256]{1,0,3,2,4:T(8,128)} %fusion.6) | data formatting | bytes 8388608 | tf_op jit(solution)/shard_map/fcar,flkecr->lakef/transpose | solution.py:72
  234.0 6.4 %reshape.188 = f32[16,32,4,512]{3,1,2,0:T(8,128)} reshape(f32[16,32,4,2,256]{4,3,1,2,0:T(2,128)} %copy.101) | data formatting | bytes 8388608 | tf_op jit(solution)/shard_map/reshape | solution.py:75
  240.4 8.8 %convolution_convert_fusion = bf16[16,32,4,512]{3,1,2,0:T(8,128)(2,1)S(1)} fusion(f32[16,32,4,512]{3,1,2,0:T(8,128)} %reshape.188, f32[512,256]{1,0:T(8,128)} %get-tuple-element.31, f32[512,256]{1,0:T(8,128)} %get-tuple-element.32), kind=kOutput, calls=%fused_computation.26 | convolution fusion | flops 6443761664 | bytes 7340032 | tf_op jit(solution)/shard_map/dot_general | solution.py:76
  249.2 2.5 broadcast_in_dim.54
  251.7 5.3 %scatter_fusion = bf16[32,32,4,512]{3,1,2,0:T(8,128)(2,1)} fusion(bf16[32,32,4,512]{3,1,2,0:T(8,128)(2,1)} %broadcast_in_dim.54, s32[16]{0:T(128)S(1)} %fusion.42, bf16[16,32,4,512]{3,1,2,0:T(8,128)(2,1)S(1)} %convolution_convert_fusion), kind=kCustom, calls=%fused_computation.2 | custom fusion | bytes 6291520 | tf_op jit(solution)/shard_map/scatter | solution.py:78
  257.0 8.0 %all-to-all-start.3 = ((bf16[32,32,4,512]{3,1,2,0:T(8,128)(2,1)}), bf16[32,32,4,512]{3,1,2,0:T(8,128)(2,1)}, u32[]{:S(2)}, u32[]{:S(2)}) async-start(bf16[32,32,4,512]{3,1,2,0:T(8,128)(2,1)} %scatter_fusion), calls=%async_computation.3 | async-start | bytes 8388608 | tf_op jit(solution)/shard_map/all_to_all | solution.py:79
  265.1 1.2 copy.105
  266.2 93.5 %all-to-all-done.3 = bf16[32,32,4,512]{3,1,2,0:T(8,128)(2,1)} async-done(((bf16[32,32,4,512]{3,1,2,0:T(8,128)(2,1)}), bf16[32,32,4,512]{3,1,2,0:T(8,128)(2,1)}, u32[]{:S(2)}, u32[]{:S(2)}) %all-to-all-start.3) | async-done | bytes 4194336 | tf_op jit(solution)/shard_map/all_to_all | solution.py:79
  359.7 3.4 convert_element_type.72
  363.1 0.0 copy-start.2
  363.1 1.7 select_reduce_fusion
  364.9 0.0 copy-done.2
  364.9 0.2 fusion.47
  365.1 1.1 copy.103
  366.2 0.9 copy.104
  (5 shorter events, 0.0 us)
Async XLA Ops:
  10.5 105.8 %all-to-all-start = ((bf16[32,32,4,512]{3,1,2,0:T(8,128)(2,1)}), bf16[32,32,4,512]{3,1,2,0:T(8,128)(2,1)}, u32[]{:S(2)}, u32[]{:S(2)}) async-start(bf16[32,32,4,512]{3,1,2,0:T(8,128)(2,1)} %broadcast_select_fusion), calls=%async_computation | async-start | bytes 8388608 | tf_op jit(solution)/shard_map/all_to_all | solution.py:46
  23.4 13.0 %copy-start.4 = (s32[32,16]{0,1:T(8,128)S(1)}, s32[32,16]{0,1:T(8,128)}, u32[]{:S(2)}) copy-start(s32[32,16]{0,1:T(8,128)} %param.7) | copy-start | bytes 6148
  38.8 6.7 %copy-start = (bf16[1,16,1,4,32,256]{4,1,3,5,2,0:T(8,128)(2,1)S(1)}, bf16[1,16,1,4,32,256]{4,1,3,5,2,0:T(8,128)(2,1)}, u32[]{:S(2)}) copy-start(bf16[1,16,1,4,32,256]{4,1,3,5,2,0:T(8,128)(2,1)} %copy.117) | copy-start | bytes 3145732
  38.8 6.7 %copy-start.1 = (bf16[1,16,1,4,32,256]{4,1,3,5,2,0:T(8,128)(2,1)S(1)}, bf16[1,16,1,4,32,256]{4,1,3,5,2,0:T(8,128)(2,1)}, u32[]{:S(2)}) copy-start(bf16[1,16,1,4,32,256]{4,1,3,5,2,0:T(8,128)(2,1)} %copy.118) | copy-start | bytes 3145732
  148.1 13.2 %copy-start.3 = (bf16[1,2,32,4,256]{4,3,2,1,0:T(4,128)(2,1)S(1)}, bf16[1,2,32,4,256]{4,3,2,1,0:T(4,128)(2,1)}, u32[]{:S(2)}) copy-start(bf16[1,2,32,4,256]{4,3,2,1,0:T(4,128)(2,1)} %param.6) | copy-start | bytes 393220
  154.9 20.2 %all-to-all-start.1 = ((bf16[256,2,32,8,4]{0,2,4,1,3:T(8,128)(2,1)}), bf16[256,2,32,8,4]{0,2,4,1,3:T(8,128)(2,1)S(1)}, u32[]{:S(2)}, u32[]{:S(2)}) async-start(bf16[256,2,32,8,4]{0,2,4,1,3:T(8,128)(2,1)} %copy.95), calls=%async_computation.1 | async-start | bytes 2097152 | tf_op jit(solution)/shard_map/all_to_all | solution.py:63
  177.6 20.6 %all-to-all-start.2 = ((bf16[256,2,32,8,4]{0,2,4,1,3:T(8,128)(2,1)}), bf16[256,2,32,8,4]{0,2,4,1,3:T(8,128)(2,1)S(1)}, u32[]{:S(2)}, u32[]{:S(2)}) async-start(bf16[256,2,32,8,4]{0,2,4,1,3:T(8,128)(2,1)} %broadcast_in_dim.56), calls=%async_computation.2 | async-start | bytes 2097152 | tf_op jit(solution)/shard_map/all_to_all | solution.py:70
  257.0 102.7 %all-to-all-start.3 = ((bf16[32,32,4,512]{3,1,2,0:T(8,128)(2,1)}), bf16[32,32,4,512]{3,1,2,0:T(8,128)(2,1)}, u32[]{:S(2)}, u32[]{:S(2)}) async-start(bf16[32,32,4,512]{3,1,2,0:T(8,128)(2,1)} %scatter_fusion), calls=%async_computation.3 | async-start | bytes 8388608 | tf_op jit(solution)/shard_map/all_to_all | solution.py:79
  363.1 1.8 copy-start.2

commit v3 on v0

--- a/solution.py
+++ b/solution.py
@@ -39,10 +39,8 @@
     present = jnp.any(wanted, axis=1)
     slot_for = jnp.sum(jnp.where(wanted, block_lists % owned, 0), axis=1)
     chosen = (slot_for[None, :] == jnp.arange(owned, dtype=jnp.int32)[:, None]) & present[None, :]
-    present_rows = present[:, None, None, None]
-    zero_half = jnp.zeros((), jnp.bfloat16)
     copy_now = response.astype(jnp.bfloat16)
-    outgoing = jnp.where(present_rows, copy_now[slot_for], zero_half)
+    outgoing = copy_now[slot_for]
     arrived = lax.all_to_all(outgoing, "target", split_axis=0, concat_axis=0, tiled=True)
     data_real = jnp.moveaxis(data_spectra[0, :, 0], -1, 0)
     data_imag = jnp.moveaxis(data_spectra[0, :, 1], -1, 0)
@@ -73,7 +71,9 @@
     grad_flat = grad_spectra.reshape(grad_spectra.shape[:3] + (samples,))
     grad_time = jnp.dot(grad_flat, dft_table.T, precision=lax.Precision.HIGHEST)
     grad_half = grad_time.astype(jnp.bfloat16)
-    returning = jnp.zeros((owners,) + grad_time.shape[1:], jnp.bfloat16).at[own_owner].set(grad_half)
+    match = own_owner[None, :] == jnp.arange(owners, dtype=jnp.int32)[:, None]
+    entry_for = jnp.argmax(match, axis=1)
+    returning = grad_half[entry_for]
     received = lax.all_to_all(returning, "target", split_axis=0, concat_axis=0, tiled=True)
     taken = jnp.where(
         chosen[:, :, None, None, None], received[None].astype(jnp.float32), jnp.zeros((), jnp.float32)

time: 383 us -> 378 us (0.987)
    gather x1 -> x2, local copies, waits for them, and re-layouts: 2.74 us -> 8.43 us  [the longest x1 5.64 us: per_device(): outgoing = copy_now[slot_for]]
    scatter x1 -> x0, local copies, waits for them, and re-layouts: 5.24 us -> none  [per_device(): jnp.zeros((owners,) + grad_time.shape[1:], jnp.bfloat16).at[own_owner]]
    select_n x3 -> x4, other arithmetic: 4.47 us -> 0.21 us  [the longest x1 0.19 us: per_device(): own_owner = own_ids // owned]
    unnamed x18 -> x17, local copies, waits for them, and re-layouts: 19 us -> 17.8 us
  transfers between devices with their start and end apart: 4 -> 4, of which waited for: 4 -> 4; matrix products, arithmetic and copies ran while one was open for 11% -> 12% of each run, Pallas kernels for 0% -> 0%
where the time goes in v3:
time: 378 us; the launch traced here: 376 us
  waiting for transfers between devices  185 us (49%)
  local copies, waits for them, and re-layouts  84.5 us (22%)
  matrix products  37.9 us (10%)
  other arithmetic  36.8 us (10%)
  starting transfers between devices  30.9 us (8%)
    all_to_all x1, waiting for transfers between devices, per_device(): lax.all_to_all(returning, 'target', split_axis=0, concat_axis=0, tiled=True)  93.5 us
    all_to_all x1, waiting for transfers between devices, per_device(): lax.all_to_all(outgoing, 'target', split_axis=0, concat_axis=0, tiled=True)  56.1 us
    all_to_all x1, waiting for transfers between devices, per_device(): lax.all_to_all(split_value, 'surface', split_axis=3, concat_axis=3, tiled...  25 us
    unnamed x17, local copies, waits for them, and re-layouts  17.8 us
    transpose x1, local copies, waits for them, and re-layouts, per_device(): jnp.einsum('fcar,flkecr->lakef', misfit, backward, preferred_element_type...  15.8 us
    another operation x1, other arithmetic, per_device(): jnp.stack([jnp.stack([-data_real, -data_imag], 3), jnp.stack([data_imag,...  14.8 us
    dot_general x1, matrix products, per_device(): jnp.einsum('flakc,flkcdr->fdar', spectra, forward, preferred_element_type...  13.4 us
    dot_general x1, matrix products, per_device(): jnp.einsum('fcar,flkecr->lakef', misfit, backward, preferred_element_type...  12.9 us
  transfers between devices with their start and end apart: 4, of which 4 were waited for; matrix products, arithmetic and copies ran while one was open for 12% of the time, Pallas kernels for 0%

profile of v3, /device:TPU:1, one launch (start us, length us, event | category | flops | bytes accessed | tf_op | source)
XLA Modules:
  0.0 376.3 jit_solution(11236835119518214674)
XLA Ops:
  0.6 0.7 fusion.50
  1.4 0.7 fusion.38
  2.1 1.1 convert_element_type.50
  3.2 5.6 %gather_fusion = bf16[32,32,4,512]{3,2,1,0:T(4,128)(2,1)} fusion(bf16[2,32,4,512]{3,2,1,0:T(4,128)(2,1)S(1)} %convert_element_type.50, s32[1024]{0:T(1024)S(1)} %pad_clamp_fusion.2), kind=kCustom, calls=%fused_computation | custom fusion | bytes 8388736 | tf_op jit(solution)/shard_map/gather | solution.py:43
  8.9 11.1 %all-to-all-start = ((bf16[32,32,4,512]{3,2,1,0:T(4,128)(2,1)}), bf16[32,32,4,512]{3,2,1,0:T(4,128)(2,1)}, u32[]{:S(2)}, u32[]{:S(2)}) async-start(bf16[32,32,4,512]{3,2,1,0:T(4,128)(2,1)} %gather_fusion), calls=%async_computation | async-start | bytes 8388608 | tf_op jit(solution)/shard_map/all_to_all | solution.py:44
  20.0 1.8 fusion.52
  21.7 0.0 copy-start.4
  21.8 6.5 %copy.116 = bf16[1,16,1,4,32,256]{4,1,3,5,2,0:T(8,128)(2,1)} copy(bf16[1,16,1,4,32,256]{5,4,3,2,1,0:T(8,128)(2,1)S(1)} %get-tuple-element.28) | data formatting | bytes 2097152
  28.3 6.5 %copy.117 = bf16[1,16,1,4,32,256]{4,1,3,5,2,0:T(8,128)(2,1)} copy(bf16[1,16,1,4,32,256]{5,4,3,2,1,0:T(8,128)(2,1)S(1)} %get-tuple-element.27) | data formatting | bytes 2097152
  34.8 0.0 copy-done.4
  34.8 0.2 fusion.40
  35.0 2.2 negate_convert_fusion
  37.2 0.0 copy-start
  37.2 0.0 copy-start.1
  37.2 6.6 %fusion.9 = (bf16[256,16,4,1,32]{4,1,2,3,0:T(8,128)(2,1)S(1)}, bf16[256,16,4,1,32]{4,1,2,3,0:T(8,128)(2,1)}) fusion(bf16[1,16,1,4,32,256]{4,1,3,5,2,0:T(8,128)(2,1)} %copy.116, bf16[1,16,1,4,32,256]{4,1,3,5,2,0:T(8,128)(2,1)} %copy.117), kind=kLoop, calls=%fused_computation.17 | loop fusion | flops 1048576 | bytes 4194304 | tf_op jit(solution)/shard_map/stack | solution.py:51
  43.8 0.0 copy-done
  43.8 0.0 copy-done.1
  43.8 14.8 %maximum_bitcast_fusion = (bf16[256,16,4,1,2,32]{5,1,2,4,0,3:T(8,128)(2,1)}, bf16[256,16,4,1,2,32]{5,1,2,4,0,3:T(8,128)(2,1)}, bf16[256,16,4,1,2,32]{5,1,2,3,4,0:T(8,128)(2,1)}, bf16[256,16,4,1,2,32]{5,1,2,3,4,0:T(8,128)(2,1)}) fusion(bf16[256,16,4,1,32]{4,1,2,3,0:T(8,128)(2,1)} %get-tuple-element.34, bf16[256,16,4,1,32]{4,1,2,3,0:T(8,128)(2,1)S(1)} %get-tuple-element.33, ...), kind=kLoop, calls=%fused_computation.12 | loop fusion | flops 4194304 | bytes 12582912 | tf_op jit(solution)/shard_map/stack | solution.py:50
  58.6 56.1 %all-to-all-done = bf16[32,32,4,512]{3,2,1,0:T(4,128)(2,1)} async-done(((bf16[32,32,4,512]{3,2,1,0:T(4,128)(2,1)}), bf16[32,32,4,512]{3,2,1,0:T(4,128)(2,1)}, u32[]{:S(2)}, u32[]{:S(2)}) %all-to-all-start) | async-done | bytes 4194336 | tf_op jit(solution)/shard_map/all_to_all | solution.py:44
  114.6 5.7 %gather_fusion.1 = bf16[16,32,4,512]{3,2,1,0:T(4,128)(2,1)} fusion(bf16[32,32,4,512]{3,2,1,0:T(4,128)(2,1)} %all-to-all-done, s32[1024]{0:T(1024)S(1)} %pad_clamp_fusion.1), kind=kCustom, calls=%fused_computation.1 | custom fusion | bytes 4194368 | tf_op jit(solution)/shard_map/gather | solution.py:54
  120.3 2.8 convert_bitcast_fusion
  123.2 12.0 %copy.106 = bf16[256,16,32,4,2,1]{2,1,3,4,5,0:T(8,128)(2,1)} copy(bf16[256,16,32,4,2,1]{0,2,3,1,4,5:T(8,128)(2,1)S(1)} %convert_bitcast_fusion) | data formatting | bytes 4194304 | tf_op jit(solution)/shard_map/convert_element_type | solution.py:55
  135.2 13.4 %fusion = f32[256,2,32,32,1,1]{3,2,5,4,1,0:T(8,128)} fusion(bf16[256,16,32,4,2,1]{2,1,3,4,5,0:T(8,128)(2,1)} %copy.106, bf16[256,16,4,1,2,32]{5,1,2,3,4,0:T(8,128)(2,1)} %get-tuple-element.26, bf16[256,16,4,1,2,32]{5,1,2,3,4,0:T(8,128)(2,1)} %get-tuple-element.25), kind=kOutput, calls=%fused_computation.4 | convolution fusion | flops 136314880 | bytes 8388608 | tf_op jit(solution)/shard_map/flakc,flkcdr->fdar/dot_general | solution.py:56
  148.6 8.0 %copy.94 = f32[256,2,32,8,4]{0,2,4,1,3:T(8,128)} copy(f32[256,2,32,8,4]{2,4,3,1,0:T(4,128)} %bitcast.103) | data formatting | bytes 4194304 | tf_op jit(solution)/shard_map/reshape | solution.py:60
  156.6 0.0 copy-start.3
  156.6 6.5 %all-to-all-start.1 = ((f32[256,2,32,8,4]{0,2,4,1,3:T(8,128)}), f32[256,2,32,8,4]{0,2,4,1,3:T(8,128)S(1)}, u32[]{:S(2)}, u32[]{:S(2)}) async-start(f32[256,2,32,8,4]{0,2,4,1,3:T(8,128)} %copy.94), calls=%async_computation.1 | async-start | bytes 4194304 | tf_op jit(solution)/shard_map/all_to_all | solution.py:61
  163.1 0.0 copy-done.3
  163.1 1.1 copy.90
  164.2 25.0 %all-to-all-done.1 = f32[256,2,32,8,4]{0,2,4,1,3:T(8,128)S(1)} async-done(((f32[256,2,32,8,4]{0,2,4,1,3:T(8,128)}), f32[256,2,32,8,4]{0,2,4,1,3:T(8,128)S(1)}, u32[]{:S(2)}, u32[]{:S(2)}) %all-to-all-start.1) | async-done | bytes 2097184 | tf_op jit(solution)/shard_map/all_to_all | solution.py:61
  189.2 0.2 reduce_sum.31
  189.4 0.5 copy.115
  189.9 1.4 fusion.18
  191.3 0.3 copy.96
  191.6 1.1 broadcast_in_dim.22
  192.7 5.2 %all-to-all-start.2 = ((bf16[256,2,32,8,4]{0,2,4,1,3:T(8,128)(2,1)}), bf16[256,2,32,8,4]{0,2,4,1,3:T(8,128)(2,1)S(1)}, u32[]{:S(2)}, u32[]{:S(2)}) async-start(bf16[256,2,32,8,4]{0,2,4,1,3:T(8,128)(2,1)} %broadcast_in_dim.22), calls=%async_computation.2 | async-start | bytes 2097152 | tf_op jit(solution)/shard_map/all_to_all | solution.py:66
  198.0 0.6 iota_reduce_fusion
  198.6 2.9 sine_negate_fusion
  201.5 10.9 %all-to-all-done.2 = bf16[256,2,32,8,4]{0,2,4,1,3:T(8,128)(2,1)S(1)} async-done(((bf16[256,2,32,8,4]{0,2,4,1,3:T(8,128)(2,1)}), bf16[256,2,32,8,4]{0,2,4,1,3:T(8,128)(2,1)S(1)}, u32[]{:S(2)}, u32[]{:S(2)}) %all-to-all-start.2) | async-done | bytes 1048608 | tf_op jit(solution)/shard_map/all_to_all | solution.py:66
  212.3 0.1 copy.97
  212.4 7.0 %copy.108 = bf16[256,2,32,32,1,1]{3,2,1,5,4,0:T(8,128)(2,1)} copy(bf16[256,2,32,32,1,1]{0,2,3,1,5,4:T(8,128)(2,1)S(1)} %bitcast.104) | data formatting | bytes 2097152 | tf_op jit(solution)/shard_map/reshape | solution.py:67
  219.4 12.9 %fusion.6 = f32[16,32,4,2,256]{1,0,3,2,4:T(8,128)} fusion(bf16[256,2,32,32,1,1]{3,2,1,5,4,0:T(8,128)(2,1)} %copy.108, bf16[256,16,4,1,2,32]{5,1,2,4,0,3:T(8,128)(2,1)} %get-tuple-element.24, bf16[256,16,4,1,2,32]{5,1,2,4,0,3:T(8,128)(2,1)} %get-tuple-element.23), kind=kOutput, calls=%fused_computation.11 | convolution fusion | flops 136314880 | bytes 9437184 | tf_op jit(solution)/shard_map/fcar,flkecr->lakef/dot_general | solution.py:68
  232.3 15.8 %copy.100 = f32[16,32,4,2,256]{4,3,1,2,0:T(2,128)} copy(f32[16,32,4,2,256]{1,0,3,2,4:T(8,128)} %fusion.6) | data formatting | bytes 8388608 | tf_op jit(solution)/shard_map/fcar,flkecr->lakef/transpose | solution.py:68
  248.1 6.4 %reshape.189 = f32[16,32,4,512]{3,1,2,0:T(8,128)} reshape(f32[16,32,4,2,256]{4,3,1,2,0:T(2,128)} %copy.100) | data formatting | bytes 8388608 | tf_op jit(solution)/shard_map/reshape | solution.py:71
  254.5 8.8 %convolution_convert_fusion = bf16[16,32,4,512]{3,1,2,0:T(8,128)(2,1)S(1)} fusion(f32[16,32,4,512]{3,1,2,0:T(8,128)} %reshape.189, f32[512,256]{1,0:T(8,128)} %get-tuple-element.35, f32[512,256]{1,0:T(8,128)} %get-tuple-element.36), kind=kOutput, calls=%fused_computation.24 | convolution fusion | flops 6443761664 | bytes 7340032 | tf_op jit(solution)/shard_map/dot_general | solution.py:72
  263.3 2.8 gather_fusion.2
  266.1 8.1 %all-to-all-start.3 = ((bf16[32,32,4,512]{3,1,2,0:T(8,128)(2,1)}), bf16[32,32,4,512]{3,1,2,0:T(8,128)(2,1)}, u32[]{:S(2)}, u32[]{:S(2)}) async-start(bf16[32,32,4,512]{3,1,2,0:T(8,128)(2,1)} %gather_fusion.2), calls=%async_computation.3 | async-start | bytes 8388608 | tf_op jit(solution)/shard_map/all_to_all | solution.py:77
  274.2 1.2 copy.104
  275.4 93.5 %all-to-all-done.3 = bf16[32,32,4,512]{3,1,2,0:T(8,128)(2,1)} async-done(((bf16[32,32,4,512]{3,1,2,0:T(8,128)(2,1)}), bf16[32,32,4,512]{3,1,2,0:T(8,128)(2,1)}, u32[]{:S(2)}, u32[]{:S(2)}) %all-to-all-start.3) | async-done | bytes 4194336 | tf_op jit(solution)/shard_map/all_to_all | solution.py:77
  368.9 3.4 convert_element_type.56
  372.3 0.0 copy-start.2
  372.3 1.7 select_reduce_fusion
  374.0 0.0 copy-done.2
  374.0 0.2 fusion.49
  374.3 1.1 copy.102
  375.4 0.9 copy.103
  (7 shorter events, 0.1 us)
Async XLA Ops:
  8.9 105.7 %all-to-all-start = ((bf16[32,32,4,512]{3,2,1,0:T(4,128)(2,1)}), bf16[32,32,4,512]{3,2,1,0:T(4,128)(2,1)}, u32[]{:S(2)}, u32[]{:S(2)}) async-start(bf16[32,32,4,512]{3,2,1,0:T(4,128)(2,1)} %gather_fusion), calls=%async_computation | async-start | bytes 8388608 | tf_op jit(solution)/shard_map/all_to_all | solution.py:44
  21.7 13.0 %copy-start.4 = (s32[32,16]{0,1:T(8,128)S(1)}, s32[32,16]{0,1:T(8,128)}, u32[]{:S(2)}) copy-start(s32[32,16]{0,1:T(8,128)} %param.7) | copy-start | bytes 6148
  37.2 6.6 %copy-start = (bf16[1,16,1,4,32,256]{4,1,3,5,2,0:T(8,128)(2,1)S(1)}, bf16[1,16,1,4,32,256]{4,1,3,5,2,0:T(8,128)(2,1)}, u32[]{:S(2)}) copy-start(bf16[1,16,1,4,32,256]{4,1,3,5,2,0:T(8,128)(2,1)} %copy.116) | copy-start | bytes 3145732
  37.2 6.6 %copy-start.1 = (bf16[1,16,1,4,32,256]{4,1,3,5,2,0:T(8,128)(2,1)S(1)}, bf16[1,16,1,4,32,256]{4,1,3,5,2,0:T(8,128)(2,1)}, u32[]{:S(2)}) copy-start(bf16[1,16,1,4,32,256]{4,1,3,5,2,0:T(8,128)(2,1)} %copy.117) | copy-start | bytes 3145732
  156.6 6.5 %copy-start.3 = (bf16[1,2,32,4,256]{4,3,2,1,0:T(4,128)(2,1)S(1)}, bf16[1,2,32,4,256]{4,3,2,1,0:T(4,128)(2,1)}, u32[]{:S(2)}) copy-start(bf16[1,2,32,4,256]{4,3,2,1,0:T(4,128)(2,1)} %param.6) | copy-start | bytes 393220
  156.6 32.6 %all-to-all-start.1 = ((f32[256,2,32,8,4]{0,2,4,1,3:T(8,128)}), f32[256,2,32,8,4]{0,2,4,1,3:T(8,128)S(1)}, u32[]{:S(2)}, u32[]{:S(2)}) async-start(f32[256,2,32,8,4]{0,2,4,1,3:T(8,128)} %copy.94), calls=%async_computation.1 | async-start | bytes 4194304 | tf_op jit(solution)/shard_map/all_to_all | solution.py:61
  192.7 19.6 %all-to-all-start.2 = ((bf16[256,2,32,8,4]{0,2,4,1,3:T(8,128)(2,1)}), bf16[256,2,32,8,4]{0,2,4,1,3:T(8,128)(2,1)S(1)}, u32[]{:S(2)}, u32[]{:S(2)}) async-start(bf16[256,2,32,8,4]{0,2,4,1,3:T(8,128)(2,1)} %broadcast_in_dim.22), calls=%async_computation.2 | async-start | bytes 2097152 | tf_op jit(solution)/shard_map/all_to_all | solution.py:66
  266.1 102.8 %all-to-all-start.3 = ((bf16[32,32,4,512]{3,1,2,0:T(8,128)(2,1)}), bf16[32,32,4,512]{3,1,2,0:T(8,128)(2,1)}, u32[]{:S(2)}, u32[]{:S(2)}) async-start(bf16[32,32,4,512]{3,1,2,0:T(8,128)(2,1)} %gather_fusion.2), calls=%async_computation.3 | async-start | bytes 8388608 | tf_op jit(solution)/shard_map/all_to_all | solution.py:77
  372.3 1.8 copy-start.2

commit v4 on v3

--- a/solution.py
+++ b/solution.py
@@ -69,7 +69,7 @@
         "fcar,flkecr->lakef", misfit, backward, preferred_element_type=jnp.float32
     )
     grad_flat = grad_spectra.reshape(grad_spectra.shape[:3] + (samples,))
-    grad_time = jnp.dot(grad_flat, dft_table.T, precision=lax.Precision.HIGHEST)
+    grad_time = jnp.dot(grad_flat, dft_table.T, precision=lax.Precision.HIGH)
     grad_half = grad_time.astype(jnp.bfloat16)
     match = own_owner[None, :] == jnp.arange(owners, dtype=jnp.int32)[:, None]
     entry_for = jnp.argmax(match, axis=1)

time: 378 us -> 375 us (level)
  no operation moved by 1% of the time
where the time goes in v4:
time: 375 us; the launch traced here: 373 us
  waiting for transfers between devices  185 us (49%)
  local copies, waits for them, and re-layouts  84.5 us (23%)
  other arithmetic  36.8 us (10%)
  matrix products  35.1 us (9%)
  starting transfers between devices  30.9 us (8%)
    all_to_all x1, waiting for transfers between devices, per_device(): lax.all_to_all(returning, 'target', split_axis=0, concat_axis=0, tiled=True)  93.5 us
    all_to_all x1, waiting for transfers between devices, per_device(): lax.all_to_all(outgoing, 'target', split_axis=0, concat_axis=0, tiled=True)  56.1 us
    all_to_all x1, waiting for transfers between devices, per_device(): lax.all_to_all(split_value, 'surface', split_axis=3, concat_axis=3, tiled...  25 us
    unnamed x17, local copies, waits for them, and re-layouts  17.8 us
    transpose x1, local copies, waits for them, and re-layouts, per_device(): jnp.einsum('fcar,flkecr->lakef', misfit, backward, preferred_element_type...  15.8 us
    another operation x1, other arithmetic, per_device(): jnp.stack([jnp.stack([-data_real, -data_imag], 3), jnp.stack([data_imag,...  14.8 us
    dot_general x1, matrix products, per_device(): jnp.einsum('flakc,flkcdr->fdar', spectra, forward, preferred_element_type...  13.4 us
    dot_general x1, matrix products, per_device(): jnp.einsum('fcar,flkecr->lakef', misfit, backward, preferred_element_type...  12.9 us
  transfers between devices with their start and end apart: 4, of which 4 were waited for; matrix products, arithmetic and copies ran while one was open for 12% of the time, Pallas kernels for 0%

profile of v4, /device:TPU:1, one launch (start us, length us, event | category | flops | bytes accessed | tf_op | source)
XLA Modules:
  0.0 373.5 jit_solution(12444704143070929495)
XLA Ops:
  0.6 0.7 fusion.50
  1.4 0.7 fusion.38
  2.1 1.1 convert_element_type.50
  3.2 5.7 %gather_fusion = bf16[32,32,4,512]{3,2,1,0:T(4,128)(2,1)} fusion(bf16[2,32,4,512]{3,2,1,0:T(4,128)(2,1)S(1)} %convert_element_type.50, s32[1024]{0:T(1024)S(1)} %pad_clamp_fusion.2), kind=kCustom, calls=%fused_computation | custom fusion | bytes 8388736 | tf_op jit(solution)/shard_map/gather | solution.py:43
  8.9 11.2 %all-to-all-start = ((bf16[32,32,4,512]{3,2,1,0:T(4,128)(2,1)}), bf16[32,32,4,512]{3,2,1,0:T(4,128)(2,1)}, u32[]{:S(2)}, u32[]{:S(2)}) async-start(bf16[32,32,4,512]{3,2,1,0:T(4,128)(2,1)} %gather_fusion), calls=%async_computation | async-start | bytes 8388608 | tf_op jit(solution)/shard_map/all_to_all | solution.py:44
  20.1 1.8 fusion.52
  21.8 0.0 copy-start.4
  21.8 6.5 %copy.116 = bf16[1,16,1,4,32,256]{4,1,3,5,2,0:T(8,128)(2,1)} copy(bf16[1,16,1,4,32,256]{5,4,3,2,1,0:T(8,128)(2,1)S(1)} %get-tuple-element.28) | data formatting | bytes 2097152
  28.4 6.5 %copy.117 = bf16[1,16,1,4,32,256]{4,1,3,5,2,0:T(8,128)(2,1)} copy(bf16[1,16,1,4,32,256]{5,4,3,2,1,0:T(8,128)(2,1)S(1)} %get-tuple-element.27) | data formatting | bytes 2097152
  34.8 0.0 copy-done.4
  34.8 0.2 fusion.40
  35.1 2.2 negate_convert_fusion
  37.3 0.0 copy-start
  37.3 0.0 copy-start.1
  37.3 6.6 %fusion.9 = (bf16[256,16,4,1,32]{4,1,2,3,0:T(8,128)(2,1)S(1)}, bf16[256,16,4,1,32]{4,1,2,3,0:T(8,128)(2,1)}) fusion(bf16[1,16,1,4,32,256]{4,1,3,5,2,0:T(8,128)(2,1)} %copy.116, bf16[1,16,1,4,32,256]{4,1,3,5,2,0:T(8,128)(2,1)} %copy.117), kind=kLoop, calls=%fused_computation.17 | loop fusion | flops 1048576 | bytes 4194304 | tf_op jit(solution)/shard_map/stack | solution.py:51
  43.9 0.0 copy-done
  43.9 0.0 copy-done.1
  43.9 14.8 %maximum_bitcast_fusion = (bf16[256,16,4,1,2,32]{5,1,2,4,0,3:T(8,128)(2,1)}, bf16[256,16,4,1,2,32]{5,1,2,4,0,3:T(8,128)(2,1)}, bf16[256,16,4,1,2,32]{5,1,2,3,4,0:T(8,128)(2,1)}, bf16[256,16,4,1,2,32]{5,1,2,3,4,0:T(8,128)(2,1)}) fusion(bf16[256,16,4,1,32]{4,1,2,3,0:T(8,128)(2,1)} %get-tuple-element.34, bf16[256,16,4,1,32]{4,1,2,3,0:T(8,128)(2,1)S(1)} %get-tuple-element.33, ...), kind=kLoop, calls=%fused_computation.12 | loop fusion | flops 4194304 | bytes 12582912 | tf_op jit(solution)/shard_map/stack | solution.py:50
  58.6 56.1 %all-to-all-done = bf16[32,32,4,512]{3,2,1,0:T(4,128)(2,1)} async-done(((bf16[32,32,4,512]{3,2,1,0:T(4,128)(2,1)}), bf16[32,32,4,512]{3,2,1,0:T(4,128)(2,1)}, u32[]{:S(2)}, u32[]{:S(2)}) %all-to-all-start) | async-done | bytes 4194336 | tf_op jit(solution)/shard_map/all_to_all | solution.py:44
  114.7 5.7 %gather_fusion.1 = bf16[16,32,4,512]{3,2,1,0:T(4,128)(2,1)} fusion(bf16[32,32,4,512]{3,2,1,0:T(4,128)(2,1)} %all-to-all-done, s32[1024]{0:T(1024)S(1)} %pad_clamp_fusion.1), kind=kCustom, calls=%fused_computation.1 | custom fusion | bytes 4194368 | tf_op jit(solution)/shard_map/gather | solution.py:54
  120.4 2.8 convert_bitcast_fusion
  123.3 12.0 %copy.106 = bf16[256,16,32,4,2,1]{2,1,3,4,5,0:T(8,128)(2,1)} copy(bf16[256,16,32,4,2,1]{0,2,3,1,4,5:T(8,128)(2,1)S(1)} %convert_bitcast_fusion) | data formatting | bytes 4194304 | tf_op jit(solution)/shard_map/convert_element_type | solution.py:55
  135.3 13.4 %fusion = f32[256,2,32,32,1,1]{3,2,5,4,1,0:T(8,128)} fusion(bf16[256,16,32,4,2,1]{2,1,3,4,5,0:T(8,128)(2,1)} %copy.106, bf16[256,16,4,1,2,32]{5,1,2,3,4,0:T(8,128)(2,1)} %get-tuple-element.26, bf16[256,16,4,1,2,32]{5,1,2,3,4,0:T(8,128)(2,1)} %get-tuple-element.25), kind=kOutput, calls=%fused_computation.4 | convolution fusion | flops 136314880 | bytes 8388608 | tf_op jit(solution)/shard_map/flakc,flkcdr->fdar/dot_general | solution.py:56
  148.7 8.0 %copy.94 = f32[256,2,32,8,4]{0,2,4,1,3:T(8,128)} copy(f32[256,2,32,8,4]{2,4,3,1,0:T(4,128)} %bitcast.103) | data formatting | bytes 4194304 | tf_op jit(solution)/shard_map/reshape | solution.py:60
  156.7 0.0 copy-start.3
  156.7 6.5 %all-to-all-start.1 = ((f32[256,2,32,8,4]{0,2,4,1,3:T(8,128)}), f32[256,2,32,8,4]{0,2,4,1,3:T(8,128)S(1)}, u32[]{:S(2)}, u32[]{:S(2)}) async-start(f32[256,2,32,8,4]{0,2,4,1,3:T(8,128)} %copy.94), calls=%async_computation.1 | async-start | bytes 4194304 | tf_op jit(solution)/shard_map/all_to_all | solution.py:61
  163.2 0.0 copy-done.3
  163.2 1.1 copy.90
  164.3 25.0 %all-to-all-done.1 = f32[256,2,32,8,4]{0,2,4,1,3:T(8,128)S(1)} async-done(((f32[256,2,32,8,4]{0,2,4,1,3:T(8,128)}), f32[256,2,32,8,4]{0,2,4,1,3:T(8,128)S(1)}, u32[]{:S(2)}, u32[]{:S(2)}) %all-to-all-start.1) | async-done | bytes 2097184 | tf_op jit(solution)/shard_map/all_to_all | solution.py:61
  189.3 0.2 reduce_sum.31
  189.5 0.5 copy.115
  190.0 1.4 fusion.18
  191.4 0.3 copy.96
  191.7 1.1 broadcast_in_dim.22
  192.8 5.2 %all-to-all-start.2 = ((bf16[256,2,32,8,4]{0,2,4,1,3:T(8,128)(2,1)}), bf16[256,2,32,8,4]{0,2,4,1,3:T(8,128)(2,1)S(1)}, u32[]{:S(2)}, u32[]{:S(2)}) async-start(bf16[256,2,32,8,4]{0,2,4,1,3:T(8,128)(2,1)} %broadcast_in_dim.22), calls=%async_computation.2 | async-start | bytes 2097152 | tf_op jit(solution)/shard_map/all_to_all | solution.py:66
  198.0 0.6 iota_reduce_fusion
  198.7 2.9 sine_negate_fusion
  201.6 10.9 %all-to-all-done.2 = bf16[256,2,32,8,4]{0,2,4,1,3:T(8,128)(2,1)S(1)} async-done(((bf16[256,2,32,8,4]{0,2,4,1,3:T(8,128)(2,1)}), bf16[256,2,32,8,4]{0,2,4,1,3:T(8,128)(2,1)S(1)}, u32[]{:S(2)}, u32[]{:S(2)}) %all-to-all-start.2) | async-done | bytes 1048608 | tf_op jit(solution)/shard_map/all_to_all | solution.py:66
  212.4 0.1 copy.97
  212.5 7.0 %copy.108 = bf16[256,2,32,32,1,1]{3,2,1,5,4,0:T(8,128)(2,1)} copy(bf16[256,2,32,32,1,1]{0,2,3,1,5,4:T(8,128)(2,1)S(1)} %bitcast.104) | data formatting | bytes 2097152 | tf_op jit(solution)/shard_map/reshape | solution.py:67
  219.5 12.9 %fusion.6 = f32[16,32,4,2,256]{1,0,3,2,4:T(8,128)} fusion(bf16[256,2,32,32,1,1]{3,2,1,5,4,0:T(8,128)(2,1)} %copy.108, bf16[256,16,4,1,2,32]{5,1,2,4,0,3:T(8,128)(2,1)} %get-tuple-element.24, bf16[256,16,4,1,2,32]{5,1,2,4,0,3:T(8,128)(2,1)} %get-tuple-element.23), kind=kOutput, calls=%fused_computation.11 | convolution fusion | flops 136314880 | bytes 9437184 | tf_op jit(solution)/shard_map/fcar,flkecr->lakef/dot_general | solution.py:68
  232.4 15.8 %copy.100 = f32[16,32,4,2,256]{4,3,1,2,0:T(2,128)} copy(f32[16,32,4,2,256]{1,0,3,2,4:T(8,128)} %fusion.6) | data formatting | bytes 8388608 | tf_op jit(solution)/shard_map/fcar,flkecr->lakef/transpose | solution.py:68
  248.2 6.4 %reshape.189 = f32[16,32,4,512]{3,1,2,0:T(8,128)} reshape(f32[16,32,4,2,256]{4,3,1,2,0:T(2,128)} %copy.100) | data formatting | bytes 8388608 | tf_op jit(solution)/shard_map/reshape | solution.py:71
  254.6 5.9 %convolution_convert_fusion = bf16[16,32,4,512]{3,1,2,0:T(8,128)(2,1)S(1)} fusion(f32[16,32,4,512]{3,1,2,0:T(8,128)} %reshape.189, f32[512,256]{1,0:T(8,128)} %get-tuple-element.35, f32[512,256]{1,0:T(8,128)} %get-tuple-element.36), kind=kOutput, calls=%fused_computation.24 | convolution fusion | flops 3222536192 | bytes 7340032 | tf_op jit(solution)/shard_map/dot_general | solution.py:72
  260.6 2.8 gather_fusion.2
  263.3 8.1 %all-to-all-start.3 = ((bf16[32,32,4,512]{3,1,2,0:T(8,128)(2,1)}), bf16[32,32,4,512]{3,1,2,0:T(8,128)(2,1)}, u32[]{:S(2)}, u32[]{:S(2)}) async-start(bf16[32,32,4,512]{3,1,2,0:T(8,128)(2,1)} %gather_fusion.2), calls=%async_computation.3 | async-start | bytes 8388608 | tf_op jit(solution)/shard_map/all_to_all | solution.py:77
  271.4 1.2 copy.104
  272.6 93.5 %all-to-all-done.3 = bf16[32,32,4,512]{3,1,2,0:T(8,128)(2,1)} async-done(((bf16[32,32,4,512]{3,1,2,0:T(8,128)(2,1)}), bf16[32,32,4,512]{3,1,2,0:T(8,128)(2,1)}, u32[]{:S(2)}, u32[]{:S(2)}) %all-to-all-start.3) | async-done | bytes 4194336 | tf_op jit(solution)/shard_map/all_to_all | solution.py:77
  366.1 3.4 convert_element_type.56
  369.5 0.0 copy-start.2
  369.5 1.7 select_reduce_fusion
  371.2 0.0 copy-done.2
  371.2 0.2 fusion.49
  371.5 1.1 copy.102
  372.6 0.9 copy.103
  (7 shorter events, 0.1 us)
Async XLA Ops:
  8.9 105.8 %all-to-all-start = ((bf16[32,32,4,512]{3,2,1,0:T(4,128)(2,1)}), bf16[32,32,4,512]{3,2,1,0:T(4,128)(2,1)}, u32[]{:S(2)}, u32[]{:S(2)}) async-start(bf16[32,32,4,512]{3,2,1,0:T(4,128)(2,1)} %gather_fusion), calls=%async_computation | async-start | bytes 8388608 | tf_op jit(solution)/shard_map/all_to_all | solution.py:44
  21.8 13.0 %copy-start.4 = (s32[32,16]{0,1:T(8,128)S(1)}, s32[32,16]{0,1:T(8,128)}, u32[]{:S(2)}) copy-start(s32[32,16]{0,1:T(8,128)} %param.7) | copy-start | bytes 6148
  37.3 6.6 %copy-start = (bf16[1,16,1,4,32,256]{4,1,3,5,2,0:T(8,128)(2,1)S(1)}, bf16[1,16,1,4,32,256]{4,1,3,5,2,0:T(8,128)(2,1)}, u32[]{:S(2)}) copy-start(bf16[1,16,1,4,32,256]{4,1,3,5,2,0:T(8,128)(2,1)} %copy.116) | copy-start | bytes 3145732
  37.3 6.6 %copy-start.1 = (bf16[1,16,1,4,32,256]{4,1,3,5,2,0:T(8,128)(2,1)S(1)}, bf16[1,16,1,4,32,256]{4,1,3,5,2,0:T(8,128)(2,1)}, u32[]{:S(2)}) copy-start(bf16[1,16,1,4,32,256]{4,1,3,5,2,0:T(8,128)(2,1)} %copy.117) | copy-start | bytes 3145732
  156.7 6.5 %copy-start.3 = (bf16[1,2,32,4,256]{4,3,2,1,0:T(4,128)(2,1)S(1)}, bf16[1,2,32,4,256]{4,3,2,1,0:T(4,128)(2,1)}, u32[]{:S(2)}) copy-start(bf16[1,2,32,4,256]{4,3,2,1,0:T(4,128)(2,1)} %param.6) | copy-start | bytes 393220
  156.7 32.6 %all-to-all-start.1 = ((f32[256,2,32,8,4]{0,2,4,1,3:T(8,128)}), f32[256,2,32,8,4]{0,2,4,1,3:T(8,128)S(1)}, u32[]{:S(2)}, u32[]{:S(2)}) async-start(f32[256,2,32,8,4]{0,2,4,1,3:T(8,128)} %copy.94), calls=%async_computation.1 | async-start | bytes 4194304 | tf_op jit(solution)/shard_map/all_to_all | solution.py:61
  192.8 19.6 %all-to-all-start.2 = ((bf16[256,2,32,8,4]{0,2,4,1,3:T(8,128)(2,1)}), bf16[256,2,32,8,4]{0,2,4,1,3:T(8,128)(2,1)S(1)}, u32[]{:S(2)}, u32[]{:S(2)}) async-start(bf16[256,2,32,8,4]{0,2,4,1,3:T(8,128)(2,1)} %broadcast_in_dim.22), calls=%async_computation.2 | async-start | bytes 2097152 | tf_op jit(solution)/shard_map/all_to_all | solution.py:66
  263.3 102.7 %all-to-all-start.3 = ((bf16[32,32,4,512]{3,1,2,0:T(8,128)(2,1)}), bf16[32,32,4,512]{3,1,2,0:T(8,128)(2,1)}, u32[]{:S(2)}, u32[]{:S(2)}) async-start(bf16[32,32,4,512]{3,1,2,0:T(8,128)(2,1)} %gather_fusion.2), calls=%async_computation.3 | async-start | bytes 8388608 | tf_op jit(solution)/shard_map/all_to_all | solution.py:77
  369.5 1.8 copy-start.2

commit v5 on v4

--- a/solution.py
+++ b/solution.py
@@ -6,6 +6,7 @@
 from jax.sharding import PartitionSpec as P
 
 step_length = 0.5
+chunks = 2
 
 
 def make_table(samples):
@@ -65,21 +66,26 @@
     spread = jnp.broadcast_to(misfit_share[:, :, :, None], misfit_share.shape[:3] + (channels,) + misfit_share.shape[3:])
     gathered = lax.all_to_all(spread, "surface", split_axis=3, concat_axis=3, tiled=True)
     misfit = gathered.reshape(f_dim, parts, shots, recvs)
-    grad_spectra = jnp.einsum(
-        "fcar,flkecr->lakef", misfit, backward, preferred_element_type=jnp.float32
-    )
-    grad_flat = grad_spectra.reshape(grad_spectra.shape[:3] + (samples,))
-    grad_time = jnp.dot(grad_flat, dft_table.T, precision=lax.Precision.HIGH)
-    grad_half = grad_time.astype(jnp.bfloat16)
     match = own_owner[None, :] == jnp.arange(owners, dtype=jnp.int32)[:, None]
     entry_for = jnp.argmax(match, axis=1)
-    returning = grad_half[entry_for]
-    received = lax.all_to_all(returning, "target", split_axis=0, concat_axis=0, tiled=True)
-    taken = jnp.where(
-        chosen[:, :, None, None, None], received[None].astype(jnp.float32), jnp.zeros((), jnp.float32)
-    )
-    gradient = jnp.sum(taken, axis=1)
-    response_next = response - step_length * gradient
+    positions = response.shape[2]
+    width = positions // chunks
+    next_parts = []
+    for c in range(chunks):
+        lo, hi = c * width, (c + 1) * width
+        grad_spectra = jnp.einsum(
+            "fcar,flkecr->lakef", misfit, backward[:, :, lo:hi], preferred_element_type=jnp.float32
+        )
+        grad_flat = grad_spectra.reshape(grad_spectra.shape[:3] + (samples,))
+        grad_time = jnp.dot(grad_flat, dft_table.T, precision=lax.Precision.HIGH)
+        returning = grad_time.astype(jnp.bfloat16)[entry_for]
+        received = lax.all_to_all(returning, "target", split_axis=0, concat_axis=0, tiled=True)
+        taken = jnp.where(
+            chosen[:, :, None, None, None], received[None].astype(jnp.float32), jnp.zeros((), jnp.float32)
+        )
+        gradient = jnp.sum(taken, axis=1)
+        next_parts.append(response[:, :, lo:hi] - step_length * gradient)
+    response_next = next_parts[0] if chunks == 1 else jnp.concatenate(next_parts, axis=2)
     return (response_next, response_next.astype(jnp.bfloat16), residual_share[None])
 
 

time: 375 us -> 371 us (0.989)
  waiting for transfers between devices: 185 us -> 146 us
  other arithmetic: 36.8 us -> 47.6 us
  matrix products: 35.1 us -> 43.7 us
  starting transfers between devices: 30.9 us -> 37.7 us
  local copies, waits for them, and re-layouts: 84.5 us -> 91 us
    all_to_all x1 -> x2, waiting for transfers between devices: 93.5 us -> 64.8 us  [per_device(): lax.all_to_all(returning, 'target', split_axis=0, concat_axis=0, tiled=True)]
    another operation x1 -> x2, other arithmetic: 14.8 us -> 23.6 us  [per_device(): jnp.stack([jnp.stack([-data_real, -data_imag], 3), jnp.stack([data_imag,...]
    all_to_all x1, waiting for transfers between devices: 10.9 us -> 2.05 us  [per_device(): lax.all_to_all(spread, 'surface', split_axis=3, concat_axis=3, tiled=True)]
    dot_general x1 -> x2, matrix products: 12.9 us -> 20.2 us  [per_device(): jnp.einsum('fcar,flkecr->lakef', misfit, backward[:, :, lo:hi], preferred...]
    all_to_all x1 -> x2, starting transfers between devices: 8.08 us -> 13.9 us  [per_device(): lax.all_to_all(returning, 'target', split_axis=0, concat_axis=0, tiled=True)]
    all_to_all x1, waiting for transfers between devices: 25 us -> 20.5 us  [per_device(): lax.all_to_all(split_value, 'surface', split_axis=3, concat_axis=3, tiled...]
    unnamed x17 -> x25, local copies, waits for them, and re-layouts: 17.8 us -> 20.5 us
    transpose x1 -> x2, local copies, waits for them, and re-layouts: 15.8 us -> 16.1 us  [per_device(): jnp.einsum('fcar,flkecr->lakef', misfit, backward[:, :, lo:hi], preferred...]
  transfers between devices with their start and end apart: 4 -> 5, of which waited for: 4 -> 5; matrix products, arithmetic and copies ran while one was open for 12% -> 23% of each run, Pallas kernels for 0% -> 0%
where the time goes in v5:
time: 371 us; the launch traced here: 367 us
  waiting for transfers between devices  146 us (39%)
  local copies, waits for them, and re-layouts  91 us (25%)
  other arithmetic  47.6 us (13%)
  matrix products  43.7 us (12%)
  starting transfers between devices  37.7 us (10%)
    all_to_all x2, waiting for transfers between devices, per_device(): lax.all_to_all(returning, 'target', split_axis=0, concat_axis=0, tiled=True)  64.8 us
    all_to_all x1, waiting for transfers between devices, per_device(): lax.all_to_all(outgoing, 'target', split_axis=0, concat_axis=0, tiled=True)  58.5 us
    another operation x2, other arithmetic, per_device(): jnp.stack([jnp.stack([-data_real, -data_imag], 3), jnp.stack([data_imag,...  23.6 us
    unnamed x25, local copies, waits for them, and re-layouts  20.5 us
    all_to_all x1, waiting for transfers between devices, per_device(): lax.all_to_all(split_value, 'surface', split_axis=3, concat_axis=3, tiled...  20.5 us
    dot_general x2, matrix products, per_device(): jnp.einsum('fcar,flkecr->lakef', misfit, backward[:, :, lo:hi], preferred...  20.2 us
    transpose x2, local copies, waits for them, and re-layouts, per_device(): jnp.einsum('fcar,flkecr->lakef', misfit, backward[:, :, lo:hi], preferred...  16.1 us
    all_to_all x2, starting transfers between devices, per_device(): lax.all_to_all(returning, 'target', split_axis=0, concat_axis=0, tiled=True)  13.9 us
  transfers between devices with their start and end apart: 5, of which 5 were waited for; matrix products, arithmetic and copies ran while one was open for 23% of the time, Pallas kernels for 0%

profile of v5, /device:TPU:1, one launch (start us, length us, event | category | flops | bytes accessed | tf_op | source)
XLA Modules:
  0.0 366.9 jit_solution(10870306684224233639)
XLA Ops:
  0.6 0.7 fusion.55
  1.4 0.7 fusion.42
  2.1 1.1 convert_element_type.57
  3.2 5.6 %gather_fusion = bf16[32,32,4,512]{3,2,1,0:T(4,128)(2,1)} fusion(bf16[2,32,4,512]{3,2,1,0:T(4,128)(2,1)S(1)} %convert_element_type.57, s32[1024]{0:T(1024)S(1)} %pad_clamp_fusion.2), kind=kCustom, calls=%fused_computation | custom fusion | bytes 8388736 | tf_op jit(solution)/shard_map/gather | solution.py:44
  8.8 11.9 %all-to-all-start = ((bf16[32,32,4,512]{3,2,1,0:T(4,128)(2,1)}), bf16[32,32,4,512]{3,2,1,0:T(4,128)(2,1)}, u32[]{:S(2)}, u32[]{:S(2)}) async-start(bf16[32,32,4,512]{3,2,1,0:T(4,128)(2,1)} %gather_fusion), calls=%async_computation | async-start | bytes 8388608 | tf_op jit(solution)/shard_map/all_to_all | solution.py:45
  20.7 1.8 fusion.57
  22.5 0.0 copy-start.8
  22.5 6.5 %copy.142 = bf16[1,16,1,4,32,256]{4,1,3,5,2,0:T(8,128)(2,1)} copy(bf16[1,16,1,4,32,256]{5,4,3,2,1,0:T(8,128)(2,1)S(1)} %get-tuple-element.29) | data formatting | bytes 2097152
  29.0 6.5 %copy.141 = bf16[1,16,1,4,32,256]{4,1,3,5,2,0:T(8,128)(2,1)} copy(bf16[1,16,1,4,32,256]{5,4,3,2,1,0:T(8,128)(2,1)S(1)} %get-tuple-element.30) | data formatting | bytes 2097152
  35.5 0.2 fusion.44
  35.7 2.0 cosine_convert_fusion
  37.7 2.0 negate_convert_fusion
  39.7 2.9 fusion.10
  42.6 0.6 copy-done.1
  43.2 0.5 fusion.9
  43.7 1.6 copy-done
  45.4 11.3 %maximum_bitcast_fusion.1 = (bf16[256,16,4,1,2,32]{5,1,2,4,0,3:T(8,128)(2,1)}, bf16[256,16,4,1,2,32]{5,1,2,3,4,0:T(8,128)(2,1)}, bf16[256,16,4,1,2,32]{5,1,2,3,4,0:T(8,128)(2,1)}, bf16[256,16,4,1,2,32]{5,1,2,4,0,3:T(8,128)(2,1)}) fusion(bf16[256,16,4,1,32]{4,1,2,3,0:T(8,128)(2,1)S(1)} %fusion.9, bf16[256,16,4,1,32]{4,1,2,3,0:T(8,128)(2,1)S(1)} %bitcast.112, ...), kind=kLoop, calls=%fused_computation.13 | loop fusion | flops 4194304 | bytes 12582912 | tf_op jit(solution)/shard_map/stack | solution.py:51
  56.7 58.5 %all-to-all-done = bf16[32,32,4,512]{3,2,1,0:T(4,128)(2,1)} async-done(((bf16[32,32,4,512]{3,2,1,0:T(4,128)(2,1)}), bf16[32,32,4,512]{3,2,1,0:T(4,128)(2,1)}, u32[]{:S(2)}, u32[]{:S(2)}) %all-to-all-start) | async-done | bytes 4194336 | tf_op jit(solution)/shard_map/all_to_all | solution.py:45
  115.2 5.7 %gather_fusion.1 = bf16[16,32,4,512]{3,2,1,0:T(4,128)(2,1)} fusion(bf16[32,32,4,512]{3,2,1,0:T(4,128)(2,1)} %all-to-all-done, s32[1024]{0:T(1024)S(1)} %pad_clamp_fusion.1), kind=kCustom, calls=%fused_computation.1 | custom fusion | bytes 4194368 | tf_op jit(solution)/shard_map/gather | solution.py:55
  120.9 2.8 convert_bitcast_fusion
  123.8 12.0 %copy.127 = bf16[256,16,32,4,2,1]{2,1,3,4,5,0:T(8,128)(2,1)} copy(bf16[256,16,32,4,2,1]{0,2,3,1,4,5:T(8,128)(2,1)S(1)} %convert_bitcast_fusion) | data formatting | bytes 4194304 | tf_op jit(solution)/shard_map/convert_element_type | solution.py:56
  135.8 13.6 %fusion = f32[256,2,32,32,1,1]{3,2,5,4,1,0:T(8,128)} fusion(bf16[256,16,32,4,2,1]{2,1,3,4,5,0:T(8,128)(2,1)} %copy.127, bf16[256,16,4,1,2,32]{5,1,2,3,4,0:T(8,128)(2,1)} %get-tuple-element.27, bf16[256,16,4,1,2,32]{5,1,2,3,4,0:T(8,128)(2,1)} %get-tuple-element.26), kind=kOutput, calls=%fused_computation.6 | convolution fusion | flops 136314880 | bytes 8388608 | tf_op jit(solution)/shard_map/flakc,flkcdr->fdar/dot_general | solution.py:57
  149.3 8.0 %copy.112 = f32[256,2,32,8,4]{0,2,4,1,3:T(8,128)} copy(f32[256,2,32,8,4]{2,4,3,1,0:T(4,128)} %bitcast.114) | data formatting | bytes 4194304 | tf_op jit(solution)/shard_map/reshape | solution.py:61
  157.4 6.5 %all-to-all-start.1 = ((f32[256,2,32,8,4]{0,2,4,1,3:T(8,128)}), f32[256,2,32,8,4]{0,2,4,1,3:T(8,128)S(1)}, u32[]{:S(2)}, u32[]{:S(2)}) async-start(f32[256,2,32,8,4]{0,2,4,1,3:T(8,128)} %copy.112), calls=%async_computation.1 | async-start | bytes 4194304 | tf_op jit(solution)/shard_map/all_to_all | solution.py:62
  163.9 0.0 copy-done.7
  163.9 1.1 copy.108
  165.0 1.9 fusion.39
  166.9 1.9 sine_negate_fusion
  168.8 0.7 iota_reduce_fusion
  169.5 20.5 %all-to-all-done.1 = f32[256,2,32,8,4]{0,2,4,1,3:T(8,128)S(1)} async-done(((f32[256,2,32,8,4]{0,2,4,1,3:T(8,128)}), f32[256,2,32,8,4]{0,2,4,1,3:T(8,128)S(1)}, u32[]{:S(2)}, u32[]{:S(2)}) %all-to-all-start.1) | async-done | bytes 2097184 | tf_op jit(solution)/shard_map/all_to_all | solution.py:62
  190.0 0.2 reduce_sum.40
  190.2 0.5 copy.140
  190.7 2.4 fusion.22
  193.0 0.3 copy.114
  193.4 1.1 broadcast_in_dim.56
  194.5 5.5 %all-to-all-start.2 = ((bf16[256,2,32,8,4]{0,2,4,1,3:T(8,128)(2,1)}), bf16[256,2,32,8,4]{0,2,4,1,3:T(8,128)(2,1)S(1)}, u32[]{:S(2)}, u32[]{:S(2)}) async-start(bf16[256,2,32,8,4]{0,2,4,1,3:T(8,128)(2,1)} %broadcast_in_dim.56), calls=%async_computation.2 | async-start | bytes 2097152 | tf_op jit(solution)/shard_map/all_to_all | solution.py:67
  200.0 12.3 %pad_maximum_fusion = (bf16[256,16,2,2,2,32]{5,1,2,4,0,3:T(8,128)(2,1)}, bf16[256,16,2,2,2,32]{5,1,2,4,0,3:T(8,128)(2,1)}) fusion(bf16[256,16,4,1,2,32]{5,1,2,4,0,3:T(8,128)(2,1)} %get-tuple-element.25, bf16[256,16,4,1,2,32]{5,1,2,4,0,3:T(8,128)(2,1)} %get-tuple-element.28), kind=kLoop, calls=%fused_computation.11 | loop fusion | flops 2097152 | bytes 8388608 | tf_op jit(solution)/shard_map/stack | solution.py:51
  212.2 2.1 all-to-all-done.2
  214.3 0.1 copy.115
  214.4 6.9 %copy.129 = bf16[256,2,32,32,1,1]{3,2,1,5,4,0:T(8,128)(2,1)} copy(bf16[256,2,32,32,1,1]{0,2,3,1,5,4:T(8,128)(2,1)S(1)} %bitcast.115) | data formatting | bytes 2097152 | tf_op jit(solution)/shard_map/reshape | solution.py:68
  221.3 10.1 %fusion.14 = f32[16,32,2,2,256]{1,0,3,2,4:T(8,128)} fusion(bf16[256,2,32,32,1,1]{3,2,1,5,4,0:T(8,128)(2,1)} %copy.129, bf16[256,16,2,2,2,32]{5,1,2,4,0,3:T(8,128)(2,1)} %get-tuple-element.23), kind=kOutput, calls=%fused_computation.27 | convolution fusion | flops 67108864 | bytes 5242880 | tf_op jit(solution)/shard_map/fcar,flkecr->lakef/dot_general | solution.py:76
  231.4 7.5 %copy.122 = f32[16,32,2,2,256]{4,3,1,2,0:T(2,128)S(1)} copy(f32[16,32,2,2,256]{1,0,3,2,4:T(8,128)} %fusion.14) | data formatting | bytes 4194304 | tf_op jit(solution)/shard_map/fcar,flkecr->lakef/transpose | solution.py:76
  238.9 2.7 reshape.195
  241.6 0.0 copy-done.3
  241.6 3.4 convolution_convert_fusion
  245.0 2.0 gather_fusion.3
  247.1 8.4 %all-to-all-start.4 = ((bf16[32,32,2,512]{3,1,2,0:T(8,128)(2,1)}), bf16[32,32,2,512]{3,1,2,0:T(8,128)(2,1)S(1)}, u32[]{:S(2)}, u32[]{:S(2)}) async-start(bf16[32,32,2,512]{3,1,2,0:T(8,128)(2,1)} %gather_fusion.3), calls=%async_computation.4 | async-start | bytes 4194304 | tf_op jit(solution)/shard_map/all_to_all | solution.py:82
  255.4 10.1 %fusion.11 = f32[16,32,2,2,256]{1,0,3,2,4:T(8,128)} fusion(bf16[256,2,32,32,1,1]{3,2,1,5,4,0:T(8,128)(2,1)} %copy.129, bf16[256,16,2,2,2,32]{5,1,2,4,0,3:T(8,128)(2,1)} %get-tuple-element.24), kind=kOutput, calls=%fused_computation.26 | convolution fusion | flops 67108864 | bytes 5242880 | tf_op jit(solution)/shard_map/fcar,flkecr->lakef/dot_general | solution.py:76
  265.6 8.5 %copy.118 = f32[16,32,2,2,256]{4,3,1,2,0:T(2,128)} copy(f32[16,32,2,2,256]{1,0,3,2,4:T(8,128)} %fusion.11) | data formatting | bytes 4194304 | tf_op jit(solution)/shard_map/fcar,flkecr->lakef/transpose | solution.py:76
  274.1 3.9 %reshape.194 = f32[16,32,2,512]{3,1,2,0:T(8,128)} reshape(f32[16,32,2,2,256]{4,3,1,2,0:T(2,128)} %copy.118) | data formatting | bytes 4194304 | tf_op jit(solution)/shard_map/reshape | solution.py:79
  278.0 3.7 convolution_convert_fusion.1
  281.7 2.0 gather_fusion.2
  283.7 21.1 %all-to-all-done.4 = bf16[32,32,2,512]{3,1,2,0:T(8,128)(2,1)S(1)} async-done(((bf16[32,32,2,512]{3,1,2,0:T(8,128)(2,1)}), bf16[32,32,2,512]{3,1,2,0:T(8,128)(2,1)S(1)}, u32[]{:S(2)}, u32[]{:S(2)}) %all-to-all-start.4) | async-done | bytes 2097184 | tf_op jit(solution)/shard_map/all_to_all | solution.py:82
  304.8 5.5 %all-to-all-start.3 = ((bf16[32,32,2,512]{3,1,2,0:T(8,128)(2,1)}), bf16[32,32,2,512]{3,1,2,0:T(8,128)(2,1)}, u32[]{:S(2)}, u32[]{:S(2)}) async-start(bf16[32,32,2,512]{3,1,2,0:T(8,128)(2,1)} %gather_fusion.2), calls=%async_computation.3 | async-start | bytes 4194304 | tf_op jit(solution)/shard_map/all_to_all | solution.py:82
  310.3 2.2 fusion.58
  312.5 1.2 copy.125
  313.7 2.5 convert_element_type.65
  316.2 43.7 %all-to-all-done.3 = bf16[32,32,2,512]{3,1,2,0:T(8,128)(2,1)} async-done(((bf16[32,32,2,512]{3,1,2,0:T(8,128)(2,1)}), bf16[32,32,2,512]{3,1,2,0:T(8,128)(2,1)}, u32[]{:S(2)}, u32[]{:S(2)}) %all-to-all-start.3) | async-done | bytes 2097184 | tf_op jit(solution)/shard_map/all_to_all | solution.py:82
  359.9 2.3 convert_element_type.63
  362.2 0.5 copy-done.2
  362.7 1.6 select_reduce_fusion.1
  364.4 0.2 copy_subtract_fusion
  364.6 0.9 copy.124
  365.5 1.1 copy.123
  (21 shorter events, 0.1 us)
Async XLA Ops:
  8.8 106.4 %all-to-all-start = ((bf16[32,32,4,512]{3,2,1,0:T(4,128)(2,1)}), bf16[32,32,4,512]{3,2,1,0:T(4,128)(2,1)}, u32[]{:S(2)}, u32[]{:S(2)}) async-start(bf16[32,32,4,512]{3,2,1,0:T(4,128)(2,1)} %gather_fusion), calls=%async_computation | async-start | bytes 8388608 | tf_op jit(solution)/shard_map/all_to_all | solution.py:45
  22.5 13.0 %copy-start.8 = (s32[32,16]{0,1:T(8,128)S(1)}, s32[32,16]{0,1:T(8,128)}, u32[]{:S(2)}) copy-start(s32[32,16]{0,1:T(8,128)} %param.7) | copy-start | bytes 6148
  39.7 3.5 copy-start.1
  43.2 2.2 copy-start
  157.4 6.5 %copy-start.7 = (bf16[1,2,32,4,256]{4,3,2,1,0:T(4,128)(2,1)S(1)}, bf16[1,2,32,4,256]{4,3,2,1,0:T(4,128)(2,1)}, u32[]{:S(2)}) copy-start(bf16[1,2,32,4,256]{4,3,2,1,0:T(4,128)(2,1)} %param.6) | copy-start | bytes 393220
  157.4 32.6 %all-to-all-start.1 = ((f32[256,2,32,8,4]{0,2,4,1,3:T(8,128)}), f32[256,2,32,8,4]{0,2,4,1,3:T(8,128)S(1)}, u32[]{:S(2)}, u32[]{:S(2)}) async-start(f32[256,2,32,8,4]{0,2,4,1,3:T(8,128)} %copy.112), calls=%async_computation.1 | async-start | bytes 4194304 | tf_op jit(solution)/shard_map/all_to_all | solution.py:62
  166.9 74.7 %copy-start.3 = (f32[512,256]{1,0:T(8,128)}, f32[512,256]{1,0:T(8,128)S(1)}, u32[]{:S(2)}) copy-start(f32[512,256]{1,0:T(8,128)S(1)} %fusion.39) | copy-start | bytes 1572868
  168.8 72.8 %copy-start.4 = (f32[512,256]{1,0:T(8,128)}, f32[512,256]{1,0:T(8,128)S(1)}, u32[]{:S(2)}) copy-start(f32[512,256]{1,0:T(8,128)S(1)} %sine_negate_fusion) | copy-start | bytes 1572868
  194.5 19.8 %all-to-all-start.2 = ((bf16[256,2,32,8,4]{0,2,4,1,3:T(8,128)(2,1)}), bf16[256,2,32,8,4]{0,2,4,1,3:T(8,128)(2,1)S(1)}, u32[]{:S(2)}, u32[]{:S(2)}) async-start(bf16[256,2,32,8,4]{0,2,4,1,3:T(8,128)(2,1)} %broadcast_in_dim.56), calls=%async_computation.2 | async-start | bytes 2097152 | tf_op jit(solution)/shard_map/all_to_all | solution.py:67
  247.1 57.7 %all-to-all-start.4 = ((bf16[32,32,2,512]{3,1,2,0:T(8,128)(2,1)}), bf16[32,32,2,512]{3,1,2,0:T(8,128)(2,1)S(1)}, u32[]{:S(2)}, u32[]{:S(2)}) async-start(bf16[32,32,2,512]{3,1,2,0:T(8,128)(2,1)} %gather_fusion.3), calls=%async_computation.4 | async-start | bytes 4194304 | tf_op jit(solution)/shard_map/all_to_all | solution.py:82
  283.7 28.8 %copy-start.5 = (f32[1,2,32,4,256]{2,3,1,4,0:T(4,128)S(1)}, f32[1,2,32,4,256]{2,3,1,4,0:T(4,128)}, u32[]{:S(2)}) copy-start(f32[1,2,32,4,256]{2,3,1,4,0:T(4,128)} %get-tuple-element.31) | copy-start | bytes 786436
  304.8 55.1 %all-to-all-start.3 = ((bf16[32,32,2,512]{3,1,2,0:T(8,128)(2,1)}), bf16[32,32,2,512]{3,1,2,0:T(8,128)(2,1)}, u32[]{:S(2)}, u32[]{:S(2)}) async-start(bf16[32,32,2,512]{3,1,2,0:T(8,128)(2,1)} %gather_fusion.2), calls=%async_computation.3 | async-start | bytes 4194304 | tf_op jit(solution)/shard_map/all_to_all | solution.py:82
  359.9 2.8 copy-start.2
  362.7 1.6 copy-start.6

commit v6 on v5

--- a/solution.py
+++ b/solution.py
@@ -6,7 +6,7 @@
 from jax.sharding import PartitionSpec as P
 
 step_length = 0.5
-chunks = 2
+chunks = 4
 
 
 def make_table(samples):

time: 371 us -> 390 us (1.051)
  waiting for transfers between devices: 146 us -> 121 us
  local copies, waits for them, and re-layouts: 91 us -> 105 us
  starting transfers between devices: 37.7 us -> 51.3 us
  matrix products: 43.7 us -> 52.2 us
  other arithmetic: 47.6 us -> 53.8 us
    all_to_all x2 -> x4, waiting for transfers between devices: 64.8 us -> 41.5 us  [per_device(): lax.all_to_all(returning, 'target', split_axis=0, concat_axis=0, tiled=True)]
    another operation x2 -> x3, other arithmetic: 3.98 us -> 18.1 us
    all_to_all x2 -> x4, starting transfers between devices: 13.9 us -> 27.8 us  [per_device(): lax.all_to_all(returning, 'target', split_axis=0, concat_axis=0, tiled=True)]
    another operation x2 -> x1, other arithmetic: 23.6 us -> 11.3 us  [per_device(): jnp.stack([jnp.stack([-data_real, -data_imag], 3), jnp.stack([data_imag,...]
    another operation x0 -> x4, local copies, waits for them, and re-layouts: none -> 12.3 us
    reshape x2 -> x0, local copies, waits for them, and re-layouts: 6.63 us -> none  [per_device(): grad_flat = grad_spectra.reshape(grad_spectra.shape[:3] + (samples,))]
    dot_general x2 -> x4, matrix products: 20.2 us -> 26.7 us  [per_device(): jnp.einsum('fcar,flkecr->lakef', misfit, backward[:, :, lo:hi], preferred...]
    convert_element_type x2 -> x4, other arithmetic: 4.83 us -> 8.8 us  [per_device(): received[None].astype(jnp.float32)]
  transfers between devices with their start and end apart: 5 -> 7, of which waited for: 5 -> 7; matrix products, arithmetic and copies ran while one was open for 23% -> 31% of each run, Pallas kernels for 0% -> 0%
where the time goes in v6:
time: 390 us; the launch traced here: 385 us
  waiting for transfers between devices  121 us (31%)
  local copies, waits for them, and re-layouts  105 us (27%)
  other arithmetic  53.8 us (14%)
  matrix products  52.2 us (13%)
  starting transfers between devices  51.3 us (13%)
    all_to_all x1, waiting for transfers between devices, per_device(): lax.all_to_all(outgoing, 'target', split_axis=0, concat_axis=0, tiled=True)  58.5 us
    all_to_all x4, waiting for transfers between devices, per_device(): lax.all_to_all(returning, 'target', split_axis=0, concat_axis=0, tiled=True)  41.5 us
    all_to_all x4, starting transfers between devices, per_device(): lax.all_to_all(returning, 'target', split_axis=0, concat_axis=0, tiled=True)  27.8 us
    dot_general x4, matrix products, per_device(): jnp.einsum('fcar,flkecr->lakef', misfit, backward[:, :, lo:hi], preferred...  26.7 us
    unnamed x21, local copies, waits for them, and re-layouts  21.1 us
    all_to_all x1, waiting for transfers between devices, per_device(): lax.all_to_all(split_value, 'surface', split_axis=3, concat_axis=3, tiled...  20.6 us
    transpose x4, local copies, waits for them, and re-layouts, per_device(): jnp.einsum('fcar,flkecr->lakef', misfit, backward[:, :, lo:hi], preferred...  19 us
    another operation x3, other arithmetic  18.1 us
  transfers between devices with their start and end apart: 7, of which 7 were waited for; matrix products, arithmetic and copies ran while one was open for 31% of the time, Pallas kernels for 0%

profile of v6, /device:TPU:1, one launch (start us, length us, event | category | flops | bytes accessed | tf_op | source)
XLA Modules:
  0.0 384.5 jit_solution(10845788318893438522)
XLA Ops:
  2.1 1.1 convert_element_type.111
  3.2 5.7 %gather_fusion = bf16[32,32,4,512]{3,2,1,0:T(4,128)(2,1)} fusion(bf16[2,32,4,512]{3,2,1,0:T(4,128)(2,1)S(1)} %convert_element_type.111, s32[1024]{0:T(1024)S(1)} %pad_clamp_fusion.2), kind=kCustom, calls=%fused_computation | custom fusion | bytes 8388736 | tf_op jit(solution)/shard_map/gather | solution.py:44
  8.9 11.4 %all-to-all-start = ((bf16[32,32,4,512]{3,2,1,0:T(4,128)(2,1)}), bf16[32,32,4,512]{3,2,1,0:T(4,128)(2,1)}, u32[]{:S(2)}, u32[]{:S(2)}) async-start(bf16[32,32,4,512]{3,2,1,0:T(4,128)(2,1)} %gather_fusion), calls=%async_computation | async-start | bytes 8388608 | tf_op jit(solution)/shard_map/all_to_all | solution.py:45
  20.3 1.8 fusion.75
  22.1 6.5 %copy.212 = bf16[1,16,1,4,32,256]{4,1,3,5,2,0:T(8,128)(2,1)} copy(bf16[1,16,1,4,32,256]{5,4,3,2,1,0:T(8,128)(2,1)S(1)} %get-tuple-element.37) | data formatting | bytes 2097152
  28.6 6.5 %copy.213 = bf16[1,16,1,4,32,256]{4,1,3,5,2,0:T(8,128)(2,1)} copy(bf16[1,16,1,4,32,256]{5,4,3,2,1,0:T(8,128)(2,1)S(1)} %get-tuple-element.36) | data formatting | bytes 2097152
  35.4 2.0 cosine_convert_fusion
  37.3 2.0 negate_convert_fusion
  39.4 2.9 fusion.11
  43.4 1.6 copy-done
  45.0 11.3 %maximum_bitcast_fusion.1 = (bf16[256,16,4,1,2,32]{5,1,2,4,0,3:T(8,128)(2,1)}, bf16[256,16,4,1,2,32]{5,1,2,3,4,0:T(8,128)(2,1)}, bf16[256,16,4,1,2,32]{5,1,2,3,4,0:T(8,128)(2,1)}, bf16[256,16,4,1,2,32]{5,1,2,4,0,3:T(8,128)(2,1)}) fusion(bf16[256,16,4,1,32]{4,1,2,3,0:T(8,128)(2,1)S(1)} %fusion.11, bf16[256,16,4,1,32]{4,1,2,3,0:T(8,128)(2,1)S(1)} %bitcast.177, ...), kind=kLoop, calls=%fused_computation.17 | loop fusion | flops 4194304 | bytes 12582912 | tf_op jit(solution)/shard_map/stack | solution.py:51
  56.3 58.5 %all-to-all-done = bf16[32,32,4,512]{3,2,1,0:T(4,128)(2,1)} async-done(((bf16[32,32,4,512]{3,2,1,0:T(4,128)(2,1)}), bf16[32,32,4,512]{3,2,1,0:T(4,128)(2,1)}, u32[]{:S(2)}, u32[]{:S(2)}) %all-to-all-start) | async-done | bytes 4194336 | tf_op jit(solution)/shard_map/all_to_all | solution.py:45
  114.8 5.7 %gather_fusion.1 = bf16[16,32,4,512]{3,2,1,0:T(4,128)(2,1)} fusion(bf16[32,32,4,512]{3,2,1,0:T(4,128)(2,1)} %all-to-all-done, s32[1024]{0:T(1024)S(1)} %pad_clamp_fusion.1), kind=kCustom, calls=%fused_computation.1 | custom fusion | bytes 4194368 | tf_op jit(solution)/shard_map/gather | solution.py:55
  120.6 2.8 convert_bitcast_fusion
  123.4 12.0 %copy.191 = bf16[256,16,32,4,2,1]{2,1,3,4,5,0:T(8,128)(2,1)} copy(bf16[256,16,32,4,2,1]{0,2,3,1,4,5:T(8,128)(2,1)S(1)} %convert_bitcast_fusion) | data formatting | bytes 4194304 | tf_op jit(solution)/shard_map/convert_element_type | solution.py:56
  135.4 13.6 %fusion = f32[256,2,32,32,1,1]{3,2,5,4,1,0:T(8,128)} fusion(bf16[256,16,32,4,2,1]{2,1,3,4,5,0:T(8,128)(2,1)} %copy.191, bf16[256,16,4,1,2,32]{5,1,2,3,4,0:T(8,128)(2,1)} %get-tuple-element.34, bf16[256,16,4,1,2,32]{5,1,2,3,4,0:T(8,128)(2,1)} %get-tuple-element.33), kind=kOutput, calls=%fused_computation.12 | convolution fusion | flops 136314880 | bytes 8388608 | tf_op jit(solution)/shard_map/flakc,flkcdr->fdar/dot_general | solution.py:57
  149.0 8.0 %copy.164 = f32[256,2,32,8,4]{0,2,4,1,3:T(8,128)} copy(f32[256,2,32,8,4]{2,4,3,1,0:T(4,128)} %bitcast.178) | data formatting | bytes 4194304 | tf_op jit(solution)/shard_map/reshape | solution.py:61
  157.0 6.5 %all-to-all-start.1 = ((f32[256,2,32,8,4]{0,2,4,1,3:T(8,128)}), f32[256,2,32,8,4]{0,2,4,1,3:T(8,128)S(1)}, u32[]{:S(2)}, u32[]{:S(2)}) async-start(f32[256,2,32,8,4]{0,2,4,1,3:T(8,128)} %copy.164), calls=%async_computation.1 | async-start | bytes 4194304 | tf_op jit(solution)/shard_map/all_to_all | solution.py:62
  163.5 1.1 copy.160
  165.2 1.9 fusion.55
  167.2 1.9 sine_negate_fusion
  169.1 20.6 %all-to-all-done.1 = f32[256,2,32,8,4]{0,2,4,1,3:T(8,128)S(1)} async-done(((f32[256,2,32,8,4]{0,2,4,1,3:T(8,128)}), f32[256,2,32,8,4]{0,2,4,1,3:T(8,128)S(1)}, u32[]{:S(2)}, u32[]{:S(2)}) %all-to-all-start.1) | async-done | bytes 2097184 | tf_op jit(solution)/shard_map/all_to_all | solution.py:62
  189.8 1.3 copy.211
  191.2 1.7 fusion.38
  193.2 1.1 broadcast_in_dim.80
  194.3 5.7 %all-to-all-start.2 = ((bf16[256,2,32,8,4]{0,2,4,1,3:T(8,128)(2,1)}), bf16[256,2,32,8,4]{0,2,4,1,3:T(8,128)(2,1)}, u32[]{:S(2)}, u32[]{:S(2)}) async-start(bf16[256,2,32,8,4]{0,2,4,1,3:T(8,128)(2,1)} %broadcast_in_dim.80), calls=%async_computation.2 | async-start | bytes 2097152 | tf_op jit(solution)/shard_map/all_to_all | solution.py:67
  200.0 14.1 %fusion.10 = (bf16[256,16,2,2,32]{4,1,3,0,2:T(8,128)(2,1)}, bf16[256,16,2,2,32]{4,1,3,0,2:T(8,128)(2,1)}, bf16[256,16,2,2,32]{4,1,3,0,2:T(8,128)(2,1)}, bf16[256,16,2,2,32]{4,1,3,0,2:T(8,128)(2,1)}) fusion(bf16[256,16,4,1,2,32]{5,1,2,4,0,3:T(8,128)(2,1)} %get-tuple-element.32, bf16[256,16,4,1,2,32]{5,1,2,4,0,3:T(8,128)(2,1)} %get-tuple-element.35), kind=kLoop, calls=%fused_computation.27 | loop fusion | flops 2097152 | bytes 8388608 | tf_op jit(solution)/shard_map/reshape.27
  214.4 2.3 copy.167
  216.7 8.6 %copy.193 = bf16[256,2,32,32,1]{3,2,1,4,0:T(8,128)(2,1)} copy(bf16[256,2,32,32,1]{0,2,3,1,4:T(8,128)(2,1)} %bitcast.179) | data formatting | bytes 2097152 | tf_op jit(solution)/shard_map/reshape | solution.py:68
  225.3 6.7 %fusion.30 = f32[16,32,1,2,256]{1,0,3,4,2:T(8,128)} fusion(bf16[256,2,32,32,1]{3,2,1,4,0:T(8,128)(2,1)} %copy.193, bf16[256,16,2,2,32]{4,1,3,0,2:T(8,128)(2,1)} %get-tuple-element.28), kind=kOutput, calls=%fused_computation.47 | convolution fusion | flops 33554432 | bytes 3145728 | tf_op jit(solution)/shard_map/fcar,flkecr->lakef/dot_general | solution.py:76
  232.0 4.7 %copy.185 = f32[16,32,1,2,256]{4,3,1,0,2:T(2,128)} copy(f32[16,32,1,2,256]{1,0,3,4,2:T(8,128)} %fusion.30) | data formatting | bytes 2097152 | tf_op jit(solution)/shard_map/fcar,flkecr->lakef/transpose | solution.py:76
  236.7 3.0 reshape.341
  239.8 2.3 convolution_convert_fusion
  242.0 1.6 gather_fusion.5
  243.6 8.1 %all-to-all-start.6 = ((bf16[32,32,1,512]{3,1,2,0:T(8,128)(2,1)}), bf16[32,32,1,512]{3,1,2,0:T(8,128)(2,1)}, u32[]{:S(2)}, u32[]{:S(2)}) async-start(bf16[32,32,1,512]{3,1,2,0:T(8,128)(2,1)} %bitcast.182), calls=%async_computation.6 | async-start | bytes 2097152 | tf_op jit(solution)/shard_map/all_to_all | solution.py:82
  251.7 6.7 %fusion.27 = f32[16,32,1,2,256]{1,0,3,4,2:T(8,128)} fusion(bf16[256,2,32,32,1]{3,2,1,4,0:T(8,128)(2,1)} %copy.193, bf16[256,16,2,2,32]{4,1,3,0,2:T(8,128)(2,1)} %get-tuple-element.31), kind=kOutput, calls=%fused_computation.46 | convolution fusion | flops 33554432 | bytes 3145728 | tf_op jit(solution)/shard_map/fcar,flkecr->lakef/dot_general | solution.py:76
  258.4 4.8 %copy.180 = f32[16,32,1,2,256]{4,3,1,0,2:T(2,128)} copy(f32[16,32,1,2,256]{1,0,3,4,2:T(8,128)} %fusion.27) | data formatting | bytes 2097152 | tf_op jit(solution)/shard_map/fcar,flkecr->lakef/transpose | solution.py:76
  263.1 3.0 reshape.339
  266.1 2.3 convolution_convert_fusion.1
  268.4 1.6 gather_fusion.4
  270.0 8.2 %all-to-all-done.6 = bf16[32,32,1,512]{3,1,2,0:T(8,128)(2,1)} async-done(((bf16[32,32,1,512]{3,1,2,0:T(8,128)(2,1)}), bf16[32,32,1,512]{3,1,2,0:T(8,128)(2,1)}, u32[]{:S(2)}, u32[]{:S(2)}) %all-to-all-start.6) | async-done | bytes 1048608 | tf_op jit(solution)/shard_map/all_to_all | solution.py:82
  278.2 6.8 %all-to-all-start.5 = ((bf16[32,32,1,512]{3,1,2,0:T(8,128)(2,1)}), bf16[32,32,1,512]{3,1,2,0:T(8,128)(2,1)}, u32[]{:S(2)}, u32[]{:S(2)}) async-start(bf16[32,32,1,512]{3,1,2,0:T(8,128)(2,1)} %bitcast.181), calls=%async_computation.5 | async-start | bytes 2097152 | tf_op jit(solution)/shard_map/all_to_all | solution.py:82
  284.9 6.7 %fusion.24 = f32[16,32,1,2,256]{1,0,3,4,2:T(8,128)} fusion(bf16[256,2,32,32,1]{3,2,1,4,0:T(8,128)(2,1)} %copy.193, bf16[256,16,2,2,32]{4,1,3,0,2:T(8,128)(2,1)} %get-tuple-element.30), kind=kOutput, calls=%fused_computation.45 | convolution fusion | flops 33554432 | bytes 3145728 | tf_op jit(solution)/shard_map/fcar,flkecr->lakef/dot_general | solution.py:76
  291.6 4.8 %copy.175 = f32[16,32,1,2,256]{4,3,1,0,2:T(2,128)} copy(f32[16,32,1,2,256]{1,0,3,4,2:T(8,128)} %fusion.24) | data formatting | bytes 2097152 | tf_op jit(solution)/shard_map/fcar,flkecr->lakef/transpose | solution.py:76
  296.4 3.0 reshape.337
  299.4 2.3 convolution_convert_fusion.2
  301.7 1.6 gather_fusion.3
  303.3 8.0 %all-to-all-done.5 = bf16[32,32,1,512]{3,1,2,0:T(8,128)(2,1)} async-done(((bf16[32,32,1,512]{3,1,2,0:T(8,128)(2,1)}), bf16[32,32,1,512]{3,1,2,0:T(8,128)(2,1)}, u32[]{:S(2)}, u32[]{:S(2)}) %all-to-all-start.5) | async-done | bytes 1048608 | tf_op jit(solution)/shard_map/all_to_all | solution.py:82
  311.3 6.5 %all-to-all-start.4 = ((bf16[32,32,1,512]{3,1,2,0:T(8,128)(2,1)}), bf16[32,32,1,512]{3,1,2,0:T(8,128)(2,1)}, u32[]{:S(2)}, u32[]{:S(2)}) async-start(bf16[32,32,1,512]{3,1,2,0:T(8,128)(2,1)} %bitcast.180), calls=%async_computation.4 | async-start | bytes 2097152 | tf_op jit(solution)/shard_map/all_to_all | solution.py:82
  317.8 6.7 %fusion.21 = f32[16,32,1,2,256]{1,0,3,4,2:T(8,128)} fusion(bf16[256,2,32,32,1]{3,2,1,4,0:T(8,128)(2,1)} %copy.193, bf16[256,16,2,2,32]{4,1,3,0,2:T(8,128)(2,1)} %get-tuple-element.29), kind=kOutput, calls=%fused_computation.44 | convolution fusion | flops 33554432 | bytes 3145728 | tf_op jit(solution)/shard_map/fcar,flkecr->lakef/dot_general | solution.py:76
  324.4 4.7 %copy.170 = f32[16,32,1,2,256]{4,3,1,0,2:T(2,128)} copy(f32[16,32,1,2,256]{1,0,3,4,2:T(8,128)} %fusion.21) | data formatting | bytes 2097152 | tf_op jit(solution)/shard_map/fcar,flkecr->lakef/transpose | solution.py:76
  329.2 3.2 reshape.335
  332.3 2.3 convolution_convert_fusion.3
  334.6 1.6 gather_fusion.2
  336.2 8.1 %all-to-all-done.4 = bf16[32,32,1,512]{3,1,2,0:T(8,128)(2,1)} async-done(((bf16[32,32,1,512]{3,1,2,0:T(8,128)(2,1)}), bf16[32,32,1,512]{3,1,2,0:T(8,128)(2,1)}, u32[]{:S(2)}, u32[]{:S(2)}) %all-to-all-start.4) | async-done | bytes 1048608 | tf_op jit(solution)/shard_map/all_to_all | solution.py:82
  344.3 6.5 %all-to-all-start.3 = ((bf16[32,32,1,512]{3,1,2,0:T(8,128)(2,1)}), bf16[32,32,1,512]{3,1,2,0:T(8,128)(2,1)}, u32[]{:S(2)}, u32[]{:S(2)}) async-start(bf16[32,32,1,512]{3,1,2,0:T(8,128)(2,1)} %bitcast.41), calls=%async_computation.3 | async-start | bytes 2097152 | tf_op jit(solution)/shard_map/all_to_all | solution.py:82
  351.8 1.2 copy.189
  353.0 1.5 bitcast_convert_fusion
  354.5 2.9 bitcast_convert_fusion.1
  357.3 2.8 bitcast_convert_fusion.2
  360.1 17.2 %all-to-all-done.3 = bf16[32,32,1,512]{3,1,2,0:T(8,128)(2,1)} async-done(((bf16[32,32,1,512]{3,1,2,0:T(8,128)(2,1)}), bf16[32,32,1,512]{3,1,2,0:T(8,128)(2,1)}, u32[]{:S(2)}, u32[]{:S(2)}) %all-to-all-start.3) | async-done | bytes 1048608 | tf_op jit(solution)/shard_map/all_to_all | solution.py:82
  377.3 1.6 bitcast_convert_fusion.3
  379.2 2.9 select_reduce_fusion.3
  383.2 1.1 copy.187
  (34 shorter events, 6.5 us)
Async XLA Ops:
  8.9 105.9 %all-to-all-start = ((bf16[32,32,4,512]{3,2,1,0:T(4,128)(2,1)}), bf16[32,32,4,512]{3,2,1,0:T(4,128)(2,1)}, u32[]{:S(2)}, u32[]{:S(2)}) async-start(bf16[32,32,4,512]{3,2,1,0:T(4,128)(2,1)} %gather_fusion), calls=%async_computation | async-start | bytes 8388608 | tf_op jit(solution)/shard_map/all_to_all | solution.py:45
  22.1 13.0 %copy-start.6 = (s32[32,16]{0,1:T(8,128)S(1)}, s32[32,16]{0,1:T(8,128)}, u32[]{:S(2)}) copy-start(s32[32,16]{0,1:T(8,128)} %param.7) | copy-start | bytes 6148
  39.4 3.5 copy-start.1
  42.8 2.2 copy-start
  157.0 6.5 %copy-start.5 = (bf16[1,2,32,4,256]{4,3,2,1,0:T(4,128)(2,1)S(1)}, bf16[1,2,32,4,256]{4,3,2,1,0:T(4,128)(2,1)}, u32[]{:S(2)}) copy-start(bf16[1,2,32,4,256]{4,3,2,1,0:T(4,128)(2,1)} %param.6) | copy-start | bytes 393220
  157.0 32.6 %all-to-all-start.1 = ((f32[256,2,32,8,4]{0,2,4,1,3:T(8,128)}), f32[256,2,32,8,4]{0,2,4,1,3:T(8,128)S(1)}, u32[]{:S(2)}, u32[]{:S(2)}) async-start(f32[256,2,32,8,4]{0,2,4,1,3:T(8,128)} %copy.164), calls=%async_computation.1 | async-start | bytes 4194304 | tf_op jit(solution)/shard_map/all_to_all | solution.py:62
  194.3 20.1 %all-to-all-start.2 = ((bf16[256,2,32,8,4]{0,2,4,1,3:T(8,128)(2,1)}), bf16[256,2,32,8,4]{0,2,4,1,3:T(8,128)(2,1)}, u32[]{:S(2)}, u32[]{:S(2)}) async-start(bf16[256,2,32,8,4]{0,2,4,1,3:T(8,128)(2,1)} %broadcast_in_dim.80), calls=%async_computation.2 | async-start | bytes 2097152 | tf_op jit(solution)/shard_map/all_to_all | solution.py:67
  243.6 34.6 %all-to-all-start.6 = ((bf16[32,32,1,512]{3,1,2,0:T(8,128)(2,1)}), bf16[32,32,1,512]{3,1,2,0:T(8,128)(2,1)}, u32[]{:S(2)}, u32[]{:S(2)}) async-start(bf16[32,32,1,512]{3,1,2,0:T(8,128)(2,1)} %bitcast.182), calls=%async_computation.6 | async-start | bytes 2097152 | tf_op jit(solution)/shard_map/all_to_all | solution.py:82
  278.2 33.1 %all-to-all-start.5 = ((bf16[32,32,1,512]{3,1,2,0:T(8,128)(2,1)}), bf16[32,32,1,512]{3,1,2,0:T(8,128)(2,1)}, u32[]{:S(2)}, u32[]{:S(2)}) async-start(bf16[32,32,1,512]{3,1,2,0:T(8,128)(2,1)} %bitcast.181), calls=%async_computation.5 | async-start | bytes 2097152 | tf_op jit(solution)/shard_map/all_to_all | solution.py:82
  311.3 33.0 %all-to-all-start.4 = ((bf16[32,32,1,512]{3,1,2,0:T(8,128)(2,1)}), bf16[32,32,1,512]{3,1,2,0:T(8,128)(2,1)}, u32[]{:S(2)}, u32[]{:S(2)}) async-start(bf16[32,32,1,512]{3,1,2,0:T(8,128)(2,1)} %bitcast.180), calls=%async_computation.4 | async-start | bytes 2097152 | tf_op jit(solution)/shard_map/all_to_all | solution.py:82
  329.2 21.6 %copy-start.3 = (f32[2,32,4,512]{3,2,1,0:T(4,128)S(1)}, f32[2,32,4,512]{3,2,1,0:T(4,128)}, u32[]{:S(2)}) copy-start(f32[2,32,4,512]{3,2,1,0:T(4,128)} %param.4) | copy-start | bytes 1572868
  344.3 33.0 %all-to-all-start.3 = ((bf16[32,32,1,512]{3,1,2,0:T(8,128)(2,1)}), bf16[32,32,1,512]{3,1,2,0:T(8,128)(2,1)}, u32[]{:S(2)}, u32[]{:S(2)}) async-start(bf16[32,32,1,512]{3,1,2,0:T(8,128)(2,1)} %bitcast.41), calls=%async_computation.3 | async-start | bytes 2097152 | tf_op jit(solution)/shard_map/all_to_all | solution.py:82
  377.3 1.9 copy-start.2
  379.2 2.9 copy-start.4

commit v7 on v5

--- a/solution.py
+++ b/solution.py
@@ -33,7 +33,6 @@
     samples = response.shape[3]
     freqs = samples // 2
     dft_table = make_table(samples)
-    table_half = dft_table.astype(jnp.bfloat16).reshape(samples, 2, freqs)
     own_ids = lax.dynamic_slice_in_dim(block_lists, my_index, 1, 0)[0]
     own_owner = own_ids // owned
     wanted = block_lists // owned == my_index
@@ -41,7 +40,10 @@
     slot_for = jnp.sum(jnp.where(wanted, block_lists % owned, 0), axis=1)
     chosen = (slot_for[None, :] == jnp.arange(owned, dtype=jnp.int32)[:, None]) & present[None, :]
     copy_now = response.astype(jnp.bfloat16)
-    outgoing = copy_now[slot_for]
+    own_spectra = jnp.dot(
+        copy_now, dft_table.astype(jnp.bfloat16), preferred_element_type=jnp.float32
+    ).astype(jnp.bfloat16)
+    outgoing = own_spectra.reshape(own_spectra.shape[:3] + (2, freqs))[slot_for]
     arrived = lax.all_to_all(outgoing, "target", split_axis=0, concat_axis=0, tiled=True)
     data_real = jnp.moveaxis(data_spectra[0, :, 0], -1, 0)
     data_imag = jnp.moveaxis(data_spectra[0, :, 1], -1, 0)
@@ -51,11 +53,9 @@
     backward = jnp.stack(
         [jnp.stack([-data_real, -data_imag], 3), jnp.stack([data_imag, -data_real], 3)], 3
     )
-    spectra = jnp.einsum(
-        "lakn,ncf->flakc", arrived[own_owner], table_half, preferred_element_type=jnp.float32
-    ).astype(jnp.bfloat16)
+    spectra = arrived[own_owner]
     partial_value = jnp.einsum(
-        "flakc,flkcdr->fdar", spectra, forward, preferred_element_type=jnp.float32
+        "lakcf,flkcdr->fdar", spectra, forward, preferred_element_type=jnp.float32
     )
     f_dim, parts, shots, recvs = partial_value.shape
     split_value = partial_value.reshape(f_dim, parts, shots, channels, recvs // channels)

time: 371 us -> 363 us (0.978)
  waiting for transfers between devices: 146 us -> 154 us
  local copies, waits for them, and re-layouts: 91 us -> 85.3 us
  other arithmetic: 47.6 us -> 43.6 us
    convert_element_type x1 -> x0, local copies, waits for them, and re-layouts: 12 us -> none  [per_device(): spectra = jnp.einsum('lakn,ncf->flakc', arrived[own_owner], table_half, p...]
    gather x2 -> x3, local copies, waits for them, and re-layouts: 11.3 us -> 17.6 us  [the longest x2 14.9 us: per_device(): spectra = arrived[own_owner]]
    all_to_all x1, waiting for transfers between devices: 58.5 us -> 62.6 us  [per_device(): lax.all_to_all(outgoing, 'target', split_axis=0, concat_axis=0, tiled=True)]
    another operation x2 -> x0, other arithmetic: 3.98 us -> none
    all_to_all x1, waiting for transfers between devices: 20.5 us -> 24.4 us  [per_device(): lax.all_to_all(split_value, 'surface', split_axis=3, concat_axis=3, tiled...]
  transfers between devices with their start and end apart: 5 -> 5, of which waited for: 5 -> 5; matrix products, arithmetic and copies ran while one was open for 23% -> 22% of each run, Pallas kernels for 0% -> 0%
where the time goes in v7:
time: 363 us; the launch traced here: 361 us
  waiting for transfers between devices  154 us (42%)
  local copies, waits for them, and re-layouts  85.3 us (23%)
  other arithmetic  43.6 us (12%)
  matrix products  41 us (11%)
  starting transfers between devices  36.5 us (10%)
    all_to_all x2, waiting for transfers between devices, per_device(): lax.all_to_all(returning, 'target', split_axis=0, concat_axis=0, tiled=True)  64.8 us
    all_to_all x1, waiting for transfers between devices, per_device(): lax.all_to_all(outgoing, 'target', split_axis=0, concat_axis=0, tiled=True)  62.6 us
    all_to_all x1, waiting for transfers between devices, per_device(): lax.all_to_all(split_value, 'surface', split_axis=3, concat_axis=3, tiled...  24.4 us
    another operation x2, other arithmetic, per_device(): jnp.stack([jnp.stack([-data_real, -data_imag], 3), jnp.stack([data_imag,...  23.6 us
    unnamed x25, local copies, waits for them, and re-layouts  20.5 us
    dot_general x2, matrix products, per_device(): jnp.einsum('fcar,flkecr->lakef', misfit, backward[:, :, lo:hi], preferred...  20.2 us
    transpose x2, local copies, waits for them, and re-layouts, per_device(): jnp.einsum('fcar,flkecr->lakef', misfit, backward[:, :, lo:hi], preferred...  16.1 us
    gather x2, local copies, waits for them, and re-layouts, per_device(): spectra = arrived[own_owner]  14.9 us
  transfers between devices with their start and end apart: 5, of which 5 were waited for; matrix products, arithmetic and copies ran while one was open for 22% of the time, Pallas kernels for 0%

profile of v7, /device:TPU:1, one launch (start us, length us, event | category | flops | bytes accessed | tf_op | source)
XLA Modules:
  0.0 361.2 jit_solution(12778920145435969447)
XLA Ops:
  0.6 1.9 fusion.32
  2.5 0.0 copy-start.3
  2.6 1.9 sine_negate_fusion
  4.5 0.0 copy-start.4
  4.5 0.8 fusion.48
  5.3 0.7 fusion.35
  6.0 1.1 convert_element_type.47
  7.2 0.3 convolution_convert_fusion.2
  7.5 2.8 gather_fusion
  10.3 11.1 %all-to-all-start = ((bf16[32,32,4,2,256]{4,1,3,2,0:T(8,128)(2,1)}), bf16[32,32,4,2,256]{4,1,3,2,0:T(8,128)(2,1)}, u32[]{:S(2)}, u32[]{:S(2)}) async-start(bf16[32,32,4,2,256]{4,1,3,2,0:T(8,128)(2,1)} %gather_fusion), calls=%async_computation | async-start | bytes 8388608 | tf_op jit(solution)/shard_map/all_to_all | solution.py:47
  21.4 1.8 fusion.50
  23.2 0.0 copy-start.8
  23.2 6.5 %copy.164 = bf16[1,16,1,4,32,256]{4,1,3,5,2,0:T(8,128)(2,1)} copy(bf16[1,16,1,4,32,256]{5,4,3,2,1,0:T(8,128)(2,1)S(1)} %get-tuple-element.29) | data formatting | bytes 2097152
  29.7 6.5 %copy.163 = bf16[1,16,1,4,32,256]{4,1,3,5,2,0:T(8,128)(2,1)} copy(bf16[1,16,1,4,32,256]{5,4,3,2,1,0:T(8,128)(2,1)S(1)} %get-tuple-element.30) | data formatting | bytes 2097152
  36.2 0.0 copy-done.8
  36.2 0.2 fusion.37
  36.4 2.9 fusion.10
  39.3 0.6 copy-done.1
  39.9 0.5 fusion.9
  40.4 1.6 copy-done
  42.0 11.3 %maximum_bitcast_fusion.1 = (bf16[256,16,4,1,2,32]{5,1,2,4,0,3:T(8,128)(2,1)}, bf16[256,16,4,1,2,32]{5,1,2,3,4,0:T(8,128)(2,1)}, bf16[256,16,4,1,2,32]{5,1,2,3,4,0:T(8,128)(2,1)}, bf16[256,16,4,1,2,32]{5,1,2,4,0,3:T(8,128)(2,1)}) fusion(bf16[256,16,4,1,32]{4,1,2,3,0:T(8,128)(2,1)S(1)} %fusion.9, bf16[256,16,4,1,32]{4,1,2,3,0:T(8,128)(2,1)S(1)} %bitcast.111, ...), kind=kLoop, calls=%fused_computation.13 | loop fusion | flops 4194304 | bytes 12582912 | tf_op jit(solution)/shard_map/stack | solution.py:53
  53.4 62.6 %all-to-all-done = bf16[32,32,4,2,256]{4,1,3,2,0:T(8,128)(2,1)} async-done(((bf16[32,32,4,2,256]{4,1,3,2,0:T(8,128)(2,1)}), bf16[32,32,4,2,256]{4,1,3,2,0:T(8,128)(2,1)}, u32[]{:S(2)}, u32[]{:S(2)}) %all-to-all-start) | async-done | bytes 4194336 | tf_op jit(solution)/shard_map/all_to_all | solution.py:47
  116.0 2.9 gather_fusion.1
  118.9 12.0 %copy.149 = bf16[16,32,4,2,256,1]{1,0,2,3,5,4:T(8,128)(2,1)} copy(bf16[16,32,4,2,256,1]{4,1,3,2,0,5:T(8,128)(2,1)S(1)} %bitcast.114) | data formatting | bytes 4194304 | tf_op jit(solution)/shard_map/gather | solution.py:56
  130.9 13.4 %fusion = f32[256,2,32,32,1,1]{3,2,5,4,1,0:T(8,128)} fusion(bf16[16,32,4,2,256,1]{1,0,2,3,5,4:T(8,128)(2,1)} %copy.149, bf16[256,16,4,1,2,32]{5,1,2,3,4,0:T(8,128)(2,1)} %get-tuple-element.27, bf16[256,16,4,1,2,32]{5,1,2,3,4,0:T(8,128)(2,1)} %get-tuple-element.26), kind=kOutput, calls=%fused_computation.6 | convolution fusion | flops 136314880 | bytes 8388608 | tf_op jit(solution)/shard_map/lakcf,flkcdr->fdar/dot_general | solution.py:57
  144.3 8.0 %copy.134 = f32[256,2,32,8,4]{0,2,4,1,3:T(8,128)} copy(f32[256,2,32,8,4]{2,4,3,1,0:T(4,128)} %bitcast.113) | data formatting | bytes 4194304 | tf_op jit(solution)/shard_map/reshape | solution.py:61
  152.3 6.5 %all-to-all-start.1 = ((f32[256,2,32,8,4]{0,2,4,1,3:T(8,128)}), f32[256,2,32,8,4]{0,2,4,1,3:T(8,128)S(1)}, u32[]{:S(2)}, u32[]{:S(2)}) async-start(f32[256,2,32,8,4]{0,2,4,1,3:T(8,128)} %copy.134), calls=%async_computation.1 | async-start | bytes 4194304 | tf_op jit(solution)/shard_map/all_to_all | solution.py:62
  158.8 1.1 copy.129
  159.9 0.6 iota_reduce_fusion
  160.5 24.4 %all-to-all-done.1 = f32[256,2,32,8,4]{0,2,4,1,3:T(8,128)S(1)} async-done(((f32[256,2,32,8,4]{0,2,4,1,3:T(8,128)}), f32[256,2,32,8,4]{0,2,4,1,3:T(8,128)S(1)}, u32[]{:S(2)}, u32[]{:S(2)}) %all-to-all-start.1) | async-done | bytes 2097184 | tf_op jit(solution)/shard_map/all_to_all | solution.py:62
  185.0 0.2 reduce_sum.40
  185.1 0.5 copy.162
  185.6 2.4 fusion.20
  188.0 0.3 copy.136
  188.3 1.1 broadcast_in_dim.56
  189.5 5.2 %all-to-all-start.2 = ((bf16[256,2,32,8,4]{0,2,4,1,3:T(8,128)(2,1)}), bf16[256,2,32,8,4]{0,2,4,1,3:T(8,128)(2,1)S(1)}, u32[]{:S(2)}, u32[]{:S(2)}) async-start(bf16[256,2,32,8,4]{0,2,4,1,3:T(8,128)(2,1)} %broadcast_in_dim.56), calls=%async_computation.2 | async-start | bytes 2097152 | tf_op jit(solution)/shard_map/all_to_all | solution.py:67
  194.7 12.3 %pad_maximum_fusion = (bf16[256,16,2,2,2,32]{5,1,2,4,0,3:T(8,128)(2,1)}, bf16[256,16,2,2,2,32]{5,1,2,4,0,3:T(8,128)(2,1)}) fusion(bf16[256,16,4,1,2,32]{5,1,2,4,0,3:T(8,128)(2,1)} %get-tuple-element.25, bf16[256,16,4,1,2,32]{5,1,2,4,0,3:T(8,128)(2,1)} %get-tuple-element.28), kind=kLoop, calls=%fused_computation.11 | loop fusion | flops 2097152 | bytes 8388608 | tf_op jit(solution)/shard_map/stack | solution.py:53
  207.0 2.1 all-to-all-done.2
  209.1 0.1 copy.137
  209.2 6.9 %copy.151 = bf16[256,2,32,32,1,1]{3,2,1,5,4,0:T(8,128)(2,1)} copy(bf16[256,2,32,32,1,1]{0,2,3,1,5,4:T(8,128)(2,1)S(1)} %bitcast.115) | data formatting | bytes 2097152 | tf_op jit(solution)/shard_map/reshape | solution.py:68
  216.0 10.1 %fusion.14 = f32[16,32,2,2,256]{1,0,3,2,4:T(8,128)} fusion(bf16[256,2,32,32,1,1]{3,2,1,5,4,0:T(8,128)(2,1)} %copy.151, bf16[256,16,2,2,2,32]{5,1,2,4,0,3:T(8,128)(2,1)} %get-tuple-element.23), kind=kOutput, calls=%fused_computation.27 | convolution fusion | flops 67108864 | bytes 5242880 | tf_op jit(solution)/shard_map/fcar,flkecr->lakef/dot_general | solution.py:76
  226.1 7.5 %copy.144 = f32[16,32,2,2,256]{4,3,1,2,0:T(2,128)S(1)} copy(f32[16,32,2,2,256]{1,0,3,2,4:T(8,128)} %fusion.14) | data formatting | bytes 4194304 | tf_op jit(solution)/shard_map/fcar,flkecr->lakef/transpose | solution.py:76
  233.7 2.7 reshape.154
  236.4 0.0 copy-done.3
  236.4 3.4 convolution_convert_fusion
  239.8 2.0 gather_fusion.3
  241.9 8.0 %all-to-all-start.4 = ((bf16[32,32,2,512]{3,1,2,0:T(8,128)(2,1)}), bf16[32,32,2,512]{3,1,2,0:T(8,128)(2,1)S(1)}, u32[]{:S(2)}, u32[]{:S(2)}) async-start(bf16[32,32,2,512]{3,1,2,0:T(8,128)(2,1)} %gather_fusion.3), calls=%async_computation.4 | async-start | bytes 4194304 | tf_op jit(solution)/shard_map/all_to_all | solution.py:82
  249.9 10.1 %fusion.11 = f32[16,32,2,2,256]{1,0,3,2,4:T(8,128)} fusion(bf16[256,2,32,32,1,1]{3,2,1,5,4,0:T(8,128)(2,1)} %copy.151, bf16[256,16,2,2,2,32]{5,1,2,4,0,3:T(8,128)(2,1)} %get-tuple-element.24), kind=kOutput, calls=%fused_computation.26 | convolution fusion | flops 67108864 | bytes 5242880 | tf_op jit(solution)/shard_map/fcar,flkecr->lakef/dot_general | solution.py:76
  260.0 8.5 %copy.140 = f32[16,32,2,2,256]{4,3,1,2,0:T(2,128)} copy(f32[16,32,2,2,256]{1,0,3,2,4:T(8,128)} %fusion.11) | data formatting | bytes 4194304 | tf_op jit(solution)/shard_map/fcar,flkecr->lakef/transpose | solution.py:76
  268.5 3.9 %reshape.153 = f32[16,32,2,512]{3,1,2,0:T(8,128)} reshape(f32[16,32,2,2,256]{4,3,1,2,0:T(2,128)} %copy.140) | data formatting | bytes 4194304 | tf_op jit(solution)/shard_map/reshape | solution.py:79
  272.5 3.7 %convolution_convert_fusion.1 = bf16[16,32,2,512]{3,1,2,0:T(8,128)(2,1)S(1)} fusion(f32[16,32,2,512]{3,1,2,0:T(8,128)} %reshape.153, f32[512,256]{1,0:T(8,128)} %copy-done.4, f32[512,256]{1,0:T(8,128)} %copy-done.3), kind=kOutput, calls=%fused_computation.29 | convolution fusion | flops 1611399168 | bytes 4194304 | tf_op jit(solution)/shard_map/dot_general | solution.py:80
  276.1 2.0 gather_fusion.2
  278.1 21.1 %all-to-all-done.4 = bf16[32,32,2,512]{3,1,2,0:T(8,128)(2,1)S(1)} async-done(((bf16[32,32,2,512]{3,1,2,0:T(8,128)(2,1)}), bf16[32,32,2,512]{3,1,2,0:T(8,128)(2,1)S(1)}, u32[]{:S(2)}, u32[]{:S(2)}) %all-to-all-start.4) | async-done | bytes 2097184 | tf_op jit(solution)/shard_map/all_to_all | solution.py:82
  299.3 5.6 %all-to-all-start.3 = ((bf16[32,32,2,512]{3,1,2,0:T(8,128)(2,1)}), bf16[32,32,2,512]{3,1,2,0:T(8,128)(2,1)}, u32[]{:S(2)}, u32[]{:S(2)}) async-start(bf16[32,32,2,512]{3,1,2,0:T(8,128)(2,1)} %gather_fusion.2), calls=%async_computation.3 | async-start | bytes 4194304 | tf_op jit(solution)/shard_map/all_to_all | solution.py:82
  304.9 2.2 fusion.51
  307.1 1.2 copy.147
  308.3 2.5 convert_element_type.54
  310.8 43.7 %all-to-all-done.3 = bf16[32,32,2,512]{3,1,2,0:T(8,128)(2,1)} async-done(((bf16[32,32,2,512]{3,1,2,0:T(8,128)(2,1)}), bf16[32,32,2,512]{3,1,2,0:T(8,128)(2,1)}, u32[]{:S(2)}, u32[]{:S(2)}) %all-to-all-start.3) | async-done | bytes 2097184 | tf_op jit(solution)/shard_map/all_to_all | solution.py:82
  354.5 2.3 convert_element_type.52
  356.8 0.5 copy-done.2
  357.3 1.6 select_reduce_fusion.1
  358.9 0.2 copy_subtract_fusion
  359.2 0.9 copy.146
  360.1 1.1 copy.145
  (20 shorter events, 0.2 us)
Async XLA Ops:
  2.5 233.8 %copy-start.3 = (f32[512,256]{1,0:T(8,128)}, f32[512,256]{1,0:T(8,128)S(1)}, u32[]{:S(2)}) copy-start(f32[512,256]{1,0:T(8,128)S(1)} %fusion.32) | copy-start | bytes 1572868
  4.5 231.9 %copy-start.4 = (f32[512,256]{1,0:T(8,128)}, f32[512,256]{1,0:T(8,128)S(1)}, u32[]{:S(2)}) copy-start(f32[512,256]{1,0:T(8,128)S(1)} %sine_negate_fusion) | copy-start | bytes 1572868
  10.3 105.8 %all-to-all-start = ((bf16[32,32,4,2,256]{4,1,3,2,0:T(8,128)(2,1)}), bf16[32,32,4,2,256]{4,1,3,2,0:T(8,128)(2,1)}, u32[]{:S(2)}, u32[]{:S(2)}) async-start(bf16[32,32,4,2,256]{4,1,3,2,0:T(8,128)(2,1)} %gather_fusion), calls=%async_computation | async-start | bytes 8388608 | tf_op jit(solution)/shard_map/all_to_all | solution.py:47
  23.2 13.0 %copy-start.8 = (s32[32,16]{0,1:T(8,128)S(1)}, s32[32,16]{0,1:T(8,128)}, u32[]{:S(2)}) copy-start(s32[32,16]{0,1:T(8,128)} %param.7) | copy-start | bytes 6148
  36.4 3.5 copy-start.1
  39.9 2.2 copy-start
  152.3 6.5 %copy-start.7 = (bf16[1,2,32,4,256]{4,3,2,1,0:T(4,128)(2,1)S(1)}, bf16[1,2,32,4,256]{4,3,2,1,0:T(4,128)(2,1)}, u32[]{:S(2)}) copy-start(bf16[1,2,32,4,256]{4,3,2,1,0:T(4,128)(2,1)} %param.6) | copy-start | bytes 393220
  152.3 32.6 %all-to-all-start.1 = ((f32[256,2,32,8,4]{0,2,4,1,3:T(8,128)}), f32[256,2,32,8,4]{0,2,4,1,3:T(8,128)S(1)}, u32[]{:S(2)}, u32[]{:S(2)}) async-start(f32[256,2,32,8,4]{0,2,4,1,3:T(8,128)} %copy.134), calls=%async_computation.1 | async-start | bytes 4194304 | tf_op jit(solution)/shard_map/all_to_all | solution.py:62
  189.5 19.6 %all-to-all-start.2 = ((bf16[256,2,32,8,4]{0,2,4,1,3:T(8,128)(2,1)}), bf16[256,2,32,8,4]{0,2,4,1,3:T(8,128)(2,1)S(1)}, u32[]{:S(2)}, u32[]{:S(2)}) async-start(bf16[256,2,32,8,4]{0,2,4,1,3:T(8,128)(2,1)} %broadcast_in_dim.56), calls=%async_computation.2 | async-start | bytes 2097152 | tf_op jit(solution)/shard_map/all_to_all | solution.py:67
  241.9 57.4 %all-to-all-start.4 = ((bf16[32,32,2,512]{3,1,2,0:T(8,128)(2,1)}), bf16[32,32,2,512]{3,1,2,0:T(8,128)(2,1)S(1)}, u32[]{:S(2)}, u32[]{:S(2)}) async-start(bf16[32,32,2,512]{3,1,2,0:T(8,128)(2,1)} %gather_fusion.3), calls=%async_computation.4 | async-start | bytes 4194304 | tf_op jit(solution)/shard_map/all_to_all | solution.py:82
  278.1 29.0 %copy-start.5 = (f32[1,2,32,4,256]{2,3,1,4,0:T(4,128)S(1)}, f32[1,2,32,4,256]{2,3,1,4,0:T(4,128)}, u32[]{:S(2)}) copy-start(f32[1,2,32,4,256]{2,3,1,4,0:T(4,128)} %get-tuple-element.31) | copy-start | bytes 786436
  299.3 55.2 %all-to-all-start.3 = ((bf16[32,32,2,512]{3,1,2,0:T(8,128)(2,1)}), bf16[32,32,2,512]{3,1,2,0:T(8,128)(2,1)}, u32[]{:S(2)}, u32[]{:S(2)}) async-start(bf16[32,32,2,512]{3,1,2,0:T(8,128)(2,1)} %gather_fusion.2), calls=%async_computation.3 | async-start | bytes 4194304 | tf_op jit(solution)/shard_map/all_to_all | solution.py:82
  354.5 2.8 copy-start.2
  357.3 1.6 copy-start.6

commit v8 on v7

--- a/solution.py
+++ b/solution.py
@@ -76,14 +76,14 @@
         grad_spectra = jnp.einsum(
             "fcar,flkecr->lakef", misfit, backward[:, :, lo:hi], preferred_element_type=jnp.float32
         )
-        grad_flat = grad_spectra.reshape(grad_spectra.shape[:3] + (samples,))
-        grad_time = jnp.dot(grad_flat, dft_table.T, precision=lax.Precision.HIGH)
-        returning = grad_time.astype(jnp.bfloat16)[entry_for]
+        returning = grad_spectra.astype(jnp.bfloat16)[entry_for]
         received = lax.all_to_all(returning, "target", split_axis=0, concat_axis=0, tiled=True)
         taken = jnp.where(
-            chosen[:, :, None, None, None], received[None].astype(jnp.float32), jnp.zeros((), jnp.float32)
+            chosen[:, :, None, None, None, None], received[None].astype(jnp.float32), jnp.zeros((), jnp.float32)
         )
-        gradient = jnp.sum(taken, axis=1)
+        summed = jnp.sum(taken, axis=1)
+        summed_flat = summed.reshape(summed.shape[:3] + (samples,))
+        gradient = jnp.dot(summed_flat, dft_table.T, precision=lax.Precision.HIGH)
         next_parts.append(response[:, :, lo:hi] - step_length * gradient)
     response_next = next_parts[0] if chunks == 1 else jnp.concatenate(next_parts, axis=2)
     return (response_next, response_next.astype(jnp.bfloat16), residual_share[None])

time: 363 us -> 352 us (0.970)
  local copies, waits for them, and re-layouts: 85.3 us -> 70.7 us
  matrix products: 41 us -> 32.8 us
  waiting for transfers between devices: 154 us -> 162 us
  other arithmetic: 43.6 us -> 47.3 us
    transpose x2 -> x0, local copies, waits for them, and re-layouts: 16.1 us -> none  [per_device(): jnp.einsum('fcar,flkecr->lakef', misfit, backward[:, :, lo:hi], preferred...]
    all_to_all x2, waiting for transfers between devices: 64.8 us -> 76.4 us  [per_device(): lax.all_to_all(returning, 'target', split_axis=0, concat_axis=0, tiled=True)]
    convert_element_type x0 -> x2, local copies, waits for them, and re-layouts: none -> 9.76 us  [per_device(): returning = grad_spectra.astype(jnp.bfloat16)[entry_for]]
    reshape x2, local copies, waits for them, and re-layouts: 6.63 us -> 0.04 us  [per_device(): summed_flat = summed.reshape(summed.shape[:3] + (samples,))]
    dot_general x2, matrix products: 7.1 us -> 1.34 us  [per_device(): gradient = jnp.dot(summed_flat, dft_table.T, precision=lax.Precision.HIGH)]
    all_to_all x1, waiting for transfers between devices: 62.6 us -> 58.3 us  [per_device(): lax.all_to_all(outgoing, 'target', split_axis=0, concat_axis=0, tiled=True)]
    unnamed x25 -> x27, local copies, waits for them, and re-layouts: 20.5 us -> 18.7 us
  transfers between devices with their start and end apart: 5 -> 5, of which waited for: 5 -> 5; matrix products, arithmetic and copies ran while one was open for 22% -> 21% of each run, Pallas kernels for 0% -> 0%
where the time goes in v8:
time: 352 us; the launch traced here: 350 us
  waiting for transfers between devices  162 us (46%)
  local copies, waits for them, and re-layouts  70.7 us (20%)
  other arithmetic  47.3 us (13%)
  starting transfers between devices  36.5 us (10%)
  matrix products  32.8 us (9%)
    all_to_all x2, waiting for transfers between devices, per_device(): lax.all_to_all(returning, 'target', split_axis=0, concat_axis=0, tiled=True)  76.4 us
    all_to_all x1, waiting for transfers between devices, per_device(): lax.all_to_all(outgoing, 'target', split_axis=0, concat_axis=0, tiled=True)  58.3 us
    another operation x2, other arithmetic, per_device(): jnp.stack([jnp.stack([-data_real, -data_imag], 3), jnp.stack([data_imag,...  27 us
    all_to_all x1, waiting for transfers between devices, per_device(): lax.all_to_all(split_value, 'surface', split_axis=3, concat_axis=3, tiled...  25.2 us
    unnamed x27, local copies, waits for them, and re-layouts  18.7 us
    dot_general x2, matrix products, per_device(): jnp.einsum('fcar,flkecr->lakef', misfit, backward[:, :, lo:hi], preferred...  17.7 us
    gather x2, local copies, waits for them, and re-layouts, per_device(): spectra = arrived[own_owner]  14.9 us
    all_to_all x2, starting transfers between devices, per_device(): lax.all_to_all(returning, 'target', split_axis=0, concat_axis=0, tiled=True)  13.6 us
  transfers between devices with their start and end apart: 5, of which 5 were waited for; matrix products, arithmetic and copies ran while one was open for 21% of the time, Pallas kernels for 0%

profile of v8, /device:TPU:1, one launch (start us, length us, event | category | flops | bytes accessed | tf_op | source)
XLA Modules:
  0.0 350.2 jit_solution(13269576661046373476)
XLA Ops:
  0.6 2.1 sine_negate_fusion
  2.7 0.0 copy-start.3
  2.7 0.0 copy-start.5
  2.7 1.5 convert_element_type.53
  4.2 0.3 convolution_convert_fusion
  4.6 0.0 copy-done.3
  4.6 0.0 copy-done.5
  4.6 0.7 fusion.50
  5.3 0.7 fusion.37
  6.1 2.8 gather_fusion
  8.8 11.1 %all-to-all-start = ((bf16[32,32,4,2,256]{4,1,3,2,0:T(8,128)(2,1)}), bf16[32,32,4,2,256]{4,1,3,2,0:T(8,128)(2,1)}, u32[]{:S(2)}, u32[]{:S(2)}) async-start(bf16[32,32,4,2,256]{4,1,3,2,0:T(8,128)(2,1)} %gather_fusion), calls=%async_computation | async-start | bytes 8388608 | tf_op jit(solution)/shard_map/all_to_all | solution.py:47
  20.0 0.0 copy-start.9
  20.0 1.8 fusion.52
  21.7 6.5 %copy.212 = bf16[1,16,1,4,32,256]{4,1,3,5,2,0:T(8,128)(2,1)} copy(bf16[1,16,1,4,32,256]{5,4,3,2,1,0:T(8,128)(2,1)S(1)} %get-tuple-element.42) | data formatting | bytes 2097152
  28.3 6.5 %copy.213 = bf16[1,16,1,4,32,256]{4,1,3,5,2,0:T(8,128)(2,1)} copy(bf16[1,16,1,4,32,256]{5,4,3,2,1,0:T(8,128)(2,1)S(1)} %get-tuple-element.41) | data formatting | bytes 2097152
  34.8 0.0 copy-done.9
  34.8 0.2 fusion.39
  35.0 0.0 copy-start
  35.0 0.0 copy-start.1
  35.0 6.6 %fusion.11 = (bf16[256,16,4,1,32]{4,1,2,3,0:T(8,128)(2,1)S(1)}, bf16[256,16,4,1,32]{4,1,2,3,0:T(8,128)(2,1)}) fusion(bf16[1,16,1,4,32,256]{4,1,3,5,2,0:T(8,128)(2,1)} %copy.212, bf16[1,16,1,4,32,256]{4,1,3,5,2,0:T(8,128)(2,1)} %copy.213), kind=kLoop, calls=%fused_computation.27 | loop fusion | flops 1048576 | bytes 4194304 | tf_op jit(solution)/shard_map/stack | solution.py:54
  41.6 0.0 copy-done
  41.6 14.8 %maximum_bitcast_fusion.1 = (bf16[256,16,4,1,2,32]{5,1,2,4,0,3:T(8,128)(2,1)}, bf16[256,16,4,1,2,32]{5,1,2,3,4,0:T(8,128)(2,1)}, bf16[256,16,4,1,2,32]{5,1,2,3,4,0:T(8,128)(2,1)}, bf16[256,16,4,1,2,32]{5,1,2,4,0,3:T(8,128)(2,1)}) fusion(bf16[256,16,4,1,32]{4,1,2,3,0:T(8,128)(2,1)S(1)} %get-tuple-element.49, bf16[256,16,4,1,32]{4,1,2,3,0:T(8,128)(2,1)S(1)} %bitcast.116, ...), kind=kLoop, calls=%fused_computation.13 | loop fusion | flops 4194304 | bytes 12582912 | tf_op jit(solution)/shard_map/stack | solution.py:53
  56.3 58.3 %all-to-all-done = bf16[32,32,4,2,256]{4,1,3,2,0:T(8,128)(2,1)} async-done(((bf16[32,32,4,2,256]{4,1,3,2,0:T(8,128)(2,1)}), bf16[32,32,4,2,256]{4,1,3,2,0:T(8,128)(2,1)}, u32[]{:S(2)}, u32[]{:S(2)}) %all-to-all-start) | async-done | bytes 4194336 | tf_op jit(solution)/shard_map/all_to_all | solution.py:47
  114.6 2.9 gather_fusion.1
  117.5 12.0 %copy.198 = bf16[16,32,4,2,256,1]{1,0,2,3,5,4:T(8,128)(2,1)} copy(bf16[16,32,4,2,256,1]{4,1,3,2,0,5:T(8,128)(2,1)S(1)} %bitcast.118) | data formatting | bytes 4194304 | tf_op jit(solution)/shard_map/gather | solution.py:56
  129.5 13.4 %fusion = f32[256,2,32,32,1,1]{3,2,5,4,1,0:T(8,128)} fusion(bf16[16,32,4,2,256,1]{1,0,2,3,5,4:T(8,128)(2,1)} %copy.198, bf16[256,16,4,1,2,32]{5,1,2,3,4,0:T(8,128)(2,1)} %get-tuple-element.39, bf16[256,16,4,1,2,32]{5,1,2,3,4,0:T(8,128)(2,1)} %get-tuple-element.38), kind=kOutput, calls=%fused_computation.6 | convolution fusion | flops 136314880 | bytes 8388608 | tf_op jit(solution)/shard_map/lakcf,flkcdr->fdar/dot_general | solution.py:57
  142.9 8.1 %copy.181 = f32[256,2,32,8,4]{0,2,4,1,3:T(8,128)} copy(f32[256,2,32,8,4]{2,4,3,1,0:T(4,128)} %bitcast.117) | data formatting | bytes 4194304 | tf_op jit(solution)/shard_map/reshape | solution.py:61
  150.9 6.4 %all-to-all-start.1 = ((f32[256,2,32,8,4]{0,2,4,1,3:T(8,128)}), f32[256,2,32,8,4]{0,2,4,1,3:T(8,128)S(1)}, u32[]{:S(2)}, u32[]{:S(2)}) async-start(f32[256,2,32,8,4]{0,2,4,1,3:T(8,128)} %copy.181), calls=%async_computation.1 | async-start | bytes 4194304 | tf_op jit(solution)/shard_map/all_to_all | solution.py:62
  157.3 0.3 copy.176
  157.6 0.6 iota_reduce_fusion
  158.3 25.2 %all-to-all-done.1 = f32[256,2,32,8,4]{0,2,4,1,3:T(8,128)S(1)} async-done(((f32[256,2,32,8,4]{0,2,4,1,3:T(8,128)}), f32[256,2,32,8,4]{0,2,4,1,3:T(8,128)S(1)}, u32[]{:S(2)}, u32[]{:S(2)}) %all-to-all-start.1) | async-done | bytes 2097184 | tf_op jit(solution)/shard_map/all_to_all | solution.py:62
  183.4 0.2 reduce_sum.40
  183.6 0.5 copy.211
  184.1 1.3 fusion.22
  185.4 0.3 copy.183
  185.8 1.1 broadcast_in_dim.56
  186.9 5.4 %all-to-all-start.2 = ((bf16[256,2,32,8,4]{0,2,4,1,3:T(8,128)(2,1)}), bf16[256,2,32,8,4]{0,2,4,1,3:T(8,128)(2,1)S(1)}, u32[]{:S(2)}, u32[]{:S(2)}) async-start(bf16[256,2,32,8,4]{0,2,4,1,3:T(8,128)(2,1)} %broadcast_in_dim.56), calls=%async_computation.2 | async-start | bytes 2097152 | tf_op jit(solution)/shard_map/all_to_all | solution.py:67
  192.3 12.3 %pad_maximum_fusion = (bf16[256,16,2,2,2,32]{5,1,2,4,0,3:T(8,128)(2,1)}, bf16[256,16,2,2,2,32]{5,1,2,4,0,3:T(8,128)(2,1)}) fusion(bf16[256,16,4,1,2,32]{5,1,2,4,0,3:T(8,128)(2,1)} %get-tuple-element.37, bf16[256,16,4,1,2,32]{5,1,2,4,0,3:T(8,128)(2,1)} %get-tuple-element.40), kind=kLoop, calls=%fused_computation.11 | loop fusion | flops 2097152 | bytes 8388608 | tf_op jit(solution)/shard_map/stack | solution.py:53
  204.6 2.1 all-to-all-done.2
  206.7 0.1 copy.184
  206.8 6.9 %copy.200 = bf16[256,2,32,32,1,1]{3,2,1,5,4,0:T(8,128)(2,1)} copy(bf16[256,2,32,32,1,1]{0,2,3,1,5,4:T(8,128)(2,1)S(1)} %bitcast.119) | data formatting | bytes 2097152 | tf_op jit(solution)/shard_map/reshape | solution.py:68
  213.7 8.9 %fusion.10 = bf16[16,32,2,2,256]{1,0,3,2,4:T(8,128)(2,1)} fusion(bf16[256,2,32,32,1,1]{3,2,1,5,4,0:T(8,128)(2,1)} %copy.200, bf16[256,16,2,2,2,32]{5,1,2,4,0,3:T(8,128)(2,1)} %get-tuple-element.35), kind=kOutput, calls=%fused_computation.25 | convolution fusion | flops 67633152 | bytes 4194304 | tf_op jit(solution)/shard_map/fcar,flkecr->lakef/dot_general | solution.py:76
  222.6 4.9 %copy.192 = bf16[16,32,2,2,256]{4,1,3,2,0:T(8,128)(2,1)S(1)} copy(bf16[16,32,2,2,256]{1,0,3,2,4:T(8,128)(2,1)} %fusion.10) | data formatting | bytes 2097152 | tf_op jit(solution)/shard_map/convert_element_type | solution.py:79
  227.5 2.1 gather_fusion.3
  229.5 8.0 %all-to-all-start.4 = ((bf16[32,32,2,2,256]{4,1,3,2,0:T(8,128)(2,1)}), bf16[32,32,2,2,256]{4,1,3,2,0:T(8,128)(2,1)S(1)}, u32[]{:S(2)}, u32[]{:S(2)}) async-start(bf16[32,32,2,2,256]{4,1,3,2,0:T(8,128)(2,1)} %gather_fusion.3), calls=%async_computation.4 | async-start | bytes 4194304 | tf_op jit(solution)/shard_map/all_to_all | solution.py:80
  237.6 8.9 %fusion.9 = bf16[16,32,2,2,256]{1,0,3,2,4:T(8,128)(2,1)} fusion(bf16[256,2,32,32,1,1]{3,2,1,5,4,0:T(8,128)(2,1)} %copy.200, bf16[256,16,2,2,2,32]{5,1,2,4,0,3:T(8,128)(2,1)} %get-tuple-element.36), kind=kOutput, calls=%fused_computation.24 | convolution fusion | flops 67633152 | bytes 4194304 | tf_op jit(solution)/shard_map/fcar,flkecr->lakef/dot_general | solution.py:76
  246.4 4.9 %copy.187 = bf16[16,32,2,2,256]{4,1,3,2,0:T(8,128)(2,1)S(1)} copy(bf16[16,32,2,2,256]{1,0,3,2,4:T(8,128)(2,1)} %fusion.9) | data formatting | bytes 2097152 | tf_op jit(solution)/shard_map/convert_element_type | solution.py:79
  251.3 2.0 gather_fusion.2
  253.3 33.6 %all-to-all-done.4 = bf16[32,32,2,2,256]{4,1,3,2,0:T(8,128)(2,1)S(1)} async-done(((bf16[32,32,2,2,256]{4,1,3,2,0:T(8,128)(2,1)}), bf16[32,32,2,2,256]{4,1,3,2,0:T(8,128)(2,1)S(1)}, u32[]{:S(2)}, u32[]{:S(2)}) %all-to-all-start.4) | async-done | bytes 2097184 | tf_op jit(solution)/shard_map/all_to_all | solution.py:80
  287.0 5.6 %all-to-all-start.3 = ((bf16[32,32,2,2,256]{4,1,3,2,0:T(8,128)(2,1)}), bf16[32,32,2,2,256]{4,1,3,2,0:T(8,128)(2,1)}, u32[]{:S(2)}, u32[]{:S(2)}) async-start(bf16[32,32,2,2,256]{4,1,3,2,0:T(8,128)(2,1)} %gather_fusion.2), calls=%async_computation.3 | async-start | bytes 4194304 | tf_op jit(solution)/shard_map/all_to_all | solution.py:80
  292.6 2.2 fusion.53
  294.8 2.2 copy.196
  297.0 2.4 convert_element_type.62
  299.4 42.7 %all-to-all-done.3 = bf16[32,32,2,2,256]{4,1,3,2,0:T(8,128)(2,1)} async-done(((bf16[32,32,2,2,256]{4,1,3,2,0:T(8,128)(2,1)}), bf16[32,32,2,2,256]{4,1,3,2,0:T(8,128)(2,1)}, u32[]{:S(2)}, u32[]{:S(2)}) %all-to-all-start.3) | async-done | bytes 2097184 | tf_op jit(solution)/shard_map/all_to_all | solution.py:80
  342.2 2.3 convert_element_type.59
  344.4 0.5 copy-done.2
  345.0 1.6 select_reduce_fusion.1
  346.7 0.0 copy-done.4
  346.7 0.0 copy-done.6
  346.7 0.0 copy-done.7
  346.7 0.7 fusion.18
  347.4 0.7 fusion.17
  348.1 0.9 copy.195
  349.0 1.1 copy.194
  (19 shorter events, 0.2 us)
Async XLA Ops:
  2.7 1.9 copy-start.3
  2.7 1.9 copy-start.5
  8.8 105.8 %all-to-all-start = ((bf16[32,32,4,2,256]{4,1,3,2,0:T(8,128)(2,1)}), bf16[32,32,4,2,256]{4,1,3,2,0:T(8,128)(2,1)}, u32[]{:S(2)}, u32[]{:S(2)}) async-start(bf16[32,32,4,2,256]{4,1,3,2,0:T(8,128)(2,1)} %gather_fusion), calls=%async_computation | async-start | bytes 8388608 | tf_op jit(solution)/shard_map/all_to_all | solution.py:47
  20.0 14.8 %copy-start.9 = (s32[32,16]{0,1:T(8,128)S(1)}, s32[32,16]{0,1:T(8,128)}, u32[]{:S(2)}) copy-start(s32[32,16]{0,1:T(8,128)} %param.7) | copy-start | bytes 6148
  35.0 6.6 %copy-start = (bf16[1,16,1,4,32,256]{4,1,3,5,2,0:T(8,128)(2,1)S(1)}, bf16[1,16,1,4,32,256]{4,1,3,5,2,0:T(8,128)(2,1)}, u32[]{:S(2)}) copy-start(bf16[1,16,1,4,32,256]{4,1,3,5,2,0:T(8,128)(2,1)} %copy.212) | copy-start | bytes 3145732
  35.0 6.6 %copy-start.1 = (bf16[1,16,1,4,32,256]{4,1,3,5,2,0:T(8,128)(2,1)S(1)}, bf16[1,16,1,4,32,256]{4,1,3,5,2,0:T(8,128)(2,1)}, u32[]{:S(2)}) copy-start(bf16[1,16,1,4,32,256]{4,1,3,5,2,0:T(8,128)(2,1)} %copy.213) | copy-start | bytes 3145732
  142.9 14.4 %copy-start.8 = (bf16[1,2,32,4,256]{4,3,2,1,0:T(4,128)(2,1)S(1)}, bf16[1,2,32,4,256]{4,3,2,1,0:T(4,128)(2,1)}, u32[]{:S(2)}) copy-start(bf16[1,2,32,4,256]{4,3,2,1,0:T(4,128)(2,1)} %param.6) | copy-start | bytes 393220
  150.9 32.5 %all-to-all-start.1 = ((f32[256,2,32,8,4]{0,2,4,1,3:T(8,128)}), f32[256,2,32,8,4]{0,2,4,1,3:T(8,128)S(1)}, u32[]{:S(2)}, u32[]{:S(2)}) async-start(f32[256,2,32,8,4]{0,2,4,1,3:T(8,128)} %copy.181), calls=%async_computation.1 | async-start | bytes 4194304 | tf_op jit(solution)/shard_map/all_to_all | solution.py:62
  186.9 19.8 %all-to-all-start.2 = ((bf16[256,2,32,8,4]{0,2,4,1,3:T(8,128)(2,1)}), bf16[256,2,32,8,4]{0,2,4,1,3:T(8,128)(2,1)S(1)}, u32[]{:S(2)}, u32[]{:S(2)}) async-start(bf16[256,2,32,8,4]{0,2,4,1,3:T(8,128)(2,1)} %broadcast_in_dim.56), calls=%async_computation.2 | async-start | bytes 2097152 | tf_op jit(solution)/shard_map/all_to_all | solution.py:67
  229.5 57.4 %all-to-all-start.4 = ((bf16[32,32,2,2,256]{4,1,3,2,0:T(8,128)(2,1)}), bf16[32,32,2,2,256]{4,1,3,2,0:T(8,128)(2,1)S(1)}, u32[]{:S(2)}, u32[]{:S(2)}) async-start(bf16[32,32,2,2,256]{4,1,3,2,0:T(8,128)(2,1)} %gather_fusion.3), calls=%async_computation.4 | async-start | bytes 4194304 | tf_op jit(solution)/shard_map/all_to_all | solution.py:80
  287.0 55.2 %all-to-all-start.3 = ((bf16[32,32,2,2,256]{4,1,3,2,0:T(8,128)(2,1)}), bf16[32,32,2,2,256]{4,1,3,2,0:T(8,128)(2,1)}, u32[]{:S(2)}, u32[]{:S(2)}) async-start(bf16[32,32,2,2,256]{4,1,3,2,0:T(8,128)(2,1)} %gather_fusion.2), calls=%async_computation.3 | async-start | bytes 4194304 | tf_op jit(solution)/shard_map/all_to_all | solution.py:80
  299.4 47.2 %copy-start.4 = (f32[512,256]{1,0:T(8,128)S(1)}, f32[512,256]{1,0:T(8,128)}, u32[]{:S(2)}) copy-start(f32[512,256]{1,0:T(8,128)} %copy-done.3) | copy-start | bytes 1572868
  299.4 47.2 %copy-start.6 = (f32[512,256]{1,0:T(8,128)S(1)}, f32[512,256]{1,0:T(8,128)}, u32[]{:S(2)}) copy-start(f32[512,256]{1,0:T(8,128)} %copy-done.5) | copy-start | bytes 1572868
  299.4 47.2 %copy-start.7 = (f32[2,32,2,512]{3,2,1,0:T(2,128)S(1)}, f32[2,32,2,512]{3,2,1,0:T(2,128)}, u32[]{:S(2)}) copy-start(f32[2,32,2,512]{3,2,1,0:T(2,128)} %get-tuple-element.45) | copy-start | bytes 786436
  342.2 2.8 copy-start.2

commit v9 on v8

--- a/solution.py
+++ b/solution.py
@@ -6,7 +6,7 @@
 from jax.sharding import PartitionSpec as P
 
 step_length = 0.5
-chunks = 2
+chunks = 1
 
 
 def make_table(samples):

time: 352 us -> 348 us (0.989)
  waiting for transfers between devices: 162 us -> 191 us
  other arithmetic: 47.3 us -> 33.5 us
  matrix products: 32.8 us -> 25.9 us
  starting transfers between devices: 36.5 us -> 30.8 us
  local copies, waits for them, and re-layouts: 70.7 us -> 65.6 us
    all_to_all x2 -> x1, waiting for transfers between devices: 76.4 us -> 93.5 us  [per_device(): lax.all_to_all(returning, 'target', split_axis=0, concat_axis=0, tiled=True)]
    another operation x2 -> x1, other arithmetic: 27 us -> 14.8 us  [per_device(): jnp.stack([jnp.stack([-data_real, -data_imag], 3), jnp.stack([data_imag,...]
    all_to_all x1, waiting for transfers between devices: 2.11 us -> 13.8 us  [per_device(): lax.all_to_all(spread, 'surface', split_axis=3, concat_axis=3, tiled=True)]
    dot_general x2 -> x1, matrix products: 17.7 us -> 11.5 us  [per_device(): jnp.einsum('fcar,flkecr->lakef', misfit, backward[:, :, lo:hi], preferred...]
    all_to_all x2 -> x1, starting transfers between devices: 13.6 us -> 8.07 us  [per_device(): lax.all_to_all(returning, 'target', split_axis=0, concat_axis=0, tiled=True)]
    unnamed x27 -> x25, local copies, waits for them, and re-layouts: 18.7 us -> 17.8 us
    convert_element_type x2 -> x1, local copies, waits for them, and re-layouts: 9.76 us -> 9.08 us  [per_device(): returning = grad_spectra.astype(jnp.bfloat16)[entry_for]]
  transfers between devices with their start and end apart: 5 -> 4, of which waited for: 5 -> 4; matrix products, arithmetic and copies ran while one was open for 21% -> 11% of each run, Pallas kernels for 0% -> 0%
where the time goes in v9:
time: 348 us; the launch traced here: 347 us
  waiting for transfers between devices  191 us (55%)
  local copies, waits for them, and re-layouts  65.6 us (19%)
  other arithmetic  33.5 us (10%)
  starting transfers between devices  30.8 us (9%)
  matrix products  25.9 us (7%)
    all_to_all x1, waiting for transfers between devices, per_device(): lax.all_to_all(returning, 'target', split_axis=0, concat_axis=0, tiled=True)  93.5 us
    all_to_all x1, waiting for transfers between devices, per_device(): lax.all_to_all(outgoing, 'target', split_axis=0, concat_axis=0, tiled=True)  58.3 us
    all_to_all x1, waiting for transfers between devices, per_device(): lax.all_to_all(split_value, 'surface', split_axis=3, concat_axis=3, tiled...  25 us
    unnamed x25, local copies, waits for them, and re-layouts  17.8 us
    gather x2, local copies, waits for them, and re-layouts, per_device(): spectra = arrived[own_owner]  14.9 us
    another operation x1, other arithmetic, per_device(): jnp.stack([jnp.stack([-data_real, -data_imag], 3), jnp.stack([data_imag,...  14.8 us
    all_to_all x1, waiting for transfers between devices, per_device(): lax.all_to_all(spread, 'surface', split_axis=3, concat_axis=3, tiled=True)  13.8 us
    dot_general x1, matrix products, per_device(): jnp.einsum('lakcf,flkcdr->fdar', spectra, forward, preferred_element_type...  13.4 us
  transfers between devices with their start and end apart: 4, of which 4 were waited for; matrix products, arithmetic and copies ran while one was open for 11% of the time, Pallas kernels for 0%

profile of v9, /device:TPU:1, one launch (start us, length us, event | category | flops | bytes accessed | tf_op | source)
XLA Modules:
  0.0 347.2 jit_solution(14270245181516516069)
XLA Ops:
  0.6 2.1 sine_negate_fusion
  2.7 0.0 copy-start.3
  2.7 0.0 copy-start.5
  2.7 0.8 fusion.40
  3.5 0.7 fusion.29
  4.2 1.1 convert_element_type.43
  5.4 0.3 convolution_convert_fusion
  5.7 0.0 copy-done.3
  5.7 2.8 gather_fusion
  8.5 0.0 copy-done.5
  8.5 11.1 %all-to-all-start = ((bf16[32,32,4,2,256]{4,1,3,2,0:T(8,128)(2,1)}), bf16[32,32,4,2,256]{4,1,3,2,0:T(8,128)(2,1)}, u32[]{:S(2)}, u32[]{:S(2)}) async-start(bf16[32,32,4,2,256]{4,1,3,2,0:T(8,128)(2,1)} %gather_fusion), calls=%async_computation | async-start | bytes 8388608 | tf_op jit(solution)/shard_map/all_to_all | solution.py:47
  19.6 0.0 copy-start.8
  19.6 1.8 fusion.42
  21.4 6.5 %copy.173 = bf16[1,16,1,4,32,256]{4,1,3,5,2,0:T(8,128)(2,1)} copy(bf16[1,16,1,4,32,256]{5,4,3,2,1,0:T(8,128)(2,1)S(1)} %get-tuple-element.38) | data formatting | bytes 2097152
  27.9 6.5 %copy.174 = bf16[1,16,1,4,32,256]{4,1,3,5,2,0:T(8,128)(2,1)} copy(bf16[1,16,1,4,32,256]{5,4,3,2,1,0:T(8,128)(2,1)S(1)} %get-tuple-element.37) | data formatting | bytes 2097152
  34.4 0.0 copy-done.8
  34.4 0.2 fusion.31
  34.6 0.0 copy-start
  34.7 0.0 copy-start.1
  34.7 6.6 %fusion.9 = (bf16[256,16,4,1,32]{4,1,2,3,0:T(8,128)(2,1)S(1)}, bf16[256,16,4,1,32]{4,1,2,3,0:T(8,128)(2,1)}) fusion(bf16[1,16,1,4,32,256]{4,1,3,5,2,0:T(8,128)(2,1)} %copy.173, bf16[1,16,1,4,32,256]{4,1,3,5,2,0:T(8,128)(2,1)} %copy.174), kind=kLoop, calls=%fused_computation.18 | loop fusion | flops 1048576 | bytes 4194304 | tf_op jit(solution)/shard_map/stack | solution.py:54
  41.3 0.0 copy-done
  41.3 0.0 copy-done.1
  41.3 14.8 %maximum_bitcast_fusion = (bf16[256,16,4,1,2,32]{5,1,2,4,0,3:T(8,128)(2,1)}, bf16[256,16,4,1,2,32]{5,1,2,4,0,3:T(8,128)(2,1)}, bf16[256,16,4,1,2,32]{5,1,2,3,4,0:T(8,128)(2,1)}, bf16[256,16,4,1,2,32]{5,1,2,3,4,0:T(8,128)(2,1)}) fusion(bf16[256,16,4,1,32]{4,1,2,3,0:T(8,128)(2,1)} %get-tuple-element.46, bf16[256,16,4,1,32]{4,1,2,3,0:T(8,128)(2,1)S(1)} %get-tuple-element.45, ...), kind=kLoop, calls=%fused_computation.13 | loop fusion | flops 4194304 | bytes 12582912 | tf_op jit(solution)/shard_map/stack | solution.py:53
  56.0 58.3 %all-to-all-done = bf16[32,32,4,2,256]{4,1,3,2,0:T(8,128)(2,1)} async-done(((bf16[32,32,4,2,256]{4,1,3,2,0:T(8,128)(2,1)}), bf16[32,32,4,2,256]{4,1,3,2,0:T(8,128)(2,1)}, u32[]{:S(2)}, u32[]{:S(2)}) %all-to-all-start) | async-done | bytes 4194336 | tf_op jit(solution)/shard_map/all_to_all | solution.py:47
  114.3 2.9 gather_fusion.1
  117.1 12.0 %copy.163 = bf16[16,32,4,2,256,1]{1,0,2,3,5,4:T(8,128)(2,1)} copy(bf16[16,32,4,2,256,1]{4,1,3,2,0,5:T(8,128)(2,1)S(1)} %bitcast.106) | data formatting | bytes 4194304 | tf_op jit(solution)/shard_map/gather | solution.py:56
  129.1 13.4 %fusion = f32[256,2,32,32,1,1]{3,2,5,4,1,0:T(8,128)} fusion(bf16[16,32,4,2,256,1]{1,0,2,3,5,4:T(8,128)(2,1)} %copy.163, bf16[256,16,4,1,2,32]{5,1,2,3,4,0:T(8,128)(2,1)} %get-tuple-element.36, bf16[256,16,4,1,2,32]{5,1,2,3,4,0:T(8,128)(2,1)} %get-tuple-element.35), kind=kOutput, calls=%fused_computation.4 | convolution fusion | flops 136314880 | bytes 8388608 | tf_op jit(solution)/shard_map/lakcf,flkcdr->fdar/dot_general | solution.py:57
  142.6 0.0 copy-start.7
  142.6 8.1 %copy.150 = f32[256,2,32,8,4]{0,2,4,1,3:T(8,128)} copy(f32[256,2,32,8,4]{2,4,3,1,0:T(4,128)} %bitcast.105) | data formatting | bytes 4194304 | tf_op jit(solution)/shard_map/reshape | solution.py:61
  150.6 6.4 %all-to-all-start.1 = ((f32[256,2,32,8,4]{0,2,4,1,3:T(8,128)}), f32[256,2,32,8,4]{0,2,4,1,3:T(8,128)S(1)}, u32[]{:S(2)}, u32[]{:S(2)}) async-start(f32[256,2,32,8,4]{0,2,4,1,3:T(8,128)} %copy.150), calls=%async_computation.1 | async-start | bytes 4194304 | tf_op jit(solution)/shard_map/all_to_all | solution.py:62
  157.0 0.0 copy-done.7
  157.0 1.1 copy.145
  158.1 25.0 %all-to-all-done.1 = f32[256,2,32,8,4]{0,2,4,1,3:T(8,128)S(1)} async-done(((f32[256,2,32,8,4]{0,2,4,1,3:T(8,128)}), f32[256,2,32,8,4]{0,2,4,1,3:T(8,128)S(1)}, u32[]{:S(2)}, u32[]{:S(2)}) %all-to-all-start.1) | async-done | bytes 2097184 | tf_op jit(solution)/shard_map/all_to_all | solution.py:62
  183.1 0.2 reduce_sum.31
  183.3 0.5 copy.172
  183.8 1.4 fusion.14
  185.2 0.3 copy.152
  185.5 1.1 broadcast_in_dim.22
  186.6 5.2 %all-to-all-start.2 = ((bf16[256,2,32,8,4]{0,2,4,1,3:T(8,128)(2,1)}), bf16[256,2,32,8,4]{0,2,4,1,3:T(8,128)(2,1)S(1)}, u32[]{:S(2)}, u32[]{:S(2)}) async-start(bf16[256,2,32,8,4]{0,2,4,1,3:T(8,128)(2,1)} %broadcast_in_dim.22), calls=%async_computation.2 | async-start | bytes 2097152 | tf_op jit(solution)/shard_map/all_to_all | solution.py:67
  191.8 0.6 iota_reduce_fusion
  192.4 13.8 %all-to-all-done.2 = bf16[256,2,32,8,4]{0,2,4,1,3:T(8,128)(2,1)S(1)} async-done(((bf16[256,2,32,8,4]{0,2,4,1,3:T(8,128)(2,1)}), bf16[256,2,32,8,4]{0,2,4,1,3:T(8,128)(2,1)S(1)}, u32[]{:S(2)}, u32[]{:S(2)}) %all-to-all-start.2) | async-done | bytes 1048608 | tf_op jit(solution)/shard_map/all_to_all | solution.py:67
  206.2 0.1 copy.153
  206.3 6.9 %copy.165 = bf16[256,2,32,32,1,1]{3,2,1,5,4,0:T(8,128)(2,1)} copy(bf16[256,2,32,32,1,1]{0,2,3,1,5,4:T(8,128)(2,1)S(1)} %bitcast.107) | data formatting | bytes 2097152 | tf_op jit(solution)/shard_map/reshape | solution.py:68
  213.2 11.5 %fusion.6 = bf16[16,32,4,2,256]{1,0,3,2,4:T(8,128)(2,1)} fusion(bf16[256,2,32,32,1,1]{3,2,1,5,4,0:T(8,128)(2,1)} %copy.165, bf16[256,16,4,1,2,32]{5,1,2,4,0,3:T(8,128)(2,1)} %get-tuple-element.34, bf16[256,16,4,1,2,32]{5,1,2,4,0,3:T(8,128)(2,1)} %get-tuple-element.33), kind=kOutput, calls=%fused_computation.12 | convolution fusion | flops 137363456 | bytes 7340032 | tf_op jit(solution)/shard_map/fcar,flkecr->lakef/dot_general | solution.py:76
  224.6 9.1 %copy.156 = bf16[16,32,4,2,256]{4,1,3,2,0:T(8,128)(2,1)S(1)} copy(bf16[16,32,4,2,256]{1,0,3,2,4:T(8,128)(2,1)} %fusion.6) | data formatting | bytes 4194304 | tf_op jit(solution)/shard_map/convert_element_type | solution.py:79
  233.7 2.8 gather_fusion.2
  236.5 8.1 %all-to-all-start.3 = ((bf16[32,32,4,2,256]{4,1,3,2,0:T(8,128)(2,1)}), bf16[32,32,4,2,256]{4,1,3,2,0:T(8,128)(2,1)}, u32[]{:S(2)}, u32[]{:S(2)}) async-start(bf16[32,32,4,2,256]{4,1,3,2,0:T(8,128)(2,1)} %gather_fusion.2), calls=%async_computation.3 | async-start | bytes 8388608 | tf_op jit(solution)/shard_map/all_to_all | solution.py:80
  244.6 1.2 copy.161
  245.8 0.0 copy-start.2
  245.8 0.0 copy-start.4
  245.8 0.0 copy-start.6
  245.8 93.5 %all-to-all-done.3 = bf16[32,32,4,2,256]{4,1,3,2,0:T(8,128)(2,1)} async-done(((bf16[32,32,4,2,256]{4,1,3,2,0:T(8,128)(2,1)}), bf16[32,32,4,2,256]{4,1,3,2,0:T(8,128)(2,1)}, u32[]{:S(2)}, u32[]{:S(2)}) %all-to-all-start.3) | async-done | bytes 4194336 | tf_op jit(solution)/shard_map/all_to_all | solution.py:80
  339.2 3.3 convert_element_type.49
  342.6 1.7 select_reduce_fusion
  344.3 0.1 copy.176
  344.4 0.0 copy-done.2
  344.4 0.0 copy-done.4
  344.4 0.0 copy-done.6
  344.4 0.7 fusion.43
  345.1 1.1 copy.159
  346.3 0.9 copy.160
  (8 shorter events, 0.1 us)
Async XLA Ops:
  2.7 3.0 copy-start.3
  2.7 5.8 %copy-start.5 = (f32[512,256]{1,0:T(8,128)}, f32[512,256]{1,0:T(8,128)S(1)}, u32[]{:S(2)}) copy-start(f32[512,256]{1,0:T(8,128)S(1)} %get-tuple-element.44) | copy-start | bytes 1572868
  8.5 105.8 %all-to-all-start = ((bf16[32,32,4,2,256]{4,1,3,2,0:T(8,128)(2,1)}), bf16[32,32,4,2,256]{4,1,3,2,0:T(8,128)(2,1)}, u32[]{:S(2)}, u32[]{:S(2)}) async-start(bf16[32,32,4,2,256]{4,1,3,2,0:T(8,128)(2,1)} %gather_fusion), calls=%async_computation | async-start | bytes 8388608 | tf_op jit(solution)/shard_map/all_to_all | solution.py:47
  19.6 14.8 %copy-start.8 = (s32[32,16]{0,1:T(8,128)S(1)}, s32[32,16]{0,1:T(8,128)}, u32[]{:S(2)}) copy-start(s32[32,16]{0,1:T(8,128)} %param.7) | copy-start | bytes 6148
  34.6 6.6 %copy-start = (bf16[1,16,1,4,32,256]{4,1,3,5,2,0:T(8,128)(2,1)S(1)}, bf16[1,16,1,4,32,256]{4,1,3,5,2,0:T(8,128)(2,1)}, u32[]{:S(2)}) copy-start(bf16[1,16,1,4,32,256]{4,1,3,5,2,0:T(8,128)(2,1)} %copy.173) | copy-start | bytes 3145732
  34.7 6.6 %copy-start.1 = (bf16[1,16,1,4,32,256]{4,1,3,5,2,0:T(8,128)(2,1)S(1)}, bf16[1,16,1,4,32,256]{4,1,3,5,2,0:T(8,128)(2,1)}, u32[]{:S(2)}) copy-start(bf16[1,16,1,4,32,256]{4,1,3,5,2,0:T(8,128)(2,1)} %copy.174) | copy-start | bytes 3145732
  142.6 14.4 %copy-start.7 = (bf16[1,2,32,4,256]{4,3,2,1,0:T(4,128)(2,1)S(1)}, bf16[1,2,32,4,256]{4,3,2,1,0:T(4,128)(2,1)}, u32[]{:S(2)}) copy-start(bf16[1,2,32,4,256]{4,3,2,1,0:T(4,128)(2,1)} %param.6) | copy-start | bytes 393220
  150.6 32.5 %all-to-all-start.1 = ((f32[256,2,32,8,4]{0,2,4,1,3:T(8,128)}), f32[256,2,32,8,4]{0,2,4,1,3:T(8,128)S(1)}, u32[]{:S(2)}, u32[]{:S(2)}) async-start(f32[256,2,32,8,4]{0,2,4,1,3:T(8,128)} %copy.150), calls=%async_computation.1 | async-start | bytes 4194304 | tf_op jit(solution)/shard_map/all_to_all | solution.py:62
  186.6 19.6 %all-to-all-start.2 = ((bf16[256,2,32,8,4]{0,2,4,1,3:T(8,128)(2,1)}), bf16[256,2,32,8,4]{0,2,4,1,3:T(8,128)(2,1)S(1)}, u32[]{:S(2)}, u32[]{:S(2)}) async-start(bf16[256,2,32,8,4]{0,2,4,1,3:T(8,128)(2,1)} %broadcast_in_dim.22), calls=%async_computation.2 | async-start | bytes 2097152 | tf_op jit(solution)/shard_map/all_to_all | solution.py:67
  236.5 102.7 %all-to-all-start.3 = ((bf16[32,32,4,2,256]{4,1,3,2,0:T(8,128)(2,1)}), bf16[32,32,4,2,256]{4,1,3,2,0:T(8,128)(2,1)}, u32[]{:S(2)}, u32[]{:S(2)}) async-start(bf16[32,32,4,2,256]{4,1,3,2,0:T(8,128)(2,1)} %gather_fusion.2), calls=%async_computation.3 | async-start | bytes 8388608 | tf_op jit(solution)/shard_map/all_to_all | solution.py:80
  245.8 98.6 %copy-start.2 = (f32[2,32,4,512]{3,2,1,0:T(4,128)S(1)}, f32[2,32,4,512]{3,2,1,0:T(4,128)}, u32[]{:S(2)}) copy-start(f32[2,32,4,512]{3,2,1,0:T(4,128)} %param.4) | copy-start | bytes 1572868
  245.8 98.6 %copy-start.4 = (f32[512,256]{1,0:T(8,128)S(1)}, f32[512,256]{1,0:T(8,128)}, u32[]{:S(2)}) copy-start(f32[512,256]{1,0:T(8,128)} %copy-done.3) | copy-start | bytes 1572868
  245.8 98.7 %copy-start.6 = (f32[512,256]{1,0:T(8,128)S(1)}, f32[512,256]{1,0:T(8,128)}, u32[]{:S(2)}) copy-start(f32[512,256]{1,0:T(8,128)} %copy-done.5) | copy-start | bytes 1572868
